TPU v7x, 512 devices: a whole 4x8x8 slice. The times are simulated.
512 devices in a mesh: sub: 128 (over z, y, core), harm: 4 (over x).
Axes of the slice: x: 4, y: 8, z: 8, core: 2. Of those that a mesh axis runs over, the one named last changes fastest.
Arguments:
- lengths: int32 [384], P('sub'), may hold values from 128 to 1024, as said below
- owners: int32 [384, 1], P('sub'), may hold values from 0 to 127, as said below
- front_inverse: bfloat16 [384, 1024, 1024], P('sub', 'harm'), may hold values from -0.1875 to 0.1875
- coupling: bfloat16 [384, 1024, 768], P('sub', 'harm'), may hold values from -0.1875 to 0.1875
- stiffness: bfloat16 [384, 768, 768], P('sub', 'harm'), may hold values from -0.21875 to 0.21875
- displacement: bfloat16 [128, 32, 768], P('sub', 'harm'), may hold values from -6 to 6
- forcing: float32 [128, 32, 768], P('sub', 'harm'), may hold values from -6 to 6
- lumped_mass: float32 [128, 768], P('sub'), may hold values from 0.2 to 2
- damping: float32 [128, 768], P('sub'), may hold values from 0.1 to 1.5
Outputs:
- interior: bfloat16 [384, 32, 1024], P('sub', None, 'harm')
- residual: float32 [128, 32, 768], P('sub', 'harm')
- modes: bfloat16 [384, 1024, 768], P('sub', 'harm')
Inputs may be any that keep to these rules, and one draw needn't show every extreme that they name: `lengths`: live interior front rows of each substructure, which are its first rows; some substructure has all 1024. `owners`: substructure k lies on sub index k // 3; on every sub index d, the first 2 of its 3 substructures are attached to block (d + 64) mod 128, the third to a block of uneven popularity; every interface block has at least one substructure.
All inputs are finite; a program needn't handle non-finite values.
Results may differ from a plain program's by a relative error of at most 0.008.
Values may be sent and summed in bfloat16 or wider, within the bound.
No kernel may reach another device: no remote copies, remote signals or barrier semaphores. Data moves between devices by JAX's collectives and lax.ppermute only.
A program may use at most 64 MiB of HBM per device.

v0:
```python
import jax
import jax.numpy as jnp
from jax import lax
from jax.sharding import Mesh
from jax.sharding import PartitionSpec as P

SUB = ("sub_0", "sub_1", "sub_2")


def copy_for_each(x, axis):
    length = lax.axis_size(axis)
    return lax.all_to_all(jnp.broadcast_to(x[None], (length, *x.shape)), axis, 0, 0, tiled=True)


def joined_along(tiles, dim):
    tiles = jnp.moveaxis(tiles, 0, dim)
    shape = tiles.shape
    return tiles.reshape(*shape[:dim], shape[dim] * shape[dim + 1], *shape[dim + 2 :])


def whole_of(x, axes, dim):
    far, near = axes
    tiles = copy_for_each(copy_for_each(x, far), near)
    return joined_along(tiles.swapaxes(0, 1).reshape(-1, *x.shape), dim)


def collect(x, axis, dim):
    tiles = copy_for_each(x, axis)
    return joined_along(tiles, dim)


def in_blocks(x, dim, length):
    shape = x.shape
    tiles = x.reshape(*shape[:dim], length, shape[dim] // length, *shape[dim + 1 :])
    return jnp.moveaxis(tiles, dim, 0)


def sent_and_summed(x, axis, dim):
    tiles = in_blocks(x, dim, lax.axis_size(axis))
    arrived = lax.all_to_all(tiles, axis, split_axis=0, concat_axis=0, tiled=True)
    return arrived.astype(jnp.float32).sum(axis=0)


def body(
    lengths, owners, front_inverse, coupling, stiffness, displacement, forcing, lumped_mass, damping
):
    nharm = lax.axis_size("harm")
    harm_idx = lax.axis_index("harm")
    front_q = coupling.shape[1]
    width = coupling.shape[2]
    width_q = stiffness.shape[1]
    nown = lax.axis_size(SUB)
    own_rows = harm_idx * front_q + jnp.arange(front_q, dtype=jnp.int32)
    live_rows = own_rows[None, :] < lengths[:, None]
    masked = jnp.where(live_rows[:, :, None], coupling, jnp.zeros_like(coupling))
    longest = jnp.max(lengths)
    empty = jnp.zeros((masked.shape[0], front_q, width), jnp.float32)
    piece = lax.all_gather(masked, "harm", axis=1, tiled=True)
    modes = lax.cond(
        jnp.int32(0) < longest,
        lambda: jnp.einsum(
            "sfg,sgn->sfn", front_inverse, piece, preferred_element_type=jnp.float32
        ),
        lambda: empty,
    ).astype(jnp.bfloat16)
    selector = (owners[:, 0][:, None] == jnp.arange(nown, dtype=jnp.int32)[None, :]).astype(
        jnp.bfloat16
    )
    group = whole_of(displacement, (("sub_0", "sub_1"), "sub_2"), 0)
    picked = jnp.einsum("so,ohn->shn", selector, group, preferred_element_type=jnp.float32).astype(
        jnp.bfloat16
    )
    own_disp = collect(picked, "harm", 1)
    inner = -jnp.einsum("sfn,shn->shf", modes, own_disp, preferred_element_type=jnp.float32)
    interior = jnp.where(live_rows[:, None, :], inner, jnp.float32(0.0)).astype(jnp.bfloat16)
    disp_cols = lax.dynamic_slice_in_dim(own_disp, harm_idx * width_q, width_q, 2)
    contrib = jnp.einsum("shf,sfn->shn", interior, masked, preferred_element_type=jnp.float32)
    contrib = contrib + jnp.einsum(
        "shj,sjn->shn", disp_cols, stiffness, preferred_element_type=jnp.float32
    )
    partial_rows = sent_and_summed(contrib.astype(jnp.bfloat16), "harm", 1)
    routing = (jnp.arange(nown, dtype=jnp.int32)[:, None] == owners[:, 0][None, :]).astype(
        jnp.float32
    )
    dense = jnp.einsum("os,shn->ohn", routing, partial_rows, precision=lax.Precision.HIGHEST)
    arrived = lax.all_to_all(
        dense.astype(jnp.bfloat16), SUB, split_axis=0, concat_axis=0, tiled=True
    ).astype(dense.dtype)
    gathered = jnp.sum(arrived, axis=0, keepdims=True)
    rows_q = displacement.shape[1]
    pairs_all = rows_q * nharm // 2
    rows = harm_idx * rows_q + jnp.arange(rows_q, dtype=jnp.int32)
    pair = (rows // 2).astype(jnp.float32)
    parity = (rows % 2).astype(jnp.float32)
    freq = 1.5 * (pair + 1.0) / pairs_all
    sign = 1.0 - 2.0 * parity
    disp = displacement.astype(jnp.float32)
    partner = disp.reshape(1, rows_q // 2, 2, width)[:, :, ::-1, :].reshape(1, rows_q, width)
    residual = (
        gathered
        - (freq * freq)[None, :, None] * lumped_mass[:, None, :] * disp
        + (sign * freq)[None, :, None] * damping[:, None, :] * partner
        - forcing
    )
    return (interior, residual, modes)


def solution(mesh):
    split = Mesh(
        mesh.devices.reshape(8, 8, 2, mesh.shape["harm"]), ("sub_0", "sub_1", "sub_2", "harm")
    )
    placed = (
        P(SUB),
        P(SUB, None),
        P(SUB, "harm", None),
        P(SUB, "harm", None),
        P(SUB, "harm", None),
        P(SUB, "harm", None),
        P(SUB, "harm", None),
        P(SUB, None),
        P(SUB, None),
    )
    return jax.shard_map(
        body,
        mesh=split,
        in_specs=placed,
        out_specs=(P(SUB, None, "harm"), P(SUB, "harm", None), P(SUB, "harm", None)),
        check_vma=False,
    )
```

profile of v0, /device:TPU:8, one launch (start us, length us, event | category | flops | bytes accessed | tf_op | source)
XLA Modules:
  0.0 159.1 jit_solution(11852261337395706234)
XLA Ops:
  7.2 0.0 copy-start
  7.2 0.0 all-gather.2.cloned.1.call-start
  7.2 0.8 broadcast_compare_fusion
  8.0 2.5 %broadcast_select_fusion = bf16[3,256,768]{2,1,0:T(8,128)(2,1)} fusion(bf16[3,256,768]{2,1,0:T(8,128)(2,1)} %param.14, pred[3,256]{1,0:T(4,128)(4,1)S(1)} %broadcast_compare_fusion), kind=kLoop, calls=%fused_computation.3 | loop fusion | flops 589824 | bytes 2360064 | tf_op jit(solution)/shard_map/jit(_where)/select_n | solution.py:55
  10.5 0.0 all-gather.2.cloned.1.call-update
  10.6 0.1 broadcast_in_dim.39
  10.6 40.4 %all_to_all.25 = bf16[64,1,8,768]{3,2,1,0:T(8,128)(2,1)S(1)} all-to-all(bf16[64,1,8,768]{3,2,1,0:T(8,128)(2,1)S(1)} %broadcast_in_dim.39), channel_id=1, replica_groups=mesh['sub_0'=8,'sub_1'=8,'sub_2'=2,'harm'=4] {'sub_0','sub_1'}, dimensions={0} | all-to-all | bytes 1572864 | tf_op jit(solution)/shard_map/all_to_all | solution.py:12
  51.0 0.1 copy.14
  51.1 0.2 broadcast_in_dim.65
  51.3 5.0 %all_to_all.26 = bf16[2,64,1,8,768]{4,1,3,2,0:T(8,128)(2,1)S(1)} all-to-all(bf16[2,64,1,8,768]{4,1,3,2,0:T(8,128)(2,1)S(1)} %broadcast_in_dim.65), channel_id=1, replica_groups=mesh['sub_0'=8,'sub_1'=8,'sub_2'=2,'harm'=4] {'sub_2'}, dimensions={0} | all-to-all | bytes 3145728 | tf_op jit(solution)/shard_map/all_to_all | solution.py:12
  56.3 1.6 %copy.15 = bf16[64,2,1,8,768]{4,1,0,3,2:T(2,128)(2,1)S(1)} copy(bf16[64,2,1,8,768]{4,0,3,2,1:T(8,128)(2,1)S(1)} %bitcast.39) | data formatting | bytes 3145728 | tf_op jit(solution)/shard_map/transpose | solution.py:24
  57.9 1.5 reshape_reshape.3
  59.4 1.8 %convolution_convert_fusion.2 = bf16[3,8,768]{2,0,1:T(4,128)(2,1)S(1)} fusion(bf16[128,8,768]{2,0,1:T(8,128)(2,1)} %reshape_reshape.3, s32[3]{0:T(128)S(1)} %bitcast.43), kind=kOutput, calls=%fused_computation.10 | convolution fusion | flops 4737408 | bytes 1609740 | tf_op jit(solution)/shard_map/so,ohn->shn/dot_general | solution.py:70
  61.2 0.7 broadcast_in_dim.66
  61.9 4.3 %all-to-all-start.2 = ((bf16[4,3,8,768]{3,2,1,0:T(8,128)(2,1)}), bf16[4,3,8,768]{3,2,1,0:T(8,128)(2,1)S(1)}, u32[]{:S(2)}, u32[]{:S(2)}) async-start(bf16[4,3,8,768]{3,2,1,0:T(8,128)(2,1)} %broadcast_in_dim.66), calls=%async_computation.2 | async-start | bytes 294912 | tf_op jit(solution)/shard_map/all_to_all | solution.py:12
  66.2 0.6 reduce_max.9
  67.5 6.7 %all-to-all-done.2 = bf16[4,3,8,768]{3,2,1,0:T(8,128)(2,1)S(1)} async-done(((bf16[4,3,8,768]{3,2,1,0:T(8,128)(2,1)}), bf16[4,3,8,768]{3,2,1,0:T(8,128)(2,1)S(1)}, u32[]{:S(2)}, u32[]{:S(2)}) %all-to-all-start.2) | async-done | bytes 147488 | tf_op jit(solution)/shard_map/all_to_all | solution.py:12
  74.3 0.6 all-gather.2.cloned.1.call-done
  74.8 4.2 %conditional.1 = (bf16[3,256,768]{2,1,0:T(8,128)(2,1)S(1)}) conditional(s32[]{:T(128)} %convert_element_type.50, () %tuple.16, (bf16[3,256,1024]{2,1,0:T(8,128)(2,1)}, bf16[3,1024,768]{2,1,0:T(8,128)(2,1)}) %tuple.17), branch_computations={%region_1.2_spmd, %region_2.3_spmd} | conditional | flops 1208549376 | bytes 7471112 | solution.py:59
  74.8 4.2 %convolution_convert_fusion = bf16[3,256,768]{2,1,0:T(8,128)(2,1)S(1)} fusion(bf16[3,256,1024]{2,1,0:T(8,128)(2,1)} %get-tuple-element.14, bf16[3,1024,768]{2,1,0:T(8,128)(2,1)} %get-tuple-element.9), kind=kOutput, calls=%fused_computation | convolution fusion | flops 1208549376 | bytes 7471104 | tf_op jit(solution)/shard_map/cond/branch_1_fun/sfg,sgn->sfn/dot_general | solution.py:61
  79.1 0.5 fusion.3
  79.5 1.2 copy-done.1
  80.7 0.3 fusion.20
  81.1 0.4 fusion.1
  81.5 9.3 %all_to_all.27 = bf16[4,3,8,768]{3,2,1,0:T(8,128)(2,1)S(1)} all-to-all(bf16[4,3,8,768]{3,2,1,0:T(8,128)(2,1)S(1)} %bitcast.41), channel_id=1, replica_groups=mesh['sub_0'=8,'sub_1'=8,'sub_2'=2,'harm'=4] {'harm'}, dimensions={0} | all-to-all | bytes 294912 | tf_op jit(solution)/shard_map/all_to_all | solution.py:40
  90.8 1.5 convolution_convert_fusion.1
  92.3 2.0 %copy.21 = bf16[128,8,768]{2,1,0:T(8,128)(2,1)} copy(bf16[128,8,768]{2,0,1:T(8,128)(2,1)S(1)} %convolution_convert_fusion.1) | data formatting | bytes 3145728 | tf_op jit(solution)/shard_map/convert_element_type | solution.py:87
  94.3 14.3 %all-to-all-start.4 = ((bf16[128,8,768]{2,1,0:T(8,128)(2,1)}), bf16[128,8,768]{2,1,0:T(8,128)(2,1)S(1)}, u32[]{:S(2)}, u32[]{:S(2)}) async-start(bf16[128,8,768]{2,1,0:T(8,128)(2,1)} %copy.21), calls=%async_computation.4 | async-start | bytes 3145728 | tf_op jit(solution)/shard_map/all_to_all | solution.py:86
  108.6 0.2 rev.3
  109.0 42.3 %all-to-all-done.4 = bf16[128,8,768]{2,1,0:T(8,128)(2,1)S(1)} async-done(((bf16[128,8,768]{2,1,0:T(8,128)(2,1)}), bf16[128,8,768]{2,1,0:T(8,128)(2,1)S(1)}, u32[]{:S(2)}, u32[]{:S(2)}) %all-to-all-start.4) | async-done | bytes 1572896 | tf_op jit(solution)/shard_map/all_to_all | solution.py:86
  151.3 0.3 convert_reduce_fusion
  151.6 0.7 fusion.7
  (30 shorter events, 0.2 us)
Async XLA Ops:
  7.2 73.9 %copy-start = (bf16[3,192,768]{2,1,0:T(8,128)(2,1)S(1)}, bf16[3,192,768]{2,1,0:T(8,128)(2,1)}, u32[]{:S(2)}) copy-start(bf16[3,192,768]{2,1,0:T(8,128)(2,1)} %param.15) | copy-start | bytes 2654212
  7.2 67.6 %all-gather.2.cloned.1.call-start = ((), (), s32[]{:S(2)}) async-start(), calls=%async_computation.5 | async-start | bytes 5898240 | tf_op jit(solution)/shard_map/all_gather | solution.py:58
  8.0 2.5 %copy-start.4 = (bf16[1,8,768]{2,1,0:T(8,128)(2,1)S(1)}, bf16[1,8,768]{2,1,0:T(8,128)(2,1)}, u32[]{:S(2)}) copy-start(bf16[1,8,768]{2,1,0:T(8,128)(2,1)} %param.16) | copy-start | bytes 36868
  57.9 1.5 copy-start.8
  59.4 6.8 %copy-start.10 = (s32[3]{0:T(128)S(1)}, s32[3]{0:T(128)}, u32[]{:S(2)}) copy-start(s32[3]{0:T(128)} %param.11) | copy-start | bytes 40
  61.9 12.3 %all-to-all-start.2 = ((bf16[4,3,8,768]{3,2,1,0:T(8,128)(2,1)}), bf16[4,3,8,768]{3,2,1,0:T(8,128)(2,1)S(1)}, u32[]{:S(2)}, u32[]{:S(2)}) async-start(bf16[4,3,8,768]{3,2,1,0:T(8,128)(2,1)} %broadcast_in_dim.66), calls=%async_computation.2 | async-start | bytes 294912 | tf_op jit(solution)/shard_map/all_to_all | solution.py:12
  79.0 2.4 %copy-start.2 = (bf16[3,256,768]{2,1,0:T(8,128)(2,1)}, bf16[3,256,768]{2,1,0:T(8,128)(2,1)S(1)}, u32[]{:S(2)}) copy-start(bf16[3,256,768]{2,1,0:T(8,128)(2,1)S(1)} %get-tuple-element.17) | copy-start | bytes 3538948
  79.0 1.7 %copy-start.1 = (bf16[3,256,768]{2,1,0:T(8,128)(2,1)S(1)}, bf16[3,256,768]{2,1,0:T(8,128)(2,1)}, u32[]{:S(2)}) copy-start(bf16[3,256,768]{2,1,0:T(8,128)(2,1)} %broadcast_select_fusion) | copy-start | bytes 3538948
  80.7 0.7 copy-start.3
  80.7 10.0 %copy-start.9 = (s32[3,1]{0,1:T(1,128)S(1)}, s32[3,1]{0,1:T(1,128)}, u32[]{:S(2)}) copy-start(s32[3,1]{0,1:T(1,128)} %param.12) | copy-start | bytes 40
  94.3 14.6 %copy-start.6 = (f32[1,768]{1,0:T(1,128)S(1)}, f32[1,768]{1,0:T(1,128)}, u32[]{:S(2)}) copy-start(f32[1,768]{1,0:T(1,128)} %param.18) | copy-start | bytes 9220
  94.3 14.6 %copy-start.7 = (f32[1,768]{1,0:T(1,128)S(1)}, f32[1,768]{1,0:T(1,128)}, u32[]{:S(2)}) copy-start(f32[1,768]{1,0:T(1,128)} %param.19) | copy-start | bytes 9220
  94.3 57.0 %all-to-all-start.4 = ((bf16[128,8,768]{2,1,0:T(8,128)(2,1)}), bf16[128,8,768]{2,1,0:T(8,128)(2,1)S(1)}, u32[]{:S(2)}, u32[]{:S(2)}) async-start(bf16[128,8,768]{2,1,0:T(8,128)(2,1)} %copy.21), calls=%async_computation.4 | async-start | bytes 3145728 | tf_op jit(solution)/shard_map/all_to_all | solution.py:86
  108.6 43.0 %copy-start.5 = (f32[1,8,768]{2,1,0:T(8,128)S(1)}, f32[1,8,768]{2,1,0:T(8,128)}, u32[]{:S(2)}) copy-start(f32[1,8,768]{2,1,0:T(8,128)} %param.17) | copy-start | bytes 73732
Sparse Core Ops, SparseCore 0:
  10.7 64.0 all-gather.1
where the time goes:
time: 160 us; the launch traced here: 159 us
  blocking collectives  54.6 us (34%)
  waiting for transfers between devices  49.6 us (31%)
  starting transfers between devices  18.6 us (12%)
  between operations  14.9 us (9%)
  matrix products  8.64 us (5%)
  local copies, waits for them, and re-layouts  7.73 us (5%)
  other arithmetic  4.97 us (3%)
    all_to_all x2, blocking collectives, copy_for_each(): lax.all_to_all(jnp.broadcast_to(x[None], (length, *x.shape)), axis, 0, 0,...  45.4 us
    all_to_all x1, waiting for transfers between devices, body(): lax.all_to_all(dense.astype(jnp.bfloat16), SUB, split_axis=0, concat_axis...  42.3 us
    all_to_all x1, starting transfers between devices, body(): lax.all_to_all(dense.astype(jnp.bfloat16), SUB, split_axis=0, concat_axis...  14.3 us
    all_to_all x1, blocking collectives, sent_and_summed(): lax.all_to_all(tiles, axis, split_axis=0, concat_axis=0, tiled=True)  9.28 us
    all_to_all x1, waiting for transfers between devices, copy_for_each(): lax.all_to_all(jnp.broadcast_to(x[None], (length, *x.shape)), axis, 0, 0,...  6.74 us
    all_to_all x1, starting transfers between devices, copy_for_each(): lax.all_to_all(jnp.broadcast_to(x[None], (length, *x.shape)), axis, 0, 0,...  4.31 us
    dot_general x1, matrix products, body(): jnp.einsum('sfg,sgn->sfn', front_inverse, piece, preferred_element_type=j...  4.2 us
  transfers between devices with their start and end apart: 3, of which 3 were waited for; matrix products, arithmetic and copies ran while one was open for 4% of the time, Pallas kernels for 0%

commit v1 on v0

v1 whole, which is shorter than its diff:
```python
import jax
import jax.numpy as jnp
from jax import lax
from jax.sharding import PartitionSpec as P


def shifted(x, axis, step):
    n = lax.axis_size(axis)
    return lax.ppermute(x, axis, [(j, (j + step) % n) for j in range(n)])


def column_block(x, index, width):
    return lax.dynamic_slice_in_dim(x, index * width, width, axis=x.ndim - 1)


def body(
    lengths, owners, front_inverse, coupling, stiffness, displacement, forcing, lumped_mass, damping
):
    nharm = lax.axis_size("harm")
    harm_idx = lax.axis_index("harm")
    nsub = lax.axis_size("sub")
    front_q = coupling.shape[1]
    width = coupling.shape[2]
    width_q = stiffness.shape[1]
    rows_q = displacement.shape[1]

    own_rows = harm_idx * front_q + jnp.arange(front_q, dtype=jnp.int32)
    live_rows = own_rows[None, :] < lengths[:, None]
    masked = jnp.where(live_rows[:, :, None], coupling, jnp.zeros_like(coupling))

    from_left = shifted(masked, "harm", 1)
    from_right = shifted(masked, "harm", -1)
    half = front_q // 2
    far = jnp.concatenate(
        [shifted(from_left[:, :half], "harm", 1), shifted(from_right[:, half:], "harm", -1)], axis=1
    )

    def modes_term(block, step):
        cols = column_block(front_inverse, (harm_idx + step) % nharm, front_q)
        return jnp.einsum("sfg,sgn->sfn", cols, block, preferred_element_type=jnp.float32)

    modes = modes_term(masked, 0)
    modes = modes + modes_term(from_left, -1)
    modes = modes + modes_term(from_right, 1)
    modes = (modes + modes_term(far, 2)).astype(jnp.bfloat16)

    disp_rows = displacement[0]
    near_block = shifted(disp_rows, "sub", nsub // 2)
    every_block = lax.all_gather(disp_rows, "sub")
    third_block = lax.dynamic_index_in_dim(every_block, owners[2, 0], 0, keepdims=False)
    picked = jnp.stack([near_block, third_block])
    own_pair = lax.all_gather(picked, "harm", axis=1, tiled=True)
    own_disp = jnp.stack([own_pair[0], own_pair[0], own_pair[1]])

    partial_y = jnp.einsum("shn,sfn->shf", own_disp, masked, preferred_element_type=jnp.float32)
    whole_y = lax.all_gather(partial_y, "harm", axis=2, tiled=True)
    inner = -jnp.einsum(
        "shg,sfg->shf",
        whole_y,
        front_inverse.astype(jnp.float32),
        precision=lax.Precision.HIGHEST,
        preferred_element_type=jnp.float32,
    )
    interior = jnp.where(live_rows[:, None, :], inner, jnp.float32(0.0)).astype(jnp.bfloat16)

    disp_cols = column_block(own_disp, harm_idx, width_q)
    contrib = jnp.einsum("shf,sfn->shn", interior, masked, preferred_element_type=jnp.float32)
    contrib = contrib + jnp.einsum(
        "shj,sjn->shn", disp_cols, stiffness, preferred_element_type=jnp.float32
    )
    pair_sum = jnp.stack([contrib[0] + contrib[1], contrib[2]])
    pair_rows = lax.psum_scatter(pair_sum, "harm", scatter_dimension=1, tiled=True)

    near_sum = shifted(pair_rows[0], "sub", nsub // 2)
    slots = jnp.arange(nsub, dtype=jnp.int32)[:, None, None] == owners[2, 0]
    spread = jnp.where(slots, pair_rows[1][None], jnp.float32(0.0))
    far_sum = lax.psum_scatter(spread, "sub", scatter_dimension=0, tiled=True)
    gathered = (near_sum[None] + far_sum)

    pairs_all = rows_q * nharm // 2
    rows = harm_idx * rows_q + jnp.arange(rows_q, dtype=jnp.int32)
    pair = (rows // 2).astype(jnp.float32)
    parity = (rows % 2).astype(jnp.float32)
    freq = 1.5 * (pair + 1.0) / pairs_all
    sign = 1.0 - 2.0 * parity
    disp = displacement.astype(jnp.float32)
    partner = disp.reshape(1, rows_q // 2, 2, width)[:, :, ::-1, :].reshape(1, rows_q, width)
    residual = (
        gathered
        - (freq * freq)[None, :, None] * lumped_mass[:, None, :] * disp
        + (sign * freq)[None, :, None] * damping[:, None, :] * partner
        - forcing
    )
    return (interior, residual, modes)


def solution(mesh):
    placed = (
        P("sub"),
        P("sub", None),
        P("sub", "harm", None),
        P("sub", "harm", None),
        P("sub", "harm", None),
        P("sub", "harm", None),
        P("sub", "harm", None),
        P("sub", None),
        P("sub", None),
    )
    return jax.shard_map(
        body,
        mesh=mesh,
        in_specs=placed,
        out_specs=(P("sub", None, "harm"), P("sub", "harm", None), P("sub", "harm", None)),
        check_vma=False,
    )
```

time: 160 us -> 364 us (2.27)
  the two profiles are of different devices: /device:TPU:8 before, /device:TPU:4 now
where the time goes in v1:
time: 364 us; the launch traced here: 363 us
  waiting for transfers between devices  272 us (75%)
  starting transfers between devices  31.4 us (9%)
  blocking collectives  23.4 us (6%)
  between operations  16 us (4%)
  matrix products  8.26 us (2%)
  other arithmetic  6.92 us (2%)
  local copies, waits for them, and re-layouts  5.23 us (1%)
    reduce_scatter x1, waiting for transfers between devices, body(): far_sum = lax.psum_scatter(spread, 'sub', scatter_dimension=0, tiled=True)  155 us
    all_gather x1, waiting for transfers between devices, body(): every_block = lax.all_gather(disp_rows, 'sub')  74.2 us
    ppermute x6, starting transfers between devices, shifted(): return lax.ppermute(x, axis, [(j, (j + step) % n) for j in range(n)])  31.2 us
    reduce_scatter x1, waiting for transfers between devices, body(): lax.psum_scatter(pair_sum, 'harm', scatter_dimension=1, tiled=True)  21.6 us
    ppermute x6, waiting for transfers between devices, shifted(): return lax.ppermute(x, axis, [(j, (j + step) % n) for j in range(n)])  21 us
    all_gather x1, blocking collectives, body(): whole_y = lax.all_gather(partial_y, 'harm', axis=2, tiled=True)  12.6 us
    all_gather x1, blocking collectives, body(): own_pair = lax.all_gather(picked, 'harm', axis=1, tiled=True)  10.7 us
  transfers between devices with their start and end apart: 9, of which 5 were waited for; matrix products, arithmetic and copies ran while one was open for 4% of the time, Pallas kernels for 0%

profile of v1, /device:TPU:4, one launch (start us, length us, event | category | flops | bytes accessed | tf_op | source)
XLA Modules:
  0.0 363.1 jit_solution(845991593042576625)
XLA Ops:
  7.2 0.7 all-gather.2.cloned.1.call-update
  8.0 10.9 %collective-permute-start = (bf16[8,768]{1,0:T(8,128)(2,1)}, bf16[8,768]{1,0:T(8,128)(2,1)S(1)}, u32[]{:S(2)}, u32[]{:S(2)}) collective-permute-start(bf16[8,768]{1,0:T(8,128)(2,1)} %bitcast.24), channel_id=1, source_target_pairs={{0,256},{4,260},{8,264},{12,268},{16,272},{20,276},{24,280},{28,28... | collective-permute-start | bytes 36872 | tf_op jit(solution)/shard_map/ppermute | solution.py:9
  18.9 1.2 slice.31
  22.1 0.7 broadcast_compare_fusion
  22.8 1.4 broadcast_select_fusion.1
  24.3 74.2 %all-gather.2.cloned.1.call-done = bf16[128,8,768]{2,1,0:T(8,128)(2,1)} async-done(((bf16[1,8,768]{2,1,0:T(8,128)(2,1)}), bf16[128,8,768]{2,1,0:T(8,128)(2,1)}) %all-gather.2.cloned.1.call-update) | async-done | bytes 1572880 | tf_op jit(solution)/shard_map/all_gather | solution.py:49
  98.4 0.7 constant_dynamic-slice_fusion
  99.1 10.7 %all_gather.10 = bf16[2,32,768]{2,1,0:T(8,128)(2,1)S(1)} all-gather(bf16[2,8,768]{2,1,0:T(8,128)(2,1)S(1)} %pad_maximum_fusion.3), channel_id=1, replica_groups=mesh['sub'=128,'harm'=4] {'harm'}, dimensions={1}, use_global_device_ids=true | all-gather | bytes 122880 | tf_op jit(solution)/shard_map/all_gather | solution.py:52
  109.9 0.5 fusion.15
  110.3 12.6 %all_gather.11 = f32[3,32,1024]{2,1,0:T(8,128)S(1)} all-gather(f32[3,32,256]{2,1,0:T(8,128)S(1)} %fusion.15), channel_id=1, replica_groups=mesh['sub'=128,'harm'=4] {'harm'}, dimensions={2}, use_global_device_ids=true | all-gather | bytes 491520 | tf_op jit(solution)/shard_map/all_gather | solution.py:56
  123.0 1.5 fusion.7
  124.5 0.3 fusion.34
  124.8 0.4 convolution_add_fusion
  125.2 0.7 pad_maximum_fusion
  125.9 0.7 iota_compare_fusion
  126.6 21.6 %reduce-scatter.3.cloned.1.call-done = f32[2,8,768]{2,1,0:T(8,128)} async-done(((f32[2,32,768]{2,1,0:T(8,128)}), f32[2,8,768]{2,1,0:T(8,128)}) %reduce-scatter.3.cloned.1.call-update) | async-done | bytes 49168 | tf_op jit(solution)/shard_map/reduce_scatter | solution.py:72
  148.2 0.8 slice_bitcast_fusion.1
  149.0 1.9 broadcast_select_fusion
  150.9 3.0 collective-permute-start.3
  153.9 3.0 collective-permute-start.2
  157.4 0.5 fusion.13
  157.9 20.7 %collective-permute-done.3 = bf16[3,256,768]{2,1,0:T(8,128)(2,1)} collective-permute-done((bf16[3,256,768]{2,1,0:T(8,128)(2,1)S(1)}, bf16[3,256,768]{2,1,0:T(8,128)(2,1)}, u32[]{:S(2)}, u32[]{:S(2)}) %collective-permute-start.3) | collective-permute-done | bytes 1179680 | tf_op jit(solution)/shard_map/ppermute | solution.py:9
  178.5 1.1 slice.47
  179.6 2.4 collective-permute-start.5
  182.0 1.1 slice.46
  183.1 3.7 %collective-permute-start.4 = (bf16[3,128,768]{2,1,0:T(8,128)(2,1)S(1)}, bf16[3,128,768]{2,1,0:T(8,128)(2,1)S(1)}, u32[]{:S(2)}, u32[]{:S(2)}) collective-permute-start(bf16[3,128,768]{2,1,0:T(8,128)(2,1)S(1)} %slice.46), channel_id=1, source_target_pairs={{0,1},{1,2},{2,3},{3,0},{4,5},{5,6},{6,7},{7,4},{8,9},{9,10},{10,1... | collective-permute-start | bytes 1769480 | tf_op jit(solution)/shard_map/ppermute | solution.py:9
  186.9 1.8 fusion.9
  188.6 1.8 fusion.11
  190.4 8.2 %collective-permute-start.1 = (f32[8,768]{1,0:T(8,128)S(1)}, f32[8,768]{1,0:T(8,128)S(1)}, u32[]{:S(2)}, u32[]{:S(2)}) collective-permute-start(f32[8,768]{1,0:T(8,128)S(1)} %get-tuple-element.5), channel_id=1, source_target_pairs={{0,256},{4,260},{8,264},{12,268},{16,272},{20,276},{24,280},{28,28... | collective-permute-start | bytes 73736 | tf_op jit(solution)/shard_map/ppermute | solution.py:9
  198.7 1.7 add_convert_fusion
  200.6 154.5 %reduce-scatter.5.cloned.1.call-done = f32[1,8,768]{2,1,0:T(8,128)} async-done(((f32[128,8,768]{2,1,0:T(8,128)}), f32[1,8,768]{2,1,0:T(8,128)}) %reduce-scatter.5.cloned.1.call-update) | async-done | bytes 24592 | tf_op jit(solution)/shard_map/reduce_scatter | solution.py:77
  355.2 1.4 fusion.20
  (34 shorter events, 0.8 us)
Async XLA Ops:
  7.2 115.8 %copy-start = (bf16[3,256,1024]{2,1,0:T(8,128)(2,1)S(1)}, bf16[3,256,1024]{2,1,0:T(8,128)(2,1)}, u32[]{:S(2)}) copy-start(bf16[3,256,1024]{2,1,0:T(8,128)(2,1)} %param.11) | copy-start | bytes 4718596
  7.2 91.2 %all-gather.2.cloned.1.call-start = ((), (), s32[]{:S(2)}) async-start(), calls=%async_computation.2 | async-start | bytes 1585152 | tf_op jit(solution)/shard_map/all_gather | solution.py:49
  7.9 140.3 %reduce-scatter.3.cloned.1.call-start = ((), (), s32[]{:S(2)}) async-start(), calls=%async_computation.3 | async-start | bytes 245760 | tf_op jit(solution)/shard_map/reduce_scatter | solution.py:72
  8.0 91.2 %collective-permute-start = (bf16[8,768]{1,0:T(8,128)(2,1)}, bf16[8,768]{1,0:T(8,128)(2,1)S(1)}, u32[]{:S(2)}, u32[]{:S(2)}) collective-permute-start(bf16[8,768]{1,0:T(8,128)(2,1)} %bitcast.24), channel_id=1, source_target_pairs={{0,256},{4,260},{8,264},{12,268},{16,272},{20,276},{24,280},{28,28... | collective-permute-start | bytes 36872 | tf_op jit(solution)/shard_map/ppermute | solution.py:9
  123.0 1.8 copy-start.1
  124.4 0.7 copy-start.2
  125.9 229.3 %reduce-scatter.5.cloned.1.call-start = ((), (), s32[]{:S(2)}) async-start(), calls=%async_computation.4 | async-start | bytes 3170304 | tf_op jit(solution)/shard_map/reduce_scatter | solution.py:77
  150.9 6.1 %copy-start.3 = (bf16[1,8,768]{2,1,0:T(8,128)(2,1)S(1)}, bf16[1,8,768]{2,1,0:T(8,128)(2,1)}, u32[]{:S(2)}) copy-start(bf16[1,8,768]{2,1,0:T(8,128)(2,1)} %param.14) | copy-start | bytes 36868
  150.9 6.1 %copy-start.5 = (f32[1,768]{1,0:T(1,128)S(1)}, f32[1,768]{1,0:T(1,128)}, u32[]{:S(2)}) copy-start(f32[1,768]{1,0:T(1,128)} %param.16) | copy-start | bytes 9220
  150.9 6.2 %copy-start.6 = (f32[1,768]{1,0:T(1,128)S(1)}, f32[1,768]{1,0:T(1,128)}, u32[]{:S(2)}) copy-start(f32[1,768]{1,0:T(1,128)} %param.17) | copy-start | bytes 9220
  150.9 27.6 %collective-permute-start.3 = (bf16[3,256,768]{2,1,0:T(8,128)(2,1)S(1)}, bf16[3,256,768]{2,1,0:T(8,128)(2,1)}, u32[]{:S(2)}, u32[]{:S(2)}) collective-permute-start(bf16[3,256,768]{2,1,0:T(8,128)(2,1)S(1)} %broadcast_select_fusion.1), channel_id=1, source_target_pairs={{0,3},{1,0},{2,1},{3,2},{4,7},{5,4},{6,5},{7,6},{8,11},{9,8},{10,9... | collective-permute-start | bytes 3538952 | tf_op jit(solution)/shard_map/ppermute | solution.py:9
  153.9 28.1 %collective-permute-start.2 = (bf16[3,256,768]{2,1,0:T(8,128)(2,1)S(1)}, bf16[3,256,768]{2,1,0:T(8,128)(2,1)}, u32[]{:S(2)}, u32[]{:S(2)}) collective-permute-start(bf16[3,256,768]{2,1,0:T(8,128)(2,1)S(1)} %broadcast_select_fusion.1), channel_id=1, source_target_pairs={{0,1},{1,2},{2,3},{3,0},{4,5},{5,6},{6,7},{7,4},{8,9},{9,10},{10,1... | collective-permute-start | bytes 3538952 | tf_op jit(solution)/shard_map/ppermute | solution.py:9
  179.6 19.1 %collective-permute-start.5 = (bf16[3,128,768]{2,1,0:T(8,128)(2,1)S(1)}, bf16[3,128,768]{2,1,0:T(8,128)(2,1)S(1)}, u32[]{:S(2)}, u32[]{:S(2)}) collective-permute-start(bf16[3,128,768]{2,1,0:T(8,128)(2,1)S(1)} %slice.47), channel_id=1, source_target_pairs={{0,3},{1,0},{2,1},{3,2},{4,7},{5,4},{6,5},{7,6},{8,11},{9,8},{10,9... | collective-permute-start | bytes 1769480 | tf_op jit(solution)/shard_map/ppermute | solution.py:9
  183.1 15.6 %collective-permute-start.4 = (bf16[3,128,768]{2,1,0:T(8,128)(2,1)S(1)}, bf16[3,128,768]{2,1,0:T(8,128)(2,1)S(1)}, u32[]{:S(2)}, u32[]{:S(2)}) collective-permute-start(bf16[3,128,768]{2,1,0:T(8,128)(2,1)S(1)} %slice.46), channel_id=1, source_target_pairs={{0,1},{1,2},{2,3},{3,0},{4,5},{5,6},{6,7},{7,4},{8,9},{9,10},{10,1... | collective-permute-start | bytes 1769480 | tf_op jit(solution)/shard_map/ppermute | solution.py:9
  190.4 164.7 %copy-start.4 = (f32[1,8,768]{2,1,0:T(8,128)S(1)}, f32[1,8,768]{2,1,0:T(8,128)}, u32[]{:S(2)}) copy-start(f32[1,8,768]{2,1,0:T(8,128)} %param.15) | copy-start | bytes 73732
  190.4 10.2 %collective-permute-start.1 = (f32[8,768]{1,0:T(8,128)S(1)}, f32[8,768]{1,0:T(8,128)S(1)}, u32[]{:S(2)}, u32[]{:S(2)}) collective-permute-start(f32[8,768]{1,0:T(8,128)S(1)} %get-tuple-element.5), channel_id=1, source_target_pairs={{0,256},{4,260},{8,264},{12,268},{16,272},{20,276},{24,280},{28,28... | collective-permute-start | bytes 73736 | tf_op jit(solution)/shard_map/ppermute | solution.py:9
Sparse Core Ops, SparseCore 0:
  11.2 87.1 all-gather.1
  126.0 22.1 reduce-scatter.2
  153.2 201.8 reduce-scatter.4

commit v2 on v0

--- a/solution.py
+++ b/solution.py
@@ -41,6 +41,23 @@
     return arrived.astype(jnp.float32).sum(axis=0)
 
 
+def shifted(x, axis, step):
+    n = lax.axis_size(axis)
+    return lax.ppermute(x, axis, [(j, (j + step) % n) for j in range(n)])
+
+
+def ring_whole(x, idx, n):
+    from_left = shifted(x, "harm", 1)
+    from_right = shifted(x, "harm", -1)
+    half = x.shape[1] // 2
+    far = jnp.concatenate(
+        [shifted(from_left[:, :half], "harm", 1), shifted(from_right[:, half:], "harm", -1)], axis=1
+    )
+    blocks = jnp.stack([x, from_right, far, from_left])
+    order = (jnp.arange(n, dtype=jnp.int32) - idx) % n
+    return jnp.concatenate([blocks[order[j]] for j in range(n)], axis=1)
+
+
 def body(
     lengths, owners, front_inverse, coupling, stiffness, displacement, forcing, lumped_mass, damping
 ):
@@ -55,7 +72,7 @@
     masked = jnp.where(live_rows[:, :, None], coupling, jnp.zeros_like(coupling))
     longest = jnp.max(lengths)
     empty = jnp.zeros((masked.shape[0], front_q, width), jnp.float32)
-    piece = lax.all_gather(masked, "harm", axis=1, tiled=True)
+    piece = ring_whole(masked, harm_idx, nharm)
     modes = lax.cond(
         jnp.int32(0) < longest,
         lambda: jnp.einsum(

time: 160 us -> 168 us (1.050)
  blocking collectives: 54.6 us -> 15.6 us
  starting transfers between devices: 18.6 us -> 47.7 us
  waiting for transfers between devices: 49.6 us -> 64.3 us
  between operations: 14.9 us -> 9.12 us
  local copies, waits for them, and re-layouts: 7.73 us -> 12.7 us
  other arithmetic: 4.97 us -> 8.65 us
    all_to_all x2 -> x1, blocking collectives: 45.4 us -> 5 us  [copy_for_each(): lax.all_to_all(jnp.broadcast_to(x[None], (length, *x.shape)), axis, 0, 0,...]
    ppermute x0 -> x4, waiting for transfers between devices: none -> 22 us  [shifted(): return lax.ppermute(x, axis, [(j, (j + step) % n) for j in range(n)])]
    all_to_all x1 -> x2, starting transfers between devices: 4.31 us -> 20 us  [copy_for_each(): lax.all_to_all(jnp.broadcast_to(x[None], (length, *x.shape)), axis, 0, 0,...]
    ppermute x0 -> x4, starting transfers between devices: none -> 14.1 us  [shifted(): return lax.ppermute(x, axis, [(j, (j + step) % n) for j in range(n)])]
    all_to_all x1 -> x2, waiting for transfers between devices: 6.74 us -> 0.01 us  [copy_for_each(): lax.all_to_all(jnp.broadcast_to(x[None], (length, *x.shape)), axis, 0, 0,...]
    another operation x0 -> x3, other arithmetic: none -> 4.23 us  [ring_whole(): blocks = jnp.stack([x, from_right, far, from_left])]
    slice x0 -> x3, local copies, waits for them, and re-layouts: none -> 2.53 us  [the longest x1 0.96 us: ring_whole(): from_right[:, half:]]
    concatenate x0 -> x1, other arithmetic: none -> 2.49 us  [ring_whole(): return jnp.concatenate([blocks[order[j]] for j in range(n)], axis=1)]
  transfers between devices with their start and end apart: 3 -> 7, of which waited for: 3 -> 2; matrix products, arithmetic and copies ran while one was open for 4% -> 6% of each run, Pallas kernels for 0% -> 0%
where the time goes in v2:
time: 168 us; the launch traced here: 167 us
  waiting for transfers between devices  64.3 us (38%)
  starting transfers between devices  47.7 us (28%)
  blocking collectives  15.6 us (9%)
  local copies, waits for them, and re-layouts  12.7 us (8%)
  between operations  9.12 us (5%)
  other arithmetic  8.65 us (5%)
  matrix products  8.63 us (5%)
    all_to_all x1, waiting for transfers between devices, body(): lax.all_to_all(dense.astype(jnp.bfloat16), SUB, split_axis=0, concat_axis...  42.3 us
    ppermute x4, waiting for transfers between devices, shifted(): return lax.ppermute(x, axis, [(j, (j + step) % n) for j in range(n)])  22 us
    all_to_all x2, starting transfers between devices, copy_for_each(): lax.all_to_all(jnp.broadcast_to(x[None], (length, *x.shape)), axis, 0, 0,...  20 us
    ppermute x4, starting transfers between devices, shifted(): return lax.ppermute(x, axis, [(j, (j + step) % n) for j in range(n)])  14.1 us
    all_to_all x1, starting transfers between devices, body(): lax.all_to_all(dense.astype(jnp.bfloat16), SUB, split_axis=0, concat_axis...  13.6 us
    all_to_all x1, blocking collectives, sent_and_summed(): lax.all_to_all(tiles, axis, split_axis=0, concat_axis=0, tiled=True)  10.6 us
    all_to_all x1, blocking collectives, copy_for_each(): lax.all_to_all(jnp.broadcast_to(x[None], (length, *x.shape)), axis, 0, 0,...  5 us
    another operation x3, other arithmetic, ring_whole(): blocks = jnp.stack([x, from_right, far, from_left])  4.23 us
  transfers between devices with their start and end apart: 7, of which 2 were waited for; matrix products, arithmetic and copies ran while one was open for 6% of the time, Pallas kernels for 0%

profile of v2, /device:TPU:8, one launch (start us, length us, event | category | flops | bytes accessed | tf_op | source)
XLA Modules:
  0.0 166.7 jit_solution(8329842622917410969)
XLA Ops:
  0.7 1.8 %broadcast_in_dim.39 = bf16[64,1,8,768]{3,2,1,0:T(8,128)(2,1)} broadcast(bf16[8,768]{1,0:T(8,128)(2,1)} %bitcast.62), dimensions={2,3} | broadcast | bytes 798720 | tf_op jit(solution)/shard_map/broadcast_in_dim | solution.py:12
  2.5 16.6 %all-to-all-start = ((bf16[64,1,8,768]{3,2,1,0:T(8,128)(2,1)}), bf16[64,1,8,768]{3,2,1,0:T(8,128)(2,1)S(1)}, u32[]{:S(2)}, u32[]{:S(2)}) async-start(bf16[64,1,8,768]{3,2,1,0:T(8,128)(2,1)} %broadcast_in_dim.39), calls=%async_computation | async-start | bytes 1572864 | tf_op jit(solution)/shard_map/all_to_all | solution.py:12
  19.3 3.4 %collective-permute-start.1 = (bf16[3,256,768]{2,1,0:T(8,128)(2,1)S(1)}, bf16[3,256,768]{2,1,0:T(8,128)(2,1)S(1)}, u32[]{:S(2)}, u32[]{:S(2)}) collective-permute-start(bf16[3,256,768]{2,1,0:T(8,128)(2,1)S(1)} %broadcast_select_fusion), channel_id=1, source_target_pairs={{0,1},{1,2},{2,3},{3,0},{4,5},{5,6},{6,7},{7,4},{8,9},{9,10},{10,1... | collective-permute-start | bytes 3538952 | tf_op jit(solution)/shard_map/ppermute | solution.py:46
  22.7 3.7 %collective-permute-start = (bf16[3,256,768]{2,1,0:T(8,128)(2,1)S(1)}, bf16[3,256,768]{2,1,0:T(8,128)(2,1)S(1)}, u32[]{:S(2)}, u32[]{:S(2)}) collective-permute-start(bf16[3,256,768]{2,1,0:T(8,128)(2,1)S(1)} %broadcast_select_fusion), channel_id=1, source_target_pairs={{0,3},{1,0},{2,1},{3,2},{4,7},{5,4},{6,5},{7,6},{8,11},{9,8},{10,9... | collective-permute-start | bytes 3538952 | tf_op jit(solution)/shard_map/ppermute | solution.py:46
  26.4 1.2 fusion.30
  27.6 22.0 %collective-permute-done.1 = bf16[3,256,768]{2,1,0:T(8,128)(2,1)S(1)} collective-permute-done((bf16[3,256,768]{2,1,0:T(8,128)(2,1)S(1)}, bf16[3,256,768]{2,1,0:T(8,128)(2,1)S(1)}, u32[]{:S(2)}, u32[]{:S(2)}) %collective-permute-start.1) | collective-permute-done | bytes 1179680 | tf_op jit(solution)/shard_map/ppermute | solution.py:46
  49.6 0.9 slice.24
  50.5 2.2 %collective-permute-start.2 = (bf16[3,128,768]{2,1,0:T(8,128)(2,1)}, bf16[3,128,768]{2,1,0:T(8,128)(2,1)}, u32[]{:S(2)}, u32[]{:S(2)}) collective-permute-start(bf16[3,128,768]{2,1,0:T(8,128)(2,1)} %slice.24), channel_id=1, source_target_pairs={{0,1},{1,2},{2,3},{3,0},{4,5},{5,6},{6,7},{7,4},{8,9},{9,10},{10,1... | collective-permute-start | bytes 1769480 | tf_op jit(solution)/shard_map/ppermute | solution.py:46
  52.7 1.0 slice.25
  54.0 4.9 %collective-permute-start.3 = (bf16[3,128,768]{2,1,0:T(8,128)(2,1)}, bf16[3,128,768]{2,1,0:T(8,128)(2,1)}, u32[]{:S(2)}, u32[]{:S(2)}) collective-permute-start(bf16[3,128,768]{2,1,0:T(8,128)(2,1)} %slice.25), channel_id=1, source_target_pairs={{0,3},{1,0},{2,1},{3,2},{4,7},{5,4},{6,5},{7,6},{8,11},{9,8},{10,9... | collective-permute-start | bytes 1769480 | tf_op jit(solution)/shard_map/ppermute | solution.py:46
  59.2 5.0 %all_to_all.25 = bf16[2,64,1,8,768]{4,1,3,2,0:T(8,128)(2,1)S(1)} all-to-all(bf16[2,64,1,8,768]{4,1,3,2,0:T(8,128)(2,1)S(1)} %broadcast_in_dim.65), channel_id=1, replica_groups=mesh['sub_0'=8,'sub_1'=8,'sub_2'=2,'harm'=4] {'sub_2'}, dimensions={0} | all-to-all | bytes 3145728 | tf_op jit(solution)/shard_map/all_to_all | solution.py:12
  64.2 1.6 copy.15
  65.8 1.5 reshape_reshape.3
  67.3 1.8 %convolution_convert_fusion.2 = bf16[3,8,768]{2,0,1:T(4,128)(2,1)S(1)} fusion(bf16[128,8,768]{2,0,1:T(8,128)(2,1)} %reshape_reshape.3, s32[3]{0:T(128)S(1)} %bitcast.63), kind=kOutput, calls=%fused_computation.17 | convolution fusion | flops 4737408 | bytes 1609740 | tf_op jit(solution)/shard_map/so,ohn->shn/dot_general | solution.py:87
  69.1 0.7 broadcast_in_dim.66
  69.8 3.5 %all-to-all-start.2 = ((bf16[4,3,8,768]{3,2,1,0:T(8,128)(2,1)}), bf16[4,3,8,768]{3,2,1,0:T(8,128)(2,1)S(1)}, u32[]{:S(2)}, u32[]{:S(2)}) async-start(bf16[4,3,8,768]{3,2,1,0:T(8,128)(2,1)} %broadcast_in_dim.66), calls=%async_computation.2 | async-start | bytes 294912 | tf_op jit(solution)/shard_map/all_to_all | solution.py:12
  73.2 0.6 fusion.21
  78.9 0.6 reduce_max.9
  82.7 1.3 maximum_bitcast_fusion
  84.0 1.7 %pad_maximum_fusion = bf16[4,3,256,768]{3,2,1,0:T(8,128)(2,1)S(1)} fusion(bf16[1,3,256,768]{3,2,1,0:T(8,128)(2,1)S(1)} %bitcast.59, bf16[1,3,256,768]{3,2,1,0:T(8,128)(2,1)S(1)} %maximum_bitcast_fusion, bf16[1,3,256,768]{3,2,1,0:T(8,128)(2,1)} %bitcast.60, bf16[1,3,256,768]{3,2,1,0:T(8,128)(2,1)S(1)} %copy-done.1), kind=kLoop, calls=%fused_computation.1 | loop fusion | flops 7077888 | bytes 9437184 | tf_op jit(solution)/shard_map/stack | solution.py:56
  86.1 2.5 %pad_maximum_fusion.1 = bf16[3,1024,768]{2,1,0:T(8,128)(2,1)} fusion(bf16[3,256,768]{2,1,0:T(8,128)(2,1)S(1)} %get-tuple-element.16, bf16[3,256,768]{2,1,0:T(8,128)(2,1)S(1)} %get-tuple-element.17, bf16[3,256,768]{2,1,0:T(8,128)(2,1)S(1)} %get-tuple-element.18, bf16[3,256,768]{2,1,0:T(8,128)(2,1)S(1)} %get-tuple-element.15), kind=kLoop, calls=%fused_computation.2 | loop fusion | flops 18874368 | bytes 9437184 | tf_op jit(solution)/shard_map/concatenate | solution.py:58
  88.6 4.2 %conditional.1 = (bf16[3,256,768]{2,1,0:T(8,128)(2,1)S(1)}) conditional(s32[]{:T(128)} %convert_element_type.50, () %tuple.16, (bf16[3,256,1024]{2,1,0:T(8,128)(2,1)}, bf16[3,1024,768]{2,1,0:T(8,128)(2,1)}) %tuple.17), branch_computations={%region_1.2_spmd, %region_2.3_spmd} | conditional | flops 1208549376 | bytes 7471112 | solution.py:76
  88.6 4.2 %convolution_convert_fusion = bf16[3,256,768]{2,1,0:T(8,128)(2,1)S(1)} fusion(bf16[3,256,1024]{2,1,0:T(8,128)(2,1)} %get-tuple-element.14, bf16[3,1024,768]{2,1,0:T(8,128)(2,1)} %get-tuple-element.9), kind=kOutput, calls=%fused_computation | convolution fusion | flops 1208549376 | bytes 7471104 | tf_op jit(solution)/shard_map/cond/branch_1_fun/sfg,sgn->sfn/dot_general | solution.py:78
  92.8 0.5 fusion.3
  93.3 1.2 copy-done.4
  94.8 0.4 fusion.1
  95.2 10.6 %all_to_all.26 = bf16[4,3,8,768]{3,2,1,0:T(8,128)(2,1)S(1)} all-to-all(bf16[4,3,8,768]{3,2,1,0:T(8,128)(2,1)S(1)} %bitcast.61), channel_id=1, replica_groups=mesh['sub_0'=8,'sub_1'=8,'sub_2'=2,'harm'=4] {'harm'}, dimensions={0} | all-to-all | bytes 294912 | tf_op jit(solution)/shard_map/all_to_all | solution.py:40
  105.9 1.5 convolution_convert_fusion.1
  107.4 2.0 %copy.21 = bf16[128,8,768]{2,1,0:T(8,128)(2,1)} copy(bf16[128,8,768]{2,0,1:T(8,128)(2,1)S(1)} %convolution_convert_fusion.1) | data formatting | bytes 3145728 | tf_op jit(solution)/shard_map/convert_element_type | solution.py:104
  109.4 13.6 %all-to-all-start.4 = ((bf16[128,8,768]{2,1,0:T(8,128)(2,1)}), bf16[128,8,768]{2,1,0:T(8,128)(2,1)S(1)}, u32[]{:S(2)}, u32[]{:S(2)}) async-start(bf16[128,8,768]{2,1,0:T(8,128)(2,1)} %copy.21), calls=%async_computation.4 | async-start | bytes 3145728 | tf_op jit(solution)/shard_map/all_to_all | solution.py:103
  123.4 42.3 %all-to-all-done.4 = bf16[128,8,768]{2,1,0:T(8,128)(2,1)S(1)} async-done(((bf16[128,8,768]{2,1,0:T(8,128)(2,1)}), bf16[128,8,768]{2,1,0:T(8,128)(2,1)S(1)}, u32[]{:S(2)}, u32[]{:S(2)}) %all-to-all-start.4) | async-done | bytes 1572896 | tf_op jit(solution)/shard_map/all_to_all | solution.py:103
  166.0 0.7 fusion.7
  (55 shorter events, 2.2 us)
Async XLA Ops:
  0.6 94.2 %copy-start = (bf16[3,192,768]{2,1,0:T(8,128)(2,1)S(1)}, bf16[3,192,768]{2,1,0:T(8,128)(2,1)}, u32[]{:S(2)}) copy-start(bf16[3,192,768]{2,1,0:T(8,128)(2,1)} %param.15) | copy-start | bytes 2654212
  0.6 18.4 %copy-start.15 = (s32[3]{0:T(128)S(1)}, s32[3]{0:T(128)}, u32[]{:S(2)}) copy-start(s32[3]{0:T(128)} %param.11) | copy-start | bytes 40
  0.7 18.5 %copy-start.2 = (bf16[3,256,768]{2,1,0:T(8,128)(2,1)S(1)}, bf16[3,256,768]{2,1,0:T(8,128)(2,1)}, u32[]{:S(2)}) copy-start(bf16[3,256,768]{2,1,0:T(8,128)(2,1)} %param.14) | copy-start | bytes 3538948
  2.5 56.4 %all-to-all-start = ((bf16[64,1,8,768]{3,2,1,0:T(8,128)(2,1)}), bf16[64,1,8,768]{3,2,1,0:T(8,128)(2,1)S(1)}, u32[]{:S(2)}, u32[]{:S(2)}) async-start(bf16[64,1,8,768]{3,2,1,0:T(8,128)(2,1)} %broadcast_in_dim.39), calls=%async_computation | async-start | bytes 1572864 | tf_op jit(solution)/shard_map/all_to_all | solution.py:12
  19.3 31.2 %copy-start.3 = (bf16[3,256,768]{2,1,0:T(8,128)(2,1)}, bf16[3,256,768]{2,1,0:T(8,128)(2,1)S(1)}, u32[]{:S(2)}) copy-start(bf16[3,256,768]{2,1,0:T(8,128)(2,1)S(1)} %broadcast_select_fusion) | copy-start | bytes 3538948
  19.3 30.3 %collective-permute-start.1 = (bf16[3,256,768]{2,1,0:T(8,128)(2,1)S(1)}, bf16[3,256,768]{2,1,0:T(8,128)(2,1)S(1)}, u32[]{:S(2)}, u32[]{:S(2)}) collective-permute-start(bf16[3,256,768]{2,1,0:T(8,128)(2,1)S(1)} %broadcast_select_fusion), channel_id=1, source_target_pairs={{0,1},{1,2},{2,3},{3,0},{4,5},{5,6},{6,7},{7,4},{8,9},{9,10},{10,1... | collective-permute-start | bytes 3538952 | tf_op jit(solution)/shard_map/ppermute | solution.py:46
  22.7 30.0 %collective-permute-start = (bf16[3,256,768]{2,1,0:T(8,128)(2,1)S(1)}, bf16[3,256,768]{2,1,0:T(8,128)(2,1)S(1)}, u32[]{:S(2)}, u32[]{:S(2)}) collective-permute-start(bf16[3,256,768]{2,1,0:T(8,128)(2,1)S(1)} %broadcast_select_fusion), channel_id=1, source_target_pairs={{0,3},{1,0},{2,1},{3,2},{4,7},{5,4},{6,5},{7,6},{8,11},{9,8},{10,9... | collective-permute-start | bytes 3538952 | tf_op jit(solution)/shard_map/ppermute | solution.py:46
  49.6 4.1 %copy-start.6 = (bf16[3,256,768]{2,1,0:T(8,128)(2,1)}, bf16[3,256,768]{2,1,0:T(8,128)(2,1)S(1)}, u32[]{:S(2)}) copy-start(bf16[3,256,768]{2,1,0:T(8,128)(2,1)S(1)} %collective-permute-done.1) | copy-start | bytes 3538948
  50.5 32.1 %collective-permute-start.2 = (bf16[3,128,768]{2,1,0:T(8,128)(2,1)}, bf16[3,128,768]{2,1,0:T(8,128)(2,1)}, u32[]{:S(2)}, u32[]{:S(2)}) collective-permute-start(bf16[3,128,768]{2,1,0:T(8,128)(2,1)} %slice.24), channel_id=1, source_target_pairs={{0,1},{1,2},{2,3},{3,0},{4,5},{5,6},{6,7},{7,4},{8,9},{9,10},{10,1... | collective-permute-start | bytes 1769480 | tf_op jit(solution)/shard_map/ppermute | solution.py:46
  52.7 1.3 copy-start.8
  54.0 28.7 %collective-permute-start.3 = (bf16[3,128,768]{2,1,0:T(8,128)(2,1)}, bf16[3,128,768]{2,1,0:T(8,128)(2,1)}, u32[]{:S(2)}, u32[]{:S(2)}) collective-permute-start(bf16[3,128,768]{2,1,0:T(8,128)(2,1)} %slice.25), channel_id=1, source_target_pairs={{0,3},{1,0},{2,1},{3,2},{4,7},{5,4},{6,5},{7,6},{8,11},{9,8},{10,9... | collective-permute-start | bytes 1769480 | tf_op jit(solution)/shard_map/ppermute | solution.py:46
  65.8 1.5 copy-start.14
  69.1 14.9 %copy-start.1 = (bf16[1,3,256,768]{3,2,1,0:T(8,128)(2,1)S(1)}, bf16[1,3,256,768]{3,2,1,0:T(8,128)(2,1)}, u32[]{:S(2)}) copy-start(bf16[1,3,256,768]{3,2,1,0:T(8,128)(2,1)} %fusion.30) | copy-start | bytes 3538948
  69.1 14.9 %copy-start.7 = (bf16[3,256,768]{2,1,0:T(8,128)(2,1)S(1)}, bf16[3,256,768]{2,1,0:T(8,128)(2,1)}, u32[]{:S(2)}) copy-start(bf16[3,256,768]{2,1,0:T(8,128)(2,1)} %copy-done.6) | copy-start | bytes 3538948
  69.8 12.9 %all-to-all-start.2 = ((bf16[4,3,8,768]{3,2,1,0:T(8,128)(2,1)}), bf16[4,3,8,768]{3,2,1,0:T(8,128)(2,1)S(1)}, u32[]{:S(2)}, u32[]{:S(2)}) async-start(bf16[4,3,8,768]{3,2,1,0:T(8,128)(2,1)} %broadcast_in_dim.66), calls=%async_computation.2 | async-start | bytes 294912 | tf_op jit(solution)/shard_map/all_to_all | solution.py:12
  92.8 2.4 %copy-start.5 = (bf16[3,256,768]{2,1,0:T(8,128)(2,1)}, bf16[3,256,768]{2,1,0:T(8,128)(2,1)S(1)}, u32[]{:S(2)}) copy-start(bf16[3,256,768]{2,1,0:T(8,128)(2,1)S(1)} %get-tuple-element.25) | copy-start | bytes 3538948
  92.8 1.7 %copy-start.4 = (bf16[3,256,768]{2,1,0:T(8,128)(2,1)S(1)}, bf16[3,256,768]{2,1,0:T(8,128)(2,1)}, u32[]{:S(2)}) copy-start(bf16[3,256,768]{2,1,0:T(8,128)(2,1)} %copy-done.3) | copy-start | bytes 3538948
  94.5 0.7 copy-start.9
  109.4 13.6 %copy-start.10 = (bf16[1,8,768]{2,1,0:T(8,128)(2,1)S(1)}, bf16[1,8,768]{2,1,0:T(8,128)(2,1)}, u32[]{:S(2)}) copy-start(bf16[1,8,768]{2,1,0:T(8,128)(2,1)} %param.16) | copy-start | bytes 36868
  109.4 13.9 %copy-start.12 = (f32[1,768]{1,0:T(1,128)S(1)}, f32[1,768]{1,0:T(1,128)}, u32[]{:S(2)}) copy-start(f32[1,768]{1,0:T(1,128)} %param.18) | copy-start | bytes 9220
  109.4 14.0 %copy-start.13 = (f32[1,768]{1,0:T(1,128)S(1)}, f32[1,768]{1,0:T(1,128)}, u32[]{:S(2)}) copy-start(f32[1,768]{1,0:T(1,128)} %param.19) | copy-start | bytes 9220
  109.4 56.3 %all-to-all-start.4 = ((bf16[128,8,768]{2,1,0:T(8,128)(2,1)}), bf16[128,8,768]{2,1,0:T(8,128)(2,1)S(1)}, u32[]{:S(2)}, u32[]{:S(2)}) async-start(bf16[128,8,768]{2,1,0:T(8,128)(2,1)} %copy.21), calls=%async_computation.4 | async-start | bytes 3145728 | tf_op jit(solution)/shard_map/all_to_all | solution.py:103
  123.1 43.0 %copy-start.11 = (f32[1,8,768]{2,1,0:T(8,128)S(1)}, f32[1,8,768]{2,1,0:T(8,128)}, u32[]{:S(2)}) copy-start(f32[1,8,768]{2,1,0:T(8,128)} %param.17) | copy-start | bytes 73732

commit v3 on v0

--- a/solution.py
+++ b/solution.py
@@ -5,6 +5,7 @@
 from jax.sharding import PartitionSpec as P
 
 SUB = ("sub_0", "sub_1", "sub_2")
+PLANE = ("sub_0", "sub_1")
 
 
 def copy_for_each(x, axis):
@@ -63,14 +64,24 @@
         ),
         lambda: empty,
     ).astype(jnp.bfloat16)
-    selector = (owners[:, 0][:, None] == jnp.arange(nown, dtype=jnp.int32)[None, :]).astype(
-        jnp.bfloat16
+    nplane = lax.axis_size(PLANE)
+    core = lax.axis_index("sub_2")
+    near = (lax.axis_index(SUB) + nown // 2) % nown
+    third = owners[2, 0]
+    other = lax.ppermute(owners[2:3, 0], "sub_2", [(0, 1), (1, 0)])[0]
+    plane = copy_for_each(displacement[0], PLANE)
+    lent = lax.ppermute(
+        lax.dynamic_index_in_dim(plane, other // 2, 0, keepdims=False), "sub_2", [(0, 1), (1, 0)]
     )
-    group = whole_of(displacement, (("sub_0", "sub_1"), "sub_2"), 0)
-    picked = jnp.einsum("so,ohn->shn", selector, group, preferred_element_type=jnp.float32).astype(
-        jnp.bfloat16
+    here = lax.dynamic_index_in_dim(plane, third // 2, 0, keepdims=False)
+    picked = jnp.stack(
+        [
+            lax.dynamic_index_in_dim(plane, near // 2, 0, keepdims=False),
+            jnp.where(third % 2 == core, here, lent),
+        ]
     )
-    own_disp = collect(picked, "harm", 1)
+    own_pair = collect(picked, "harm", 1)
+    own_disp = jnp.stack([own_pair[0], own_pair[0], own_pair[1]])
     inner = -jnp.einsum("sfn,shn->shf", modes, own_disp, preferred_element_type=jnp.float32)
     interior = jnp.where(live_rows[:, None, :], inner, jnp.float32(0.0)).astype(jnp.bfloat16)
     disp_cols = lax.dynamic_slice_in_dim(own_disp, harm_idx * width_q, width_q, 2)
@@ -79,13 +90,18 @@
         "shj,sjn->shn", disp_cols, stiffness, preferred_element_type=jnp.float32
     )
     partial_rows = sent_and_summed(contrib.astype(jnp.bfloat16), "harm", 1)
-    routing = (jnp.arange(nown, dtype=jnp.int32)[:, None] == owners[:, 0][None, :]).astype(
-        jnp.float32
+    near_part = partial_rows[0] + partial_rows[1]
+    third_part = partial_rows[2]
+    other_part = lax.ppermute(third_part, "sub_2", [(0, 1), (1, 0)])
+    slots = jnp.arange(nplane, dtype=jnp.int32)[:, None, None]
+    dense = (
+        jnp.where(slots == near // 2, near_part, jnp.float32(0.0))
+        + jnp.where((slots == third // 2) & (third % 2 == core), third_part, jnp.float32(0.0))
+        + jnp.where((slots == other // 2) & (other % 2 == core), other_part, jnp.float32(0.0))
     )
-    dense = jnp.einsum("os,shn->ohn", routing, partial_rows, precision=lax.Precision.HIGHEST)
     arrived = lax.all_to_all(
-        dense.astype(jnp.bfloat16), SUB, split_axis=0, concat_axis=0, tiled=True
-    ).astype(dense.dtype)
+        dense.astype(jnp.bfloat16), PLANE, split_axis=0, concat_axis=0, tiled=True
+    ).astype(jnp.float32)
     gathered = jnp.sum(arrived, axis=0, keepdims=True)
     rows_q = displacement.shape[1]
     pairs_all = rows_q * nharm // 2

time: 160 us -> 142 us (0.89)
  blocking collectives: 54.6 us -> 0 us
  starting transfers between devices: 18.6 us -> 43.6 us
  waiting for transfers between devices: 49.6 us -> 61.4 us
  between operations: 14.9 us -> 20.1 us
  local copies, waits for them, and re-layouts: 7.73 us -> 4.37 us
  matrix products: 8.64 us -> 5.34 us
    all_to_all x3 -> x0, blocking collectives: 54.6 us -> none  [the longest x2 45.4 us: copy_for_each(): lax.all_to_all(jnp.broadcast_to(x[None], (length, *x.shape)), axis, 0, 0,...]
    all_to_all x1 -> x2, waiting for transfers between devices: 6.74 us -> 23.4 us  [copy_for_each(): lax.all_to_all(jnp.broadcast_to(x[None], (length, *x.shape)), axis, 0, 0,...]
    all_to_all x1 -> x2, starting transfers between devices: 4.31 us -> 20.9 us  [copy_for_each(): lax.all_to_all(jnp.broadcast_to(x[None], (length, *x.shape)), axis, 0, 0,...]
    all_to_all x1 -> x2, waiting for transfers between devices: 42.3 us -> 30 us  [the longest x1 23.9 us: body(): lax.all_to_all(dense.astype(jnp.bfloat16), PLANE, split_axis=0, concat_ax...]
    ppermute x0 -> x3, starting transfers between devices: none -> 5.74 us  [the longest x1 1.92 us: body(): other_part = lax.ppermute(third_part, 'sub_2', [(0, 1), (1, 0)])]
    all_gather x1, waiting for transfers between devices: 0.55 us -> 5.55 us  [body(): piece = lax.all_gather(masked, 'harm', axis=1, tiled=True)]
    dot_general x2 -> x0, matrix products: 3.29 us -> none  [the longest x1 1.78 us: body(): jnp.einsum('so,ohn->shn', selector, group, preferred_element_type=jnp.flo...]
    all_to_all x1 -> x2, starting transfers between devices: 14.3 us -> 16.9 us  [the longest x1 13.4 us: body(): lax.all_to_all(dense.astype(jnp.bfloat16), PLANE, split_axis=0, concat_ax...]
  transfers between devices with their start and end apart: 3 -> 8, of which waited for: 3 -> 7; matrix products, arithmetic and copies ran while one was open for 4% -> 2% of each run, Pallas kernels for 0% -> 0%
where the time goes in v3:
time: 142 us; the launch traced here: 141 us
  waiting for transfers between devices  61.4 us (43%)
  starting transfers between devices  43.6 us (31%)
  between operations  20.1 us (14%)
  other arithmetic  6.15 us (4%)
  matrix products  5.34 us (4%)
  local copies, waits for them, and re-layouts  4.37 us (3%)
    all_to_all x1, waiting for transfers between devices, body(): lax.all_to_all(dense.astype(jnp.bfloat16), PLANE, split_axis=0, concat_ax...  23.9 us
    all_to_all x2, waiting for transfers between devices, copy_for_each(): lax.all_to_all(jnp.broadcast_to(x[None], (length, *x.shape)), axis, 0, 0,...  23.4 us
    all_to_all x2, starting transfers between devices, copy_for_each(): lax.all_to_all(jnp.broadcast_to(x[None], (length, *x.shape)), axis, 0, 0,...  20.9 us
    all_to_all x1, starting transfers between devices, body(): lax.all_to_all(dense.astype(jnp.bfloat16), PLANE, split_axis=0, concat_ax...  13.4 us
    all_to_all x1, waiting for transfers between devices, sent_and_summed(): lax.all_to_all(tiles, axis, split_axis=0, concat_axis=0, tiled=True)  6.06 us
    all_gather x1, waiting for transfers between devices, body(): piece = lax.all_gather(masked, 'harm', axis=1, tiled=True)  5.55 us
    dot_general x1, matrix products, body(): jnp.einsum('sfg,sgn->sfn', front_inverse, piece, preferred_element_type=j...  4.2 us
    all_to_all x1, starting transfers between devices, sent_and_summed(): lax.all_to_all(tiles, axis, split_axis=0, concat_axis=0, tiled=True)  3.54 us
  transfers between devices with their start and end apart: 8, of which 7 were waited for; matrix products, arithmetic and copies ran while one was open for 2% of the time, Pallas kernels for 0%

profile of v3, /device:TPU:8, one launch (start us, length us, event | category | flops | bytes accessed | tf_op | source)
XLA Modules:
  0.0 141.0 jit_solution(3794493898096391368)
XLA Ops:
  7.2 0.0 all-gather.2.cloned.1.call-start
  7.2 0.8 broadcast_compare_fusion
  8.0 2.5 %broadcast_select_fusion = bf16[3,256,768]{2,1,0:T(8,128)(2,1)} fusion(bf16[3,256,768]{2,1,0:T(8,128)(2,1)} %param.14, pred[3,256]{1,0:T(4,128)(4,1)S(1)} %broadcast_compare_fusion), kind=kLoop, calls=%fused_computation.3 | loop fusion | flops 589824 | bytes 2360064 | tf_op jit(solution)/shard_map/jit(_where)/select_n | solution.py:56
  10.6 0.9 broadcast_in_dim.87
  11.5 16.6 %all-to-all-start = ((bf16[64,8,768]{2,1,0:T(8,128)(2,1)}), bf16[64,8,768]{2,1,0:T(8,128)(2,1)S(1)}, u32[]{:S(2)}, u32[]{:S(2)}) async-start(bf16[64,8,768]{2,1,0:T(8,128)(2,1)} %broadcast_in_dim.87), calls=%async_computation | async-start | bytes 1572864 | tf_op jit(solution)/shard_map/all_to_all | solution.py:13
  28.1 0.6 slice.26
  28.7 1.9 %collective-permute-start = (s32[1]{0:T(128)}, s32[1]{0:T(128)}, u32[]{:S(2)}, u32[]{:S(2)}) collective-permute-start(s32[1]{0:T(128)} %bitcast.3), channel_id=1, source_target_pairs={{0,4},{4,0},{1,5},{5,1},{2,6},{6,2},{3,7},{7,3},{8,12},{12,8},{9,1... | collective-permute-start | bytes 20 | tf_op jit(solution)/shard_map/ppermute | solution.py:71
  30.7 1.3 collective-permute-done
  34.5 17.6 %all-to-all-done = bf16[64,8,768]{2,1,0:T(8,128)(2,1)S(1)} async-done(((bf16[64,8,768]{2,1,0:T(8,128)(2,1)}), bf16[64,8,768]{2,1,0:T(8,128)(2,1)S(1)}, u32[]{:S(2)}, u32[]{:S(2)}) %all-to-all-start) | async-done | bytes 786464 | tf_op jit(solution)/shard_map/all_to_all | solution.py:13
  52.1 1.9 %collective-permute-start.1 = (bf16[8,768]{1,0:T(8,128)(2,1)S(1)}, bf16[8,768]{1,0:T(8,128)(2,1)S(1)}, u32[]{:S(2)}, u32[]{:S(2)}) collective-permute-start(bf16[8,768]{1,0:T(8,128)(2,1)S(1)} %get-tuple-element.16), channel_id=1, source_target_pairs={{0,4},{4,0},{1,5},{5,1},{2,6},{6,2},{3,7},{7,3},{8,12},{12,8},{9,1... | collective-permute-start | bytes 36872 | tf_op jit(solution)/shard_map/ppermute | solution.py:73
  56.7 0.6 broadcast_in_dim.88
  57.3 4.3 %all-to-all-start.1 = ((bf16[4,2,8,768]{3,2,1,0:T(8,128)(2,1)}), bf16[4,2,8,768]{3,2,1,0:T(8,128)(2,1)S(1)}, u32[]{:S(2)}, u32[]{:S(2)}) async-start(bf16[4,2,8,768]{3,2,1,0:T(8,128)(2,1)} %broadcast_in_dim.88), calls=%async_computation.1 | async-start | bytes 196608 | tf_op jit(solution)/shard_map/all_to_all | solution.py:13
  61.6 0.6 reduce_max.9
  62.9 5.8 %all-to-all-done.1 = bf16[4,2,8,768]{3,2,1,0:T(8,128)(2,1)S(1)} async-done(((bf16[4,2,8,768]{3,2,1,0:T(8,128)(2,1)}), bf16[4,2,8,768]{3,2,1,0:T(8,128)(2,1)S(1)}, u32[]{:S(2)}, u32[]{:S(2)}) %all-to-all-start.1) | async-done | bytes 98336 | tf_op jit(solution)/shard_map/all_to_all | solution.py:13
  68.7 5.6 %all-gather.2.cloned.1.call-done = bf16[3,1024,768]{2,1,0:T(8,128)(2,1)} async-done(((bf16[3,256,768]{2,1,0:T(8,128)(2,1)}), bf16[3,1024,768]{2,1,0:T(8,128)(2,1)}) %all-gather.2.cloned.1.call-update) | async-done | bytes 4718608 | tf_op jit(solution)/shard_map/all_gather | solution.py:59
  74.3 4.2 %conditional.1 = (bf16[3,256,768]{2,1,0:T(8,128)(2,1)S(1)}) conditional(s32[]{:T(128)} %convert_element_type.44, () %tuple.16, (bf16[3,256,1024]{2,1,0:T(8,128)(2,1)}, bf16[3,1024,768]{2,1,0:T(8,128)(2,1)}) %tuple.17), branch_computations={%region_1.2_spmd, %region_2.3_spmd} | conditional | flops 1208549376 | bytes 7471112 | solution.py:60
  74.3 4.2 %convolution_convert_fusion = bf16[3,256,768]{2,1,0:T(8,128)(2,1)S(1)} fusion(bf16[3,256,1024]{2,1,0:T(8,128)(2,1)} %get-tuple-element.14, bf16[3,1024,768]{2,1,0:T(8,128)(2,1)} %get-tuple-element.9), kind=kOutput, calls=%fused_computation | convolution fusion | flops 1208549376 | bytes 7471104 | tf_op jit(solution)/shard_map/cond/branch_1_fun/sfg,sgn->sfn/dot_general | solution.py:62
  78.5 0.5 fusion.3
  79.0 1.2 copy-done.1
  80.2 0.3 fusion.15
  80.5 0.4 fusion.1
  80.9 0.7 copy.16
  81.6 3.5 %all-to-all-start.2 = ((bf16[4,3,8,768]{3,2,1,0:T(8,128)(2,1)}), bf16[4,3,8,768]{3,2,1,0:T(8,128)(2,1)S(1)}, u32[]{:S(2)}, u32[]{:S(2)}) async-start(bf16[4,3,8,768]{3,2,1,0:T(8,128)(2,1)} %bitcast.37), calls=%async_computation.2 | async-start | bytes 294912 | tf_op jit(solution)/shard_map/all_to_all | solution.py:41
  85.1 6.1 %all-to-all-done.2 = bf16[4,3,8,768]{3,2,1,0:T(8,128)(2,1)S(1)} async-done(((bf16[4,3,8,768]{3,2,1,0:T(8,128)(2,1)}), bf16[4,3,8,768]{3,2,1,0:T(8,128)(2,1)S(1)}, u32[]{:S(2)}, u32[]{:S(2)}) %all-to-all-start.2) | async-done | bytes 147488 | tf_op jit(solution)/shard_map/all_to_all | solution.py:41
  91.2 1.9 %collective-permute-start.2 = (f32[8,768]{1,0:T(8,128)S(1)}, f32[8,768]{1,0:T(8,128)S(1)}, u32[]{:S(2)}, u32[]{:S(2)}) collective-permute-start(f32[8,768]{1,0:T(8,128)S(1)} %get-tuple-element.20), channel_id=1, source_target_pairs={{0,4},{4,0},{1,5},{5,1},{2,6},{6,2},{3,7},{7,3},{8,12},{12,8},{9,1... | collective-permute-start | bytes 73736 | tf_op jit(solution)/shard_map/ppermute | solution.py:95
  93.2 1.1 collective-permute-done.2
  94.3 1.3 add_convert_fusion
  95.6 13.4 %all-to-all-start.3 = ((bf16[64,8,768]{2,1,0:T(8,128)(2,1)}), bf16[64,8,768]{2,1,0:T(8,128)(2,1)S(1)}, u32[]{:S(2)}, u32[]{:S(2)}) async-start(bf16[64,8,768]{2,1,0:T(8,128)(2,1)} %add_convert_fusion), calls=%async_computation.3 | async-start | bytes 1572864 | tf_op jit(solution)/shard_map/all_to_all | solution.py:102
  109.0 0.2 rev.3
  109.3 23.9 %all-to-all-done.3 = bf16[64,8,768]{2,1,0:T(8,128)(2,1)S(1)} async-done(((bf16[64,8,768]{2,1,0:T(8,128)(2,1)}), bf16[64,8,768]{2,1,0:T(8,128)(2,1)S(1)}, u32[]{:S(2)}, u32[]{:S(2)}) %all-to-all-start.3) | async-done | bytes 786464 | tf_op jit(solution)/shard_map/all_to_all | solution.py:102
  133.3 0.1 convert_reduce_fusion
  133.4 0.7 fusion.7
  (36 shorter events, 0.2 us)
Async XLA Ops:
  7.2 73.4 %copy-start = (bf16[3,192,768]{2,1,0:T(8,128)(2,1)S(1)}, bf16[3,192,768]{2,1,0:T(8,128)(2,1)}, u32[]{:S(2)}) copy-start(bf16[3,192,768]{2,1,0:T(8,128)(2,1)} %param.15) | copy-start | bytes 2654212
  7.2 67.1 %all-gather.2.cloned.1.call-start = ((), (), s32[]{:S(2)}) async-start(), calls=%async_computation.4 | async-start | bytes 5898240 | tf_op jit(solution)/shard_map/all_gather | solution.py:59
  8.0 2.5 %copy-start.4 = (bf16[1,8,768]{2,1,0:T(8,128)(2,1)S(1)}, bf16[1,8,768]{2,1,0:T(8,128)(2,1)}, u32[]{:S(2)}) copy-start(bf16[1,8,768]{2,1,0:T(8,128)(2,1)} %param.16) | copy-start | bytes 36868
  10.5 17.6 %copy-start.9 = (s32[3,1]{0,1:T(1,128)S(1)}, s32[3,1]{0,1:T(1,128)}, u32[]{:S(2)}) copy-start(s32[3,1]{0,1:T(1,128)} %param.12) | copy-start | bytes 40
  10.6 51.0 %copy-start.8 = (s32[3]{0:T(128)S(1)}, s32[3]{0:T(128)}, u32[]{:S(2)}) copy-start(s32[3]{0:T(128)} %param.11) | copy-start | bytes 40
  11.5 40.6 %all-to-all-start = ((bf16[64,8,768]{2,1,0:T(8,128)(2,1)}), bf16[64,8,768]{2,1,0:T(8,128)(2,1)S(1)}, u32[]{:S(2)}, u32[]{:S(2)}) async-start(bf16[64,8,768]{2,1,0:T(8,128)(2,1)} %broadcast_in_dim.87), calls=%async_computation | async-start | bytes 1572864 | tf_op jit(solution)/shard_map/all_to_all | solution.py:13
  28.7 3.3 %collective-permute-start = (s32[1]{0:T(128)}, s32[1]{0:T(128)}, u32[]{:S(2)}, u32[]{:S(2)}) collective-permute-start(s32[1]{0:T(128)} %bitcast.3), channel_id=1, source_target_pairs={{0,4},{4,0},{1,5},{5,1},{2,6},{6,2},{3,7},{7,3},{8,12},{12,8},{9,1... | collective-permute-start | bytes 20 | tf_op jit(solution)/shard_map/ppermute | solution.py:71
  52.1 4.5 %collective-permute-start.1 = (bf16[8,768]{1,0:T(8,128)(2,1)S(1)}, bf16[8,768]{1,0:T(8,128)(2,1)S(1)}, u32[]{:S(2)}, u32[]{:S(2)}) collective-permute-start(bf16[8,768]{1,0:T(8,128)(2,1)S(1)} %get-tuple-element.16), channel_id=1, source_target_pairs={{0,4},{4,0},{1,5},{5,1},{2,6},{6,2},{3,7},{7,3},{8,12},{12,8},{9,1... | collective-permute-start | bytes 36872 | tf_op jit(solution)/shard_map/ppermute | solution.py:73
  57.3 11.4 %all-to-all-start.1 = ((bf16[4,2,8,768]{3,2,1,0:T(8,128)(2,1)}), bf16[4,2,8,768]{3,2,1,0:T(8,128)(2,1)S(1)}, u32[]{:S(2)}, u32[]{:S(2)}) async-start(bf16[4,2,8,768]{3,2,1,0:T(8,128)(2,1)} %broadcast_in_dim.88), calls=%async_computation.1 | async-start | bytes 196608 | tf_op jit(solution)/shard_map/all_to_all | solution.py:13
  78.5 2.4 %copy-start.2 = (bf16[3,256,768]{2,1,0:T(8,128)(2,1)}, bf16[3,256,768]{2,1,0:T(8,128)(2,1)S(1)}, u32[]{:S(2)}) copy-start(bf16[3,256,768]{2,1,0:T(8,128)(2,1)S(1)} %get-tuple-element.25) | copy-start | bytes 3538948
  78.5 1.7 %copy-start.1 = (bf16[3,256,768]{2,1,0:T(8,128)(2,1)S(1)}, bf16[3,256,768]{2,1,0:T(8,128)(2,1)}, u32[]{:S(2)}) copy-start(bf16[3,256,768]{2,1,0:T(8,128)(2,1)} %broadcast_select_fusion) | copy-start | bytes 3538948
  80.2 1.4 copy-start.3
  81.6 27.7 %copy-start.6 = (f32[1,768]{1,0:T(1,128)S(1)}, f32[1,768]{1,0:T(1,128)}, u32[]{:S(2)}) copy-start(f32[1,768]{1,0:T(1,128)} %param.19) | copy-start | bytes 9220
  81.6 27.7 %copy-start.7 = (f32[1,768]{1,0:T(1,128)S(1)}, f32[1,768]{1,0:T(1,128)}, u32[]{:S(2)}) copy-start(f32[1,768]{1,0:T(1,128)} %param.18) | copy-start | bytes 9220
  81.6 9.6 %all-to-all-start.2 = ((bf16[4,3,8,768]{3,2,1,0:T(8,128)(2,1)}), bf16[4,3,8,768]{3,2,1,0:T(8,128)(2,1)S(1)}, u32[]{:S(2)}, u32[]{:S(2)}) async-start(bf16[4,3,8,768]{3,2,1,0:T(8,128)(2,1)} %bitcast.37), calls=%async_computation.2 | async-start | bytes 294912 | tf_op jit(solution)/shard_map/all_to_all | solution.py:41
  91.2 3.1 %collective-permute-start.2 = (f32[8,768]{1,0:T(8,128)S(1)}, f32[8,768]{1,0:T(8,128)S(1)}, u32[]{:S(2)}, u32[]{:S(2)}) collective-permute-start(f32[8,768]{1,0:T(8,128)S(1)} %get-tuple-element.20), channel_id=1, source_target_pairs={{0,4},{4,0},{1,5},{5,1},{2,6},{6,2},{3,7},{7,3},{8,12},{12,8},{9,1... | collective-permute-start | bytes 73736 | tf_op jit(solution)/shard_map/ppermute | solution.py:95
  94.3 39.1 %copy-start.5 = (f32[1,8,768]{2,1,0:T(8,128)S(1)}, f32[1,8,768]{2,1,0:T(8,128)}, u32[]{:S(2)}) copy-start(f32[1,8,768]{2,1,0:T(8,128)} %param.17) | copy-start | bytes 73732
  95.6 37.7 %all-to-all-start.3 = ((bf16[64,8,768]{2,1,0:T(8,128)(2,1)}), bf16[64,8,768]{2,1,0:T(8,128)(2,1)S(1)}, u32[]{:S(2)}, u32[]{:S(2)}) async-start(bf16[64,8,768]{2,1,0:T(8,128)(2,1)} %add_convert_fusion), calls=%async_computation.3 | async-start | bytes 1572864 | tf_op jit(solution)/shard_map/all_to_all | solution.py:102
Sparse Core Ops, SparseCore 0:
  10.7 63.5 all-gather.1

commit v4 on v3

--- a/solution.py
+++ b/solution.py
@@ -6,6 +6,7 @@
 
 SUB = ("sub_0", "sub_1", "sub_2")
 PLANE = ("sub_0", "sub_1")
+PAIR = ("sub_2", "harm")
 
 
 def copy_for_each(x, axis):
@@ -56,7 +57,9 @@
     masked = jnp.where(live_rows[:, :, None], coupling, jnp.zeros_like(coupling))
     longest = jnp.max(lengths)
     empty = jnp.zeros((masked.shape[0], front_q, width), jnp.float32)
-    piece = lax.all_gather(masked, "harm", axis=1, tiled=True)
+    whole_live = jnp.arange(nharm * front_q, dtype=jnp.int32)[None, :] < lengths[:, None]
+    piece = lax.all_gather(coupling, "harm", axis=1, tiled=True)
+    piece = jnp.where(whole_live[:, :, None], piece, jnp.zeros_like(piece))
     modes = lax.cond(
         jnp.int32(0) < longest,
         lambda: jnp.einsum(
@@ -65,22 +68,38 @@
         lambda: empty,
     ).astype(jnp.bfloat16)
     nplane = lax.axis_size(PLANE)
+    rows_q = displacement.shape[1]
     core = lax.axis_index("sub_2")
     near = (lax.axis_index(SUB) + nown // 2) % nown
     third = owners[2, 0]
     other = lax.ppermute(owners[2:3, 0], "sub_2", [(0, 1), (1, 0)])[0]
     plane = copy_for_each(displacement[0], PLANE)
-    lent = lax.ppermute(
-        lax.dynamic_index_in_dim(plane, other // 2, 0, keepdims=False), "sub_2", [(0, 1), (1, 0)]
-    )
-    here = lax.dynamic_index_in_dim(plane, third // 2, 0, keepdims=False)
-    picked = jnp.stack(
-        [
-            lax.dynamic_index_in_dim(plane, near // 2, 0, keepdims=False),
-            jnp.where(third % 2 == core, here, lent),
-        ]
-    )
-    own_pair = collect(picked, "harm", 1)
+    zero_block = jnp.zeros_like(plane[0])
+    lend = []
+    for peer_core in range(2):
+        wanted = jnp.where(peer_core == core, third, other)
+        lend.append(
+            jnp.stack(
+                [
+                    jnp.where(
+                        peer_core == core,
+                        lax.dynamic_index_in_dim(plane, near // 2, 0, keepdims=False),
+                        zero_block,
+                    ),
+                    jnp.where(
+                        wanted % 2 == core,
+                        lax.dynamic_index_in_dim(plane, wanted // 2, 0, keepdims=False),
+                        zero_block,
+                    ),
+                ]
+            )
+        )
+    lend = jnp.broadcast_to(jnp.stack(lend)[:, None], (2, nharm, 2, *zero_block.shape))
+    lent = lax.all_to_all(
+        lend.reshape(2 * nharm, 2, *zero_block.shape), PAIR, 0, 0, tiled=True
+    ).reshape(2, nharm, 2, *zero_block.shape)
+    lent = (lent[0] + lent[1]).transpose(1, 0, 2, 3)
+    own_pair = lent.reshape(2, nharm * zero_block.shape[0], width)
     own_disp = jnp.stack([own_pair[0], own_pair[0], own_pair[1]])
     inner = -jnp.einsum("sfn,shn->shf", modes, own_disp, preferred_element_type=jnp.float32)
     interior = jnp.where(live_rows[:, None, :], inner, jnp.float32(0.0)).astype(jnp.bfloat16)
@@ -89,10 +108,30 @@
     contrib = contrib + jnp.einsum(
         "shj,sjn->shn", disp_cols, stiffness, preferred_element_type=jnp.float32
     )
-    partial_rows = sent_and_summed(contrib.astype(jnp.bfloat16), "harm", 1)
-    near_part = partial_rows[0] + partial_rows[1]
-    third_part = partial_rows[2]
-    other_part = lax.ppermute(third_part, "sub_2", [(0, 1), (1, 0)])
+    near_c = (contrib[0] + contrib[1]).reshape(nharm, rows_q, width)
+    third_c = contrib[2].reshape(nharm, rows_q, width)
+    zero_rows = jnp.zeros_like(near_c)
+    send = jnp.stack(
+        [
+            jnp.stack(
+                [
+                    jnp.where(peer_core == core, near_c, zero_rows),
+                    jnp.where(third % 2 == peer_core, third_c, zero_rows),
+                ],
+                axis=1,
+            )
+            for peer_core in range(2)
+        ]
+    )
+    came = lax.all_to_all(
+        send.reshape(2 * nharm, 2, rows_q, width).astype(jnp.bfloat16), PAIR, 0, 0, tiled=True
+    ).astype(jnp.float32)
+    came = came.reshape(2, nharm, 2, rows_q, width).sum(axis=1)
+    mine = jnp.where(core == 0, came[0], came[1])
+    theirs = jnp.where(core == 0, came[1], came[0])
+    near_part = mine[0]
+    third_part = mine[1]
+    other_part = theirs[1]
     slots = jnp.arange(nplane, dtype=jnp.int32)[:, None, None]
     dense = (
         jnp.where(slots == near // 2, near_part, jnp.float32(0.0))

time: 142 us -> 144 us (1.014)
  starting transfers between devices: 43.6 us -> 40.2 us
  between operations: 20.1 us -> 22.8 us
  other arithmetic: 6.15 us -> 3.81 us
  local copies, waits for them, and re-layouts: 4.37 us -> 6.55 us
  matrix products: 5.34 us -> 7.12 us
    all_gather x1, waiting for transfers between devices: 5.55 us -> 14.3 us  [body(): piece = lax.all_gather(coupling, 'harm', axis=1, tiled=True)]
    all_to_all x2 -> x1, waiting for transfers between devices: 23.4 us -> 14.9 us  [copy_for_each(): lax.all_to_all(jnp.broadcast_to(x[None], (length, *x.shape)), axis, 0, 0,...]
    all_to_all x1 -> x2, waiting for transfers between devices: 6.06 us -> 11 us  [the longest x1 7.21 us: body(): lax.all_to_all(lend.reshape(2 * nharm, 2, *zero_block.shape), PAIR, 0, 0,...]
    all_to_all x2 -> x1, starting transfers between devices: 20.9 us -> 16.6 us  [copy_for_each(): lax.all_to_all(jnp.broadcast_to(x[None], (length, *x.shape)), axis, 0, 0,...]
    all_to_all x1 -> x2, starting transfers between devices: 3.54 us -> 7.72 us  [the longest x1 4.3 us: body(): lax.all_to_all(lend.reshape(2 * nharm, 2, *zero_block.shape), PAIR, 0, 0,...]
    ppermute x2 -> x0, starting transfers between devices: 3.83 us -> none  [the longest x1 1.92 us: body(): other_part = lax.ppermute(third_part, 'sub_2', [(0, 1), (1, 0)])]
    unnamed x20, local copies, waits for them, and re-layouts: 1.26 us -> 4.03 us
    select_n x1 -> x4, other arithmetic: 2.49 us -> 0.05 us  [the longest x1 0.02 us: body(): jnp.where(peer_core == core, near_c, zero_rows)]
  transfers between devices with their start and end apart: 8 -> 6, of which waited for: 7 -> 5; matrix products, arithmetic and copies ran while one was open for 2% -> 4% of each run, Pallas kernels for 0% -> 0%
where the time goes in v4:
time: 144 us; the launch traced here: 143 us
  waiting for transfers between devices  62.4 us (43%)
  starting transfers between devices  40.2 us (28%)
  between operations  22.8 us (16%)
  matrix products  7.12 us (5%)
  local copies, waits for them, and re-layouts  6.55 us (5%)
  other arithmetic  3.81 us (3%)
    all_to_all x1, waiting for transfers between devices, body(): lax.all_to_all(dense.astype(jnp.bfloat16), PLANE, split_axis=0, concat_ax...  22.3 us
    all_to_all x1, starting transfers between devices, copy_for_each(): lax.all_to_all(jnp.broadcast_to(x[None], (length, *x.shape)), axis, 0, 0,...  16.6 us
    all_to_all x1, waiting for transfers between devices, copy_for_each(): lax.all_to_all(jnp.broadcast_to(x[None], (length, *x.shape)), axis, 0, 0,...  14.9 us
    all_gather x1, waiting for transfers between devices, body(): piece = lax.all_gather(coupling, 'harm', axis=1, tiled=True)  14.3 us
    all_to_all x1, starting transfers between devices, body(): lax.all_to_all(dense.astype(jnp.bfloat16), PLANE, split_axis=0, concat_ax...  13.9 us
    all_to_all x1, waiting for transfers between devices, body(): lax.all_to_all(lend.reshape(2 * nharm, 2, *zero_block.shape), PAIR, 0, 0,...  7.21 us
    dot_general x1, matrix products, body(): jnp.einsum('sfg,sgn->sfn', front_inverse, piece, preferred_element_type=j...  4.33 us
    all_to_all x1, starting transfers between devices, body(): lax.all_to_all(lend.reshape(2 * nharm, 2, *zero_block.shape), PAIR, 0, 0,...  4.3 us
  transfers between devices with their start and end apart: 6, of which 5 were waited for; matrix products, arithmetic and copies ran while one was open for 4% of the time, Pallas kernels for 0%

profile of v4, /device:TPU:8, one launch (start us, length us, event | category | flops | bytes accessed | tf_op | source)
XLA Modules:
  0.0 142.9 jit_solution(18116162360787616010)
XLA Ops:
  7.2 0.0 copy-start
  7.2 0.0 all-gather.2.cloned.1.call-start
  7.2 2.4 %copy.32 = bf16[3,256,768]{1,2,0:T(8,128)(2,1)} copy(bf16[3,256,768]{2,1,0:T(8,128)(2,1)} %param.14) | data formatting | bytes 2359296 | tf_op args[3]
  9.7 0.0 all-gather.2.cloned.1.call-update
  9.7 1.0 broadcast_in_dim.107
  10.7 16.6 %all-to-all-start = ((bf16[64,8,768]{2,1,0:T(8,128)(2,1)}), bf16[64,8,768]{2,1,0:T(8,128)(2,1)S(1)}, u32[]{:S(2)}, u32[]{:S(2)}) async-start(bf16[64,8,768]{2,1,0:T(8,128)(2,1)} %broadcast_in_dim.107), calls=%async_computation | async-start | bytes 1572864 | tf_op jit(solution)/shard_map/all_to_all | solution.py:14
  27.3 0.6 slice.54
  27.9 1.9 %collective-permute-start = (s32[1]{0:T(128)}, s32[1]{0:T(128)}, u32[]{:S(2)}, u32[]{:S(2)}) collective-permute-start(s32[1]{0:T(128)} %bitcast.3), channel_id=1, source_target_pairs={{0,4},{4,0},{1,5},{5,1},{2,6},{6,2},{3,7},{7,3},{8,12},{12,8},{9,1... | collective-permute-start | bytes 20 | tf_op jit(solution)/shard_map/ppermute | solution.py:75
  32.5 0.6 reduce_max.9
  36.4 14.9 %all-to-all-done = bf16[64,8,768]{2,1,0:T(8,128)(2,1)S(1)} async-done(((bf16[64,8,768]{2,1,0:T(8,128)(2,1)}), bf16[64,8,768]{2,1,0:T(8,128)(2,1)S(1)}, u32[]{:S(2)}, u32[]{:S(2)}) %all-to-all-start) | async-done | bytes 786464 | tf_op jit(solution)/shard_map/all_to_all | solution.py:14
  51.3 0.7 broadcast_in_dim.109
  52.0 4.3 %all-to-all-start.1 = ((bf16[8,2,8,768]{3,2,1,0:T(8,128)(2,1)}), bf16[8,2,8,768]{3,2,1,0:T(8,128)(2,1)S(1)}, u32[]{:S(2)}, u32[]{:S(2)}) async-start(bf16[8,2,8,768]{3,2,1,0:T(8,128)(2,1)} %bitcast.7), calls=%async_computation.1 | async-start | bytes 393216 | tf_op jit(solution)/shard_map/all_to_all | solution.py:98
  56.3 0.1 broadcast_compare_fusion.1
  56.4 7.2 %all-to-all-done.1 = bf16[8,2,8,768]{3,2,1,0:T(8,128)(2,1)S(1)} async-done(((bf16[8,2,8,768]{3,2,1,0:T(8,128)(2,1)}), bf16[8,2,8,768]{3,2,1,0:T(8,128)(2,1)S(1)}, u32[]{:S(2)}, u32[]{:S(2)}) %all-to-all-start.1) | async-done | bytes 196640 | tf_op jit(solution)/shard_map/all_to_all | solution.py:98
  63.6 1.1 fusion.24
  64.7 14.3 %all-gather.2.cloned.1.call-done = bf16[3,1024,768]{1,2,0:T(8,128)(2,1)} async-done(((bf16[3,256,768]{1,2,0:T(8,128)(2,1)}), bf16[3,1024,768]{1,2,0:T(8,128)(2,1)}) %all-gather.2.cloned.1.call-update) | async-done | bytes 4718608 | tf_op jit(solution)/shard_map/all_gather | solution.py:61
  79.0 4.4 %conditional.1 = (bf16[3,256,768]{1,2,0:T(8,128)(2,1)S(1)}) conditional(s32[]{:T(128)} %convert_element_type.43, () %tuple.16, (bf16[3,256,1024]{2,1,0:T(8,128)(2,1)}, s32[3,1024]{1,0:T(4,128)S(1)}, bf16[3,1024,768]{1,2,0:T(8,128)(2,1)}, bf16[]{:T(256)}, s32[3]{0:T(128)S(1)}) %tuple.39), branch_computations={%region_1.2_spmd, %region_2.3_spmd} | conditional | flops 1210911744 | bytes 7489558 | solution.py:63
  79.0 0.1 broadcast_compare_fusion
  79.1 4.3 %fusion.7 = bf16[3,256,768]{1,2,0:T(8,128)(2,1)S(1)} fusion(bf16[3,256,1024]{2,1,0:T(8,128)(2,1)} %get-tuple-element.17, bf16[3,1024,768]{1,2,0:T(8,128)(2,1)} %get-tuple-element.15, pred[3,1024]{1,0:T(4,128)(4,1)S(1)} %broadcast_compare_fusion, bf16[]{:T(256)} %get-tuple-element.19), kind=kOutput, calls=%fused_computation.5 | convolution fusion | flops 1210908672 | bytes 7474178 | tf_op jit(solution)/shard_map/cond/branch_1_fun/sfg,sgn->sfn/dot_general | solution.py:65
  83.4 0.3 fusion.17
  83.8 1.4 fusion.13
  85.2 0.7 pad_maximum_fusion
  85.9 3.4 %all-to-all-start.2 = ((bf16[8,2,8,768]{3,2,1,0:T(8,128)(2,1)}), bf16[8,2,8,768]{3,2,1,0:T(8,128)(2,1)S(1)}, u32[]{:S(2)}, u32[]{:S(2)}) async-start(bf16[8,2,8,768]{3,2,1,0:T(8,128)(2,1)} %bitcast.21), calls=%async_computation.2 | async-start | bytes 393216 | tf_op jit(solution)/shard_map/all_to_all | solution.py:126
  91.9 3.8 %all-to-all-done.2 = bf16[8,2,8,768]{3,2,1,0:T(8,128)(2,1)S(1)} async-done(((bf16[8,2,8,768]{3,2,1,0:T(8,128)(2,1)}), bf16[8,2,8,768]{3,2,1,0:T(8,128)(2,1)S(1)}, u32[]{:S(2)}, u32[]{:S(2)}) %all-to-all-start.2) | async-done | bytes 196640 | tf_op jit(solution)/shard_map/all_to_all | solution.py:126
  95.7 0.0 copy-start.5
  95.7 1.3 add_convert_fusion
  97.0 13.9 %all-to-all-start.3 = ((bf16[64,8,768]{2,1,0:T(8,128)(2,1)}), bf16[64,8,768]{2,1,0:T(8,128)(2,1)S(1)}, u32[]{:S(2)}, u32[]{:S(2)}) async-start(bf16[64,8,768]{2,1,0:T(8,128)(2,1)} %add_convert_fusion), calls=%async_computation.3 | async-start | bytes 1572864 | tf_op jit(solution)/shard_map/all_to_all | solution.py:141
  111.0 0.2 rev.3
  111.4 1.5 %copy.38 = bf16[3,256,768]{2,1,0:T(8,128)(2,1)} copy(bf16[3,256,768]{1,2,0:T(8,128)(2,1)S(1)} %get-tuple-element.56) | data formatting | bytes 2359296
  112.9 22.3 %all-to-all-done.3 = bf16[64,8,768]{2,1,0:T(8,128)(2,1)S(1)} async-done(((bf16[64,8,768]{2,1,0:T(8,128)(2,1)}), bf16[64,8,768]{2,1,0:T(8,128)(2,1)S(1)}, u32[]{:S(2)}, u32[]{:S(2)}) %all-to-all-start.3) | async-done | bytes 786464 | tf_op jit(solution)/shard_map/all_to_all | solution.py:141
  135.2 0.1 convert_reduce_fusion
  135.4 0.7 fusion.28
  (40 shorter events, 0.3 us)
Async XLA Ops:
  7.2 56.5 %copy-start = (bf16[3,192,768]{2,1,0:T(8,128)(2,1)S(1)}, bf16[3,192,768]{2,1,0:T(8,128)(2,1)}, u32[]{:S(2)}) copy-start(bf16[3,192,768]{2,1,0:T(8,128)(2,1)} %param.15) | copy-start | bytes 2654212
  7.2 2.5 %copy-start.2 = (bf16[1,8,768]{2,1,0:T(8,128)(2,1)S(1)}, bf16[1,8,768]{2,1,0:T(8,128)(2,1)}, u32[]{:S(2)}) copy-start(bf16[1,8,768]{2,1,0:T(8,128)(2,1)} %param.16) | copy-start | bytes 36868
  7.2 71.8 %all-gather.2.cloned.1.call-start = ((), (), s32[]{:S(2)}) async-start(), calls=%async_computation.4 | async-start | bytes 5898240 | tf_op jit(solution)/shard_map/all_gather | solution.py:61
  9.7 17.6 %copy-start.8 = (s32[3,1]{0,1:T(1,128)S(1)}, s32[3,1]{0,1:T(1,128)}, u32[]{:S(2)}) copy-start(s32[3,1]{0,1:T(1,128)} %param.12) | copy-start | bytes 40
  9.7 22.8 %copy-start.7 = (s32[3]{0:T(128)S(1)}, s32[3]{0:T(128)}, u32[]{:S(2)}) copy-start(s32[3]{0:T(128)} %param.11) | copy-start | bytes 40
  10.7 40.6 %all-to-all-start = ((bf16[64,8,768]{2,1,0:T(8,128)(2,1)}), bf16[64,8,768]{2,1,0:T(8,128)(2,1)S(1)}, u32[]{:S(2)}, u32[]{:S(2)}) async-start(bf16[64,8,768]{2,1,0:T(8,128)(2,1)} %broadcast_in_dim.107), calls=%async_computation | async-start | bytes 1572864 | tf_op jit(solution)/shard_map/all_to_all | solution.py:14
  27.9 5.9 %collective-permute-start = (s32[1]{0:T(128)}, s32[1]{0:T(128)}, u32[]{:S(2)}, u32[]{:S(2)}) collective-permute-start(s32[1]{0:T(128)} %bitcast.3), channel_id=1, source_target_pairs={{0,4},{4,0},{1,5},{5,1},{2,6},{6,2},{3,7},{7,3},{8,12},{12,8},{9,1... | collective-permute-start | bytes 20 | tf_op jit(solution)/shard_map/ppermute | solution.py:75
  52.0 11.6 %all-to-all-start.1 = ((bf16[8,2,8,768]{3,2,1,0:T(8,128)(2,1)}), bf16[8,2,8,768]{3,2,1,0:T(8,128)(2,1)S(1)}, u32[]{:S(2)}, u32[]{:S(2)}) async-start(bf16[8,2,8,768]{3,2,1,0:T(8,128)(2,1)} %bitcast.7), calls=%async_computation.1 | async-start | bytes 393216 | tf_op jit(solution)/shard_map/all_to_all | solution.py:98
  79.0 4.7 %copy-start.1 = (bf16[3,256,768]{2,1,0:T(8,128)(2,1)S(1)}, bf16[3,256,768]{2,1,0:T(8,128)(2,1)}, u32[]{:S(2)}) copy-start(bf16[3,256,768]{2,1,0:T(8,128)(2,1)} %param.14) | copy-start | bytes 3538948
  83.7 2.2 %copy-start.3 = (bf16[3,32,256]{2,1,0:T(8,128)(2,1)}, bf16[3,32,256]{2,1,0:T(8,128)(2,1)S(1)}, u32[]{:S(2)}) copy-start(bf16[3,32,256]{2,1,0:T(8,128)(2,1)S(1)} %fusion.17) | copy-start | bytes 147460
  85.9 9.7 %all-to-all-start.2 = ((bf16[8,2,8,768]{3,2,1,0:T(8,128)(2,1)}), bf16[8,2,8,768]{3,2,1,0:T(8,128)(2,1)S(1)}, u32[]{:S(2)}, u32[]{:S(2)}) async-start(bf16[8,2,8,768]{3,2,1,0:T(8,128)(2,1)} %bitcast.21), calls=%async_computation.2 | async-start | bytes 393216 | tf_op jit(solution)/shard_map/all_to_all | solution.py:126
  95.7 15.6 %copy-start.5 = (f32[1,768]{1,0:T(1,128)S(1)}, f32[1,768]{1,0:T(1,128)}, u32[]{:S(2)}) copy-start(f32[1,768]{1,0:T(1,128)} %param.19) | copy-start | bytes 9220
  95.7 15.6 %copy-start.6 = (f32[1,768]{1,0:T(1,128)S(1)}, f32[1,768]{1,0:T(1,128)}, u32[]{:S(2)}) copy-start(f32[1,768]{1,0:T(1,128)} %param.18) | copy-start | bytes 9220
  97.0 38.2 %all-to-all-start.3 = ((bf16[64,8,768]{2,1,0:T(8,128)(2,1)}), bf16[64,8,768]{2,1,0:T(8,128)(2,1)S(1)}, u32[]{:S(2)}, u32[]{:S(2)}) async-start(bf16[64,8,768]{2,1,0:T(8,128)(2,1)} %add_convert_fusion), calls=%async_computation.3 | async-start | bytes 1572864 | tf_op jit(solution)/shard_map/all_to_all | solution.py:141
  111.3 24.0 %copy-start.4 = (f32[1,8,768]{2,1,0:T(8,128)S(1)}, f32[1,8,768]{2,1,0:T(8,128)}, u32[]{:S(2)}) copy-start(f32[1,8,768]{2,1,0:T(8,128)} %param.17) | copy-start | bytes 73732
Sparse Core Ops, SparseCore 0:
  10.7 68.2 all-gather.1

commit v5 on v4

--- a/solution.py
+++ b/solution.py
@@ -55,17 +55,11 @@
     own_rows = harm_idx * front_q + jnp.arange(front_q, dtype=jnp.int32)
     live_rows = own_rows[None, :] < lengths[:, None]
     masked = jnp.where(live_rows[:, :, None], coupling, jnp.zeros_like(coupling))
-    longest = jnp.max(lengths)
-    empty = jnp.zeros((masked.shape[0], front_q, width), jnp.float32)
     whole_live = jnp.arange(nharm * front_q, dtype=jnp.int32)[None, :] < lengths[:, None]
     piece = lax.all_gather(coupling, "harm", axis=1, tiled=True)
     piece = jnp.where(whole_live[:, :, None], piece, jnp.zeros_like(piece))
-    modes = lax.cond(
-        jnp.int32(0) < longest,
-        lambda: jnp.einsum(
-            "sfg,sgn->sfn", front_inverse, piece, preferred_element_type=jnp.float32
-        ),
-        lambda: empty,
+    modes = jnp.einsum(
+        "sfg,sgn->sfn", front_inverse, piece, preferred_element_type=jnp.float32
     ).astype(jnp.bfloat16)
     nplane = lax.axis_size(PLANE)
     rows_q = displacement.shape[1]
@@ -101,7 +95,15 @@
     lent = (lent[0] + lent[1]).transpose(1, 0, 2, 3)
     own_pair = lent.reshape(2, nharm * zero_block.shape[0], width)
     own_disp = jnp.stack([own_pair[0], own_pair[0], own_pair[1]])
-    inner = -jnp.einsum("sfn,shn->shf", modes, own_disp, preferred_element_type=jnp.float32)
+    partial_y = jnp.einsum("shn,sfn->shf", own_disp, masked, preferred_element_type=jnp.float32)
+    whole_y = collect(partial_y, "harm", 2)
+    inner = -jnp.einsum(
+        "shg,sfg->shf",
+        whole_y,
+        front_inverse.astype(jnp.float32),
+        precision=lax.Precision.HIGHEST,
+        preferred_element_type=jnp.float32,
+    )
     interior = jnp.where(live_rows[:, None, :], inner, jnp.float32(0.0)).astype(jnp.bfloat16)
     disp_cols = lax.dynamic_slice_in_dim(own_disp, harm_idx * width_q, width_q, 2)
     contrib = jnp.einsum("shf,sfn->shn", interior, masked, preferred_element_type=jnp.float32)

time: 144 us -> 142 us (0.986)
  the two profiles are of different devices: /device:TPU:8 before, /device:TPU:2 now
where the time goes in v5:
time: 142 us
  waiting for transfers between devices  64 us (45%)
  starting transfers between devices  39.2 us (28%)
  between operations  22.2 us (16%)
  matrix products  7.46 us (5%)
  local copies, waits for them, and re-layouts  5.73 us (4%)
  other arithmetic  3.15 us (2%)
    all_to_all x2, waiting for transfers between devices, copy_for_each(): lax.all_to_all(jnp.broadcast_to(x[None], (length, *x.shape)), axis, 0, 0,...  26.3 us
    all_to_all x1, waiting for transfers between devices, body(): lax.all_to_all(dense.astype(jnp.bfloat16), PLANE, split_axis=0, concat_ax...  24.1 us
    all_to_all x2, starting transfers between devices, copy_for_each(): lax.all_to_all(jnp.broadcast_to(x[None], (length, *x.shape)), axis, 0, 0,...  21.1 us
    all_to_all x1, waiting for transfers between devices, body(): lax.all_to_all(lend.reshape(2 * nharm, 2, *zero_block.shape), PAIR, 0, 0,...  7.2 us
    all_to_all x1, starting transfers between devices, body(): lax.all_to_all(dense.astype(jnp.bfloat16), PLANE, split_axis=0, concat_ax...  6.56 us
    all_to_all x1, starting transfers between devices, body(): lax.all_to_all(lend.reshape(2 * nharm, 2, *zero_block.shape), PAIR, 0, 0,...  4.83 us
    all_to_all x1, starting transfers between devices, body(): lax.all_to_all(send.reshape(2 * nharm, 2, rows_q, width).astype(jnp.bfloa...  4.75 us
    dot_general x1, matrix products, body(): jnp.einsum('sfg,sgn->sfn', front_inverse, piece, preferred_element_type=j...  4.71 us
  transfers between devices with their start and end apart: 7, of which 6 were waited for; matrix products, arithmetic and copies ran while one was open for 6% of the time, Pallas kernels for 0%

profile of v5, /device:TPU:2, one launch (start us, length us, event | category | flops | bytes accessed | tf_op | source)
XLA Modules:
  0.0 141.7 jit_solution(9232746578327348745)
XLA Ops:
  7.2 0.0 copy-start
  7.2 1.8 %broadcast_in_dim.110 = bf16[64,8,768]{2,1,0:T(8,128)(2,1)} broadcast(bf16[8,768]{1,0:T(8,128)(2,1)} %bitcast.63), dimensions={1,2} | broadcast | bytes 798720 | tf_op jit(solution)/shard_map/broadcast_in_dim | solution.py:14
  8.9 16.7 %all-to-all-start = ((bf16[64,8,768]{2,1,0:T(8,128)(2,1)}), bf16[64,8,768]{2,1,0:T(8,128)(2,1)S(1)}, u32[]{:S(2)}, u32[]{:S(2)}) async-start(bf16[64,8,768]{2,1,0:T(8,128)(2,1)} %broadcast_in_dim.110), calls=%async_computation | async-start | bytes 1572864 | tf_op jit(solution)/shard_map/all_to_all | solution.py:14
  25.7 0.0 all-gather.2.cloned.1.call-start
  25.7 0.7 all-gather.2.cloned.1.call-update
  26.4 0.6 slice.54
  27.0 1.9 %collective-permute-start = (s32[1]{0:T(128)}, s32[1]{0:T(128)}, u32[]{:S(2)}, u32[]{:S(2)}) collective-permute-start(s32[1]{0:T(128)} %bitcast.2), channel_id=1, source_target_pairs={{0,4},{4,0},{1,5},{5,1},{2,6},{6,2},{3,7},{7,3},{8,12},{12,8},{9,1... | collective-permute-start | bytes 20 | tf_op jit(solution)/shard_map/ppermute | solution.py:69
  29.0 1.1 collective-permute-done
  32.7 17.1 %all-to-all-done = bf16[64,8,768]{2,1,0:T(8,128)(2,1)S(1)} async-done(((bf16[64,8,768]{2,1,0:T(8,128)(2,1)}), bf16[64,8,768]{2,1,0:T(8,128)(2,1)S(1)}, u32[]{:S(2)}, u32[]{:S(2)}) %all-to-all-start) | async-done | bytes 786464 | tf_op jit(solution)/shard_map/all_to_all | solution.py:14
  49.9 0.7 broadcast_in_dim.112
  50.6 4.8 %all-to-all-start.1 = ((bf16[8,2,8,768]{3,2,1,0:T(8,128)(2,1)}), bf16[8,2,8,768]{3,2,1,0:T(8,128)(2,1)S(1)}, u32[]{:S(2)}, u32[]{:S(2)}) async-start(bf16[8,2,8,768]{3,2,1,0:T(8,128)(2,1)} %bitcast.6), calls=%async_computation.1 | async-start | bytes 393216 | tf_op jit(solution)/shard_map/all_to_all | solution.py:92
  55.4 0.1 broadcast_compare_fusion
  55.5 7.2 %all-to-all-done.1 = bf16[8,2,8,768]{3,2,1,0:T(8,128)(2,1)S(1)} async-done(((bf16[8,2,8,768]{3,2,1,0:T(8,128)(2,1)}), bf16[8,2,8,768]{3,2,1,0:T(8,128)(2,1)S(1)}, u32[]{:S(2)}, u32[]{:S(2)}) %all-to-all-start.1) | async-done | bytes 196640 | tf_op jit(solution)/shard_map/all_to_all | solution.py:92
  62.8 0.6 fusion.13
  63.3 0.8 broadcast_in_dim.115
  64.1 4.4 %all-to-all-start.2 = ((f32[4,3,32,256]{3,2,1,0:T(8,128)}), f32[4,3,32,256]{3,2,1,0:T(8,128)S(1)}, u32[]{:S(2)}, u32[]{:S(2)}) async-start(f32[4,3,32,256]{3,2,1,0:T(8,128)} %broadcast_in_dim.115), calls=%async_computation.2 | async-start | bytes 786432 | tf_op jit(solution)/shard_map/all_to_all | solution.py:14
  71.2 9.2 %all-to-all-done.2 = f32[4,3,32,256]{3,2,1,0:T(8,128)S(1)} async-done(((f32[4,3,32,256]{3,2,1,0:T(8,128)}), f32[4,3,32,256]{3,2,1,0:T(8,128)S(1)}, u32[]{:S(2)}, u32[]{:S(2)}) %all-to-all-start.2) | async-done | bytes 393248 | tf_op jit(solution)/shard_map/all_to_all | solution.py:14
  80.4 1.4 %fusion.11 = bf16[3,32,256]{2,1,0:T(8,128)(2,1)S(1)} fusion(f32[3,32,1024]{2,1,0:T(8,128)S(1)} %bitcast.62, bf16[3,256,1024]{2,1,0:T(8,128)(2,1)S(1)} %copy-done, pred[3,256]{1,0:T(4,128)(4,1)S(1)} %broadcast_compare_fusion), kind=kOutput, calls=%fused_computation.12 | convolution fusion | flops 302063616 | bytes 2016000 | tf_op jit(solution)/shard_map/shg,sfg->shf/dot_general | solution.py:100
  81.9 0.4 fusion.12
  82.3 0.4 convolution_add_fusion
  82.7 0.7 pad_maximum_fusion
  83.4 4.7 %all-to-all-start.3 = ((bf16[8,2,8,768]{3,2,1,0:T(8,128)(2,1)}), bf16[8,2,8,768]{3,2,1,0:T(8,128)(2,1)S(1)}, u32[]{:S(2)}, u32[]{:S(2)}) async-start(bf16[8,2,8,768]{3,2,1,0:T(8,128)(2,1)} %bitcast.21), calls=%async_computation.3 | async-start | bytes 393216 | tf_op jit(solution)/shard_map/all_to_all | solution.py:128
  90.8 4.5 %all-to-all-done.3 = bf16[8,2,8,768]{3,2,1,0:T(8,128)(2,1)S(1)} async-done(((bf16[8,2,8,768]{3,2,1,0:T(8,128)(2,1)}), bf16[8,2,8,768]{3,2,1,0:T(8,128)(2,1)S(1)}, u32[]{:S(2)}, u32[]{:S(2)}) %all-to-all-start.3) | async-done | bytes 196640 | tf_op jit(solution)/shard_map/all_to_all | solution.py:128
  95.4 1.3 add_convert_fusion
  96.6 6.6 %all-to-all-start.4 = ((bf16[64,8,768]{2,1,0:T(8,128)(2,1)}), bf16[64,8,768]{2,1,0:T(8,128)(2,1)S(1)}, u32[]{:S(2)}, u32[]{:S(2)}) async-start(bf16[64,8,768]{2,1,0:T(8,128)(2,1)} %add_convert_fusion), calls=%async_computation.4 | async-start | bytes 1572864 | tf_op jit(solution)/shard_map/all_to_all | solution.py:143
  103.3 0.2 rev.3
  103.6 0.1 iota_compare_fusion
  103.6 24.1 %all-to-all-done.4 = bf16[64,8,768]{2,1,0:T(8,128)(2,1)S(1)} async-done(((bf16[64,8,768]{2,1,0:T(8,128)(2,1)}), bf16[64,8,768]{2,1,0:T(8,128)(2,1)S(1)}, u32[]{:S(2)}, u32[]{:S(2)}) %all-to-all-start.4) | async-done | bytes 786464 | tf_op jit(solution)/shard_map/all_to_all | solution.py:143
  127.8 0.1 convert_reduce_fusion
  127.9 0.7 fusion.24
  128.6 4.7 %fusion.7 = bf16[3,256,768]{1,2,0:T(8,128)(2,1)S(1)} fusion(bf16[3,256,1024]{2,1,0:T(8,128)(2,1)S(1)} %copy-done, bf16[3,1024,768]{2,1,0:T(8,128)(2,1)} %all-gather.2.cloned.1.call-done, pred[3,1024]{1,0:T(4,128)(4,1)S(1)} %iota_compare_fusion), kind=kOutput, calls=%fused_computation.7 | convolution fusion | flops 1210908672 | bytes 7474176 | tf_op jit(solution)/shard_map/sfg,sgn->sfn/dot_general | solution.py:61
  133.4 1.5 %copy.35 = bf16[3,256,768]{2,1,0:T(8,128)(2,1)} copy(bf16[3,256,768]{1,2,0:T(8,128)(2,1)S(1)} %fusion.7) | data formatting | bytes 2359296
  (43 shorter events, 0.4 us)
Async XLA Ops:
  7.2 73.2 %copy-start = (bf16[3,256,1024]{2,1,0:T(8,128)(2,1)S(1)}, bf16[3,256,1024]{2,1,0:T(8,128)(2,1)}, u32[]{:S(2)}) copy-start(bf16[3,256,1024]{2,1,0:T(8,128)(2,1)} %param.11) | copy-start | bytes 4718596
  8.9 17.5 %copy-start.9 = (s32[3,1]{0,1:T(1,128)S(1)}, s32[3,1]{0,1:T(1,128)}, u32[]{:S(2)}) copy-start(s32[3,1]{0,1:T(1,128)} %param.10) | copy-start | bytes 40
  8.9 46.5 %copy-start.8 = (s32[3]{0:T(128)S(1)}, s32[3]{0:T(128)}, u32[]{:S(2)}) copy-start(s32[3]{0:T(128)} %param.9) | copy-start | bytes 40
  8.9 40.9 %all-to-all-start = ((bf16[64,8,768]{2,1,0:T(8,128)(2,1)}), bf16[64,8,768]{2,1,0:T(8,128)(2,1)S(1)}, u32[]{:S(2)}, u32[]{:S(2)}) async-start(bf16[64,8,768]{2,1,0:T(8,128)(2,1)} %broadcast_in_dim.110), calls=%async_computation | async-start | bytes 1572864 | tf_op jit(solution)/shard_map/all_to_all | solution.py:14
  25.7 37.1 %copy-start.1 = (bf16[3,256,768]{2,1,0:T(8,128)(2,1)S(1)}, bf16[3,256,768]{2,1,0:T(8,128)(2,1)}, u32[]{:S(2)}) copy-start(bf16[3,256,768]{2,1,0:T(8,128)(2,1)} %param.12) | copy-start | bytes 3538948
  25.7 103.0 %all-gather.2.cloned.1.call-start = ((), (), s32[]{:S(2)}) async-start(), calls=%async_computation.5 | async-start | bytes 5898240 | tf_op jit(solution)/shard_map/all_gather | solution.py:59
  27.0 3.1 %collective-permute-start = (s32[1]{0:T(128)}, s32[1]{0:T(128)}, u32[]{:S(2)}, u32[]{:S(2)}) collective-permute-start(s32[1]{0:T(128)} %bitcast.2), channel_id=1, source_target_pairs={{0,4},{4,0},{1,5},{5,1},{2,6},{6,2},{3,7},{7,3},{8,12},{12,8},{9,1... | collective-permute-start | bytes 20 | tf_op jit(solution)/shard_map/ppermute | solution.py:69
  50.6 12.1 %all-to-all-start.1 = ((bf16[8,2,8,768]{3,2,1,0:T(8,128)(2,1)}), bf16[8,2,8,768]{3,2,1,0:T(8,128)(2,1)S(1)}, u32[]{:S(2)}, u32[]{:S(2)}) async-start(bf16[8,2,8,768]{3,2,1,0:T(8,128)(2,1)} %bitcast.6), calls=%async_computation.1 | async-start | bytes 393216 | tf_op jit(solution)/shard_map/all_to_all | solution.py:92
  64.1 16.3 %all-to-all-start.2 = ((f32[4,3,32,256]{3,2,1,0:T(8,128)}), f32[4,3,32,256]{3,2,1,0:T(8,128)S(1)}, u32[]{:S(2)}, u32[]{:S(2)}) async-start(f32[4,3,32,256]{3,2,1,0:T(8,128)} %broadcast_in_dim.115), calls=%async_computation.2 | async-start | bytes 786432 | tf_op jit(solution)/shard_map/all_to_all | solution.py:14
  80.4 1.9 %copy-start.2 = (bf16[3,192,768]{2,1,0:T(8,128)(2,1)S(1)}, bf16[3,192,768]{2,1,0:T(8,128)(2,1)}, u32[]{:S(2)}) copy-start(bf16[3,192,768]{2,1,0:T(8,128)(2,1)} %param.13) | copy-start | bytes 2654212
  81.9 0.8 copy-start.4
  83.4 11.8 %all-to-all-start.3 = ((bf16[8,2,8,768]{3,2,1,0:T(8,128)(2,1)}), bf16[8,2,8,768]{3,2,1,0:T(8,128)(2,1)S(1)}, u32[]{:S(2)}, u32[]{:S(2)}) async-start(bf16[8,2,8,768]{3,2,1,0:T(8,128)(2,1)} %bitcast.21), calls=%async_computation.3 | async-start | bytes 393216 | tf_op jit(solution)/shard_map/all_to_all | solution.py:128
  90.7 12.5 %copy-start.3 = (bf16[1,8,768]{2,1,0:T(8,128)(2,1)S(1)}, bf16[1,8,768]{2,1,0:T(8,128)(2,1)}, u32[]{:S(2)}) copy-start(bf16[1,8,768]{2,1,0:T(8,128)(2,1)} %param.14) | copy-start | bytes 36868
  90.8 12.5 %copy-start.6 = (f32[1,768]{1,0:T(1,128)S(1)}, f32[1,768]{1,0:T(1,128)}, u32[]{:S(2)}) copy-start(f32[1,768]{1,0:T(1,128)} %param.16) | copy-start | bytes 9220
  90.8 12.5 %copy-start.7 = (f32[1,768]{1,0:T(1,128)S(1)}, f32[1,768]{1,0:T(1,128)}, u32[]{:S(2)}) copy-start(f32[1,768]{1,0:T(1,128)} %param.17) | copy-start | bytes 9220
  95.3 32.6 %copy-start.5 = (f32[1,8,768]{2,1,0:T(8,128)S(1)}, f32[1,8,768]{2,1,0:T(8,128)}, u32[]{:S(2)}) copy-start(f32[1,8,768]{2,1,0:T(8,128)} %param.15) | copy-start | bytes 73732
  96.6 31.2 %all-to-all-start.4 = ((bf16[64,8,768]{2,1,0:T(8,128)(2,1)}), bf16[64,8,768]{2,1,0:T(8,128)(2,1)S(1)}, u32[]{:S(2)}, u32[]{:S(2)}) async-start(bf16[64,8,768]{2,1,0:T(8,128)(2,1)} %add_convert_fusion), calls=%async_computation.4 | async-start | bytes 1572864 | tf_op jit(solution)/shard_map/all_to_all | solution.py:143
Sparse Core Ops, SparseCore 0:
  28.6 65.6 all-gather.1

commit v6 on v5

--- a/solution.py
+++ b/solution.py
@@ -41,6 +41,23 @@
     tiles = in_blocks(x, dim, lax.axis_size(axis))
     arrived = lax.all_to_all(tiles, axis, split_axis=0, concat_axis=0, tiled=True)
     return arrived.astype(jnp.float32).sum(axis=0)
+
+
+def shifted(x, axis, step):
+    n = lax.axis_size(axis)
+    return lax.ppermute(x, axis, [(j, (j + step) % n) for j in range(n)])
+
+
+def ring_whole(x, idx, n):
+    from_left = shifted(x, "harm", 1)
+    from_right = shifted(x, "harm", -1)
+    half = x.shape[1] // 2
+    far = jnp.concatenate(
+        [shifted(from_left[:, :half], "harm", 1), shifted(from_right[:, half:], "harm", -1)], axis=1
+    )
+    blocks = jnp.stack([x, from_right, far, from_left])
+    order = (jnp.arange(n, dtype=jnp.int32) - idx) % n
+    return jnp.concatenate([blocks[order[j]] for j in range(n)], axis=1)
 
 
 def body(
@@ -55,12 +72,6 @@
     own_rows = harm_idx * front_q + jnp.arange(front_q, dtype=jnp.int32)
     live_rows = own_rows[None, :] < lengths[:, None]
     masked = jnp.where(live_rows[:, :, None], coupling, jnp.zeros_like(coupling))
-    whole_live = jnp.arange(nharm * front_q, dtype=jnp.int32)[None, :] < lengths[:, None]
-    piece = lax.all_gather(coupling, "harm", axis=1, tiled=True)
-    piece = jnp.where(whole_live[:, :, None], piece, jnp.zeros_like(piece))
-    modes = jnp.einsum(
-        "sfg,sgn->sfn", front_inverse, piece, preferred_element_type=jnp.float32
-    ).astype(jnp.bfloat16)
     nplane = lax.axis_size(PLANE)
     rows_q = displacement.shape[1]
     core = lax.axis_index("sub_2")
@@ -69,6 +80,11 @@
     other = lax.ppermute(owners[2:3, 0], "sub_2", [(0, 1), (1, 0)])[0]
     plane = copy_for_each(displacement[0], PLANE)
     zero_block = jnp.zeros_like(plane[0])
+    anchor = plane[0, 0, 0] * jnp.zeros((), plane.dtype)
+    piece = ring_whole(masked + anchor, harm_idx, nharm)
+    modes = jnp.einsum(
+        "sfg,sgn->sfn", front_inverse, piece, preferred_element_type=jnp.float32
+    ).astype(jnp.bfloat16)
     lend = []
     for peer_core in range(2):
         wanted = jnp.where(peer_core == core, third, other)

time: 142 us -> 151 us (1.063)
  the two profiles are of different devices: /device:TPU:2 before, /device:TPU:8 now
where the time goes in v6:
time: 151 us; the launch traced here: 150 us
  starting transfers between devices  56.1 us (37%)
  waiting for transfers between devices  28.8 us (19%)
  local copies, waits for them, and re-layouts  27.8 us (18%)
  between operations  17.4 us (12%)
  other arithmetic  13.1 us (9%)
  matrix products  6.5 us (4%)
    all_to_all x2, starting transfers between devices, copy_for_each(): lax.all_to_all(jnp.broadcast_to(x[None], (length, *x.shape)), axis, 0, 0,...  20 us
    all_to_all x1, waiting for transfers between devices, body(): lax.all_to_all(send.reshape(2 * nharm, 2, rows_q, width).astype(jnp.bfloa...  19.5 us
    ppermute x4, starting transfers between devices, shifted(): return lax.ppermute(x, axis, [(j, (j + step) % n) for j in range(n)])  12.8 us
    all_to_all x1, starting transfers between devices, body(): lax.all_to_all(dense.astype(jnp.bfloat16), PLANE, split_axis=0, concat_ax...  12.7 us
    dynamic_slice x5, local copies, waits for them, and re-layouts, ring_whole(): return jnp.concatenate([blocks[order[j]] for j in range(n)], axis=1)  10.5 us
    all_to_all x1, waiting for transfers between devices, body(): lax.all_to_all(lend.reshape(2 * nharm, 2, *zero_block.shape), PAIR, 0, 0,...  4.46 us
    all_to_all x1, starting transfers between devices, body(): lax.all_to_all(lend.reshape(2 * nharm, 2, *zero_block.shape), PAIR, 0, 0,...  4.4 us
    all_to_all x1, starting transfers between devices, body(): lax.all_to_all(send.reshape(2 * nharm, 2, rows_q, width).astype(jnp.bfloa...  4.17 us
  transfers between devices with their start and end apart: 10, of which 5 were waited for; matrix products, arithmetic and copies ran while one was open for 27% of the time, Pallas kernels for 0%

profile of v6, /device:TPU:8, one launch (start us, length us, event | category | flops | bytes accessed | tf_op | source)
XLA Modules:
  0.0 149.7 jit_solution(5329906026604166970)
XLA Ops:
  0.7 1.8 %broadcast_in_dim.96 = bf16[64,8,768]{2,1,0:T(8,128)(2,1)} broadcast(bf16[8,768]{1,0:T(8,128)(2,1)} %bitcast.83), dimensions={1,2} | broadcast | bytes 798720 | tf_op jit(solution)/shard_map/broadcast_in_dim | solution.py:14
  2.4 16.6 %all-to-all-start = ((bf16[64,8,768]{2,1,0:T(8,128)(2,1)}), bf16[64,8,768]{2,1,0:T(8,128)(2,1)S(1)}, u32[]{:S(2)}, u32[]{:S(2)}) async-start(bf16[64,8,768]{2,1,0:T(8,128)(2,1)} %broadcast_in_dim.96), calls=%async_computation | async-start | bytes 1572864 | tf_op jit(solution)/shard_map/all_to_all | solution.py:14
  19.0 1.4 slice.75
  20.4 1.9 %collective-permute-start = (s32[1]{0:T(128)}, s32[1]{0:T(128)}, u32[]{:S(2)}, u32[]{:S(2)}) collective-permute-start(s32[1]{0:T(128)} %bitcast.2), channel_id=1, source_target_pairs={{0,4},{4,0},{1,5},{5,1},{2,6},{6,2},{3,7},{7,3},{8,12},{12,8},{9,1... | collective-permute-start | bytes 20 | tf_op jit(solution)/shard_map/ppermute | solution.py:80
  32.0 1.3 reduce.1
  33.3 3.3 %rev.3 = f32[1,4,2,768]{3,2,1,0:T(2,128)} reverse(f32[1,4,2,768]{3,2,1,0:T(2,128)} %reshape.351), dimensions={2} | reverse | bytes 49152 | tf_op jit(solution)/shard_map/rev | solution.py:171
  36.6 1.4 reshape.352
  45.1 4.4 %all-to-all-start.1 = ((bf16[8,2,8,768]{3,2,1,0:T(8,128)(2,1)}), bf16[8,2,8,768]{3,2,1,0:T(8,128)(2,1)}, u32[]{:S(2)}, u32[]{:S(2)}) async-start(bf16[8,2,8,768]{3,2,1,0:T(8,128)(2,1)} %bitcast.82), calls=%async_computation.1 | async-start | bytes 393216 | tf_op jit(solution)/shard_map/all_to_all | solution.py:108
  51.4 4.5 %all-to-all-done.1 = bf16[8,2,8,768]{3,2,1,0:T(8,128)(2,1)} async-done(((bf16[8,2,8,768]{3,2,1,0:T(8,128)(2,1)}), bf16[8,2,8,768]{3,2,1,0:T(8,128)(2,1)}, u32[]{:S(2)}, u32[]{:S(2)}) %all-to-all-start.1) | async-done | bytes 196640 | tf_op jit(solution)/shard_map/all_to_all | solution.py:108
  58.2 3.5 %all-to-all-start.2 = ((f32[4,3,32,256]{3,2,1,0:T(8,128)}), f32[4,3,32,256]{3,2,1,0:T(8,128)S(1)}, u32[]{:S(2)}, u32[]{:S(2)}) async-start(f32[4,3,32,256]{3,2,1,0:T(8,128)} %broadcast_in_dim.101), calls=%async_computation.2 | async-start | bytes 786432 | tf_op jit(solution)/shard_map/all_to_all | solution.py:14
  62.9 5.1 %collective-permute-start.1 = (bf16[3,256,768]{2,1,0:T(8,128)(2,1)}, bf16[3,256,768]{2,1,0:T(8,128)(2,1)}, u32[]{:S(2)}, u32[]{:S(2)}) collective-permute-start(bf16[3,256,768]{2,1,0:T(8,128)(2,1)} %fusion.16), channel_id=1, source_target_pairs={{0,3},{1,0},{2,1},{3,2},{4,7},{5,4},{6,5},{7,6},{8,11},{9,8},{10,9... | collective-permute-start | bytes 3538952 | tf_op jit(solution)/shard_map/ppermute | solution.py:48
  68.0 1.9 %collective-permute-start.2 = (bf16[3,256,768]{2,1,0:T(8,128)(2,1)}, bf16[3,256,768]{2,1,0:T(8,128)(2,1)}, u32[]{:S(2)}, u32[]{:S(2)}) collective-permute-start(bf16[3,256,768]{2,1,0:T(8,128)(2,1)} %fusion.16), channel_id=1, source_target_pairs={{0,1},{1,2},{2,3},{3,0},{4,5},{5,6},{6,7},{7,4},{8,9},{9,10},{10,1... | collective-permute-start | bytes 3538952 | tf_op jit(solution)/shard_map/ppermute | solution.py:48
  70.3 1.4 fusion.15
  74.1 4.2 %all-to-all-start.3 = ((bf16[8,2,8,768]{3,2,1,0:T(8,128)(2,1)}), bf16[8,2,8,768]{3,2,1,0:T(8,128)(2,1)S(1)}, u32[]{:S(2)}, u32[]{:S(2)}) async-start(bf16[8,2,8,768]{3,2,1,0:T(8,128)(2,1)} %bitcast.21), calls=%async_computation.3 | async-start | bytes 393216 | tf_op jit(solution)/shard_map/all_to_all | solution.py:144
  81.1 19.5 %all-to-all-done.3 = bf16[8,2,8,768]{3,2,1,0:T(8,128)(2,1)S(1)} async-done(((bf16[8,2,8,768]{3,2,1,0:T(8,128)(2,1)}), bf16[8,2,8,768]{3,2,1,0:T(8,128)(2,1)S(1)}, u32[]{:S(2)}, u32[]{:S(2)}) %all-to-all-start.3) | async-done | bytes 196640 | tf_op jit(solution)/shard_map/all_to_all | solution.py:144
  100.6 1.9 %slice.112 = bf16[3,128,768]{2,1,0:T(8,128)(2,1)} slice(bf16[3,256,768]{2,1,0:T(8,128)(2,1)} %collective-permute-done.1), slice={[0:3], [128:256], [0:768]} | slice | bytes 1179648 | tf_op jit(solution)/shard_map/slice | solution.py:56
  102.6 1.9 %collective-permute-start.4 = (bf16[3,128,768]{2,1,0:T(8,128)(2,1)}, bf16[3,128,768]{2,1,0:T(8,128)(2,1)}, u32[]{:S(2)}, u32[]{:S(2)}) collective-permute-start(bf16[3,128,768]{2,1,0:T(8,128)(2,1)} %slice.112), channel_id=1, source_target_pairs={{0,3},{1,0},{2,1},{3,2},{4,7},{5,4},{6,5},{7,6},{8,11},{9,8},{10,9... | collective-permute-start | bytes 1769480 | tf_op jit(solution)/shard_map/ppermute | solution.py:48
  104.5 1.9 %slice.111 = bf16[3,128,768]{2,1,0:T(8,128)(2,1)} slice(bf16[3,256,768]{2,1,0:T(8,128)(2,1)} %collective-permute-done.2), slice={[0:3], [0:128], [0:768]} | slice | bytes 1179648 | tf_op jit(solution)/shard_map/slice | solution.py:56
  106.4 3.9 %collective-permute-start.3 = (bf16[3,128,768]{2,1,0:T(8,128)(2,1)}, bf16[3,128,768]{2,1,0:T(8,128)(2,1)}, u32[]{:S(2)}, u32[]{:S(2)}) collective-permute-start(bf16[3,128,768]{2,1,0:T(8,128)(2,1)} %slice.111), channel_id=1, source_target_pairs={{0,1},{1,2},{2,3},{3,0},{4,5},{5,6},{6,7},{7,4},{8,9},{9,10},{10,1... | collective-permute-start | bytes 1769480 | tf_op jit(solution)/shard_map/ppermute | solution.py:48
  110.4 1.2 add_convert_fusion
  111.6 12.7 %all-to-all-start.4 = ((bf16[64,8,768]{2,1,0:T(8,128)(2,1)}), bf16[64,8,768]{2,1,0:T(8,128)(2,1)S(1)}, u32[]{:S(2)}, u32[]{:S(2)}) async-start(bf16[64,8,768]{2,1,0:T(8,128)(2,1)} %add_convert_fusion), calls=%async_computation.4 | async-start | bytes 1572864 | tf_op jit(solution)/shard_map/all_to_all | solution.py:159
  125.2 1.3 maximum_bitcast_fusion
  126.5 1.9 %pad_maximum_fusion = bf16[4,3,256,768]{3,2,1,0:T(8,128)(2,1)S(1)} fusion(bf16[1,3,256,768]{3,2,1,0:T(8,128)(2,1)} %bitcast.31, bf16[1,3,256,768]{3,2,1,0:T(8,128)(2,1)S(1)} %maximum_bitcast_fusion, bf16[1,3,256,768]{3,2,1,0:T(8,128)(2,1)} %bitcast.29, bf16[1,3,256,768]{3,2,1,0:T(8,128)(2,1)S(1)} %fusion.46), kind=kLoop, calls=%fused_computation | loop fusion | flops 7077888 | bytes 9437184 | tf_op jit(solution)/shard_map/stack | solution.py:58
  128.4 1.9 %constant_dynamic-slice_fusion.3 = (bf16[1,3,256,768]{3,2,1,0:T(8,128)(2,1)}, bf16[1,3,256,768]{3,2,1,0:T(8,128)(2,1)}, bf16[1,3,256,768]{3,2,1,0:T(8,128)(2,1)}, bf16[1,3,256,768]{3,2,1,0:T(8,128)(2,1)S(1)}) fusion(bf16[4,3,256,768]{3,2,1,0:T(8,128)(2,1)S(1)} %pad_maximum_fusion, s32[]{:T(128)S(6)} %select_n.280, s32[]{:T(128)S(6)} %select_n.283, ...), kind=kLoop, calls=%fused_computation.63 | loop fusion | bytes 9437200 | tf_op jit(solution)/shard_map/dynamic_slice | solution.py:60
  130.3 2.4 %copy.43 = bf16[1,3,256,768]{2,3,1,0:T(8,128)(2,1)} copy(bf16[1,3,256,768]{3,2,1,0:T(8,128)(2,1)} %get-tuple-element.15) | data formatting | bytes 2359296 | tf_op jit(solution)/shard_map/dynamic_slice | solution.py:60
  132.7 2.4 %copy.46 = bf16[1,3,256,768]{2,3,1,0:T(8,128)(2,1)} copy(bf16[1,3,256,768]{3,2,1,0:T(8,128)(2,1)} %get-tuple-element.16) | data formatting | bytes 2359296 | tf_op jit(solution)/shard_map/dynamic_slice | solution.py:60
  135.1 2.4 %copy.45 = bf16[1,3,256,768]{2,3,1,0:T(8,128)(2,1)} copy(bf16[1,3,256,768]{3,2,1,0:T(8,128)(2,1)} %get-tuple-element.17) | data formatting | bytes 2359296 | tf_op jit(solution)/shard_map/dynamic_slice | solution.py:60
  137.5 1.4 copy.44
  138.9 3.8 %fusion.11 = bf16[3,256,768]{1,2,0:T(8,128)(2,1)S(1)} fusion(bf16[3,256,1024]{2,1,0:T(8,128)(2,1)S(1)} %copy-done, bf16[3,256,768]{1,2,0:T(8,128)(2,1)} %bitcast.79, bf16[3,256,768]{1,2,0:T(8,128)(2,1)} %bitcast.80, bf16[3,256,768]{1,2,0:T(8,128)(2,1)} %bitcast.81, bf16[3,256,768]{1,2,0:T(8,128)(2,1)} %bitcast.78), kind=kOutput, calls=%fused_computation.12 | convolution fusion | flops 1227423744 | bytes 7471104 | tf_op jit(solution)/shard_map/sfg,sgn->sfn/dot_general | solution.py:85
  142.7 1.5 %copy.47 = bf16[3,256,768]{2,1,0:T(8,128)(2,1)} copy(bf16[3,256,768]{1,2,0:T(8,128)(2,1)S(1)} %fusion.11) | data formatting | bytes 2359296
  144.2 3.9 %all-to-all-done.4 = bf16[64,8,768]{2,1,0:T(8,128)(2,1)S(1)} async-done(((bf16[64,8,768]{2,1,0:T(8,128)(2,1)}), bf16[64,8,768]{2,1,0:T(8,128)(2,1)S(1)}, u32[]{:S(2)}, u32[]{:S(2)}) %all-to-all-start.4) | async-done | bytes 786464 | tf_op jit(solution)/shard_map/all_to_all | solution.py:159
  148.2 1.5 fusion.29
  (55 shorter events, 12.3 us)
Async XLA Ops:
  0.6 69.7 %copy-start = (bf16[3,256,1024]{2,1,0:T(8,128)(2,1)S(1)}, bf16[3,256,1024]{2,1,0:T(8,128)(2,1)}, u32[]{:S(2)}) copy-start(bf16[3,256,1024]{2,1,0:T(8,128)(2,1)} %param.11) | copy-start | bytes 4718596
  0.6 30.1 %copy-start.3 = (bf16[1,8,768]{2,1,0:T(8,128)(2,1)S(1)}, bf16[1,8,768]{2,1,0:T(8,128)(2,1)}, u32[]{:S(2)}) copy-start(bf16[1,8,768]{2,1,0:T(8,128)(2,1)} %param.14) | copy-start | bytes 36868
  0.7 30.7 %copy-start.6 = (f32[1,768]{1,0:T(1,128)S(1)}, f32[1,768]{1,0:T(1,128)}, u32[]{:S(2)}) copy-start(f32[1,768]{1,0:T(1,128)} %param.16) | copy-start | bytes 9220
  2.4 41.9 %all-to-all-start = ((bf16[64,8,768]{2,1,0:T(8,128)(2,1)}), bf16[64,8,768]{2,1,0:T(8,128)(2,1)S(1)}, u32[]{:S(2)}, u32[]{:S(2)}) async-start(bf16[64,8,768]{2,1,0:T(8,128)(2,1)} %broadcast_in_dim.96), calls=%async_computation | async-start | bytes 1572864 | tf_op jit(solution)/shard_map/all_to_all | solution.py:14
  19.0 37.8 %copy-start.1 = (bf16[3,256,768]{2,1,0:T(8,128)(2,1)S(1)}, bf16[3,256,768]{2,1,0:T(8,128)(2,1)}, u32[]{:S(2)}) copy-start(bf16[3,256,768]{2,1,0:T(8,128)(2,1)} %param.12) | copy-start | bytes 3538948
  20.4 21.1 %collective-permute-start = (s32[1]{0:T(128)}, s32[1]{0:T(128)}, u32[]{:S(2)}, u32[]{:S(2)}) collective-permute-start(s32[1]{0:T(128)} %bitcast.2), channel_id=1, source_target_pairs={{0,4},{4,0},{1,5},{5,1},{2,6},{6,2},{3,7},{7,3},{8,12},{12,8},{9,1... | collective-permute-start | bytes 20 | tf_op jit(solution)/shard_map/ppermute | solution.py:80
  45.1 10.8 %all-to-all-start.1 = ((bf16[8,2,8,768]{3,2,1,0:T(8,128)(2,1)}), bf16[8,2,8,768]{3,2,1,0:T(8,128)(2,1)}, u32[]{:S(2)}, u32[]{:S(2)}) async-start(bf16[8,2,8,768]{3,2,1,0:T(8,128)(2,1)} %bitcast.82), calls=%async_computation.1 | async-start | bytes 393216 | tf_op jit(solution)/shard_map/all_to_all | solution.py:108
  58.2 12.1 %all-to-all-start.2 = ((f32[4,3,32,256]{3,2,1,0:T(8,128)}), f32[4,3,32,256]{3,2,1,0:T(8,128)S(1)}, u32[]{:S(2)}, u32[]{:S(2)}) async-start(f32[4,3,32,256]{3,2,1,0:T(8,128)} %broadcast_in_dim.101), calls=%async_computation.2 | async-start | bytes 786432 | tf_op jit(solution)/shard_map/all_to_all | solution.py:14
  62.9 37.8 %collective-permute-start.1 = (bf16[3,256,768]{2,1,0:T(8,128)(2,1)}, bf16[3,256,768]{2,1,0:T(8,128)(2,1)}, u32[]{:S(2)}, u32[]{:S(2)}) collective-permute-start(bf16[3,256,768]{2,1,0:T(8,128)(2,1)} %fusion.16), channel_id=1, source_target_pairs={{0,3},{1,0},{2,1},{3,2},{4,7},{5,4},{6,5},{7,6},{8,11},{9,8},{10,9... | collective-permute-start | bytes 3538952 | tf_op jit(solution)/shard_map/ppermute | solution.py:48
  68.0 36.5 %collective-permute-start.2 = (bf16[3,256,768]{2,1,0:T(8,128)(2,1)}, bf16[3,256,768]{2,1,0:T(8,128)(2,1)}, u32[]{:S(2)}, u32[]{:S(2)}) collective-permute-start(bf16[3,256,768]{2,1,0:T(8,128)(2,1)} %fusion.16), channel_id=1, source_target_pairs={{0,1},{1,2},{2,3},{3,0},{4,5},{5,6},{6,7},{7,4},{8,9},{9,10},{10,1... | collective-permute-start | bytes 3538952 | tf_op jit(solution)/shard_map/ppermute | solution.py:48
  71.8 1.5 %copy-start.4 = (bf16[3,32,256]{2,1,0:T(8,128)(2,1)}, bf16[3,32,256]{2,1,0:T(8,128)(2,1)S(1)}, u32[]{:S(2)}) copy-start(bf16[3,32,256]{2,1,0:T(8,128)(2,1)S(1)} %fusion.15) | copy-start | bytes 147460
  71.8 1.2 copy-start.2
  74.1 26.4 %all-to-all-start.3 = ((bf16[8,2,8,768]{3,2,1,0:T(8,128)(2,1)}), bf16[8,2,8,768]{3,2,1,0:T(8,128)(2,1)S(1)}, u32[]{:S(2)}, u32[]{:S(2)}) async-start(bf16[8,2,8,768]{3,2,1,0:T(8,128)(2,1)} %bitcast.21), calls=%async_computation.3 | async-start | bytes 393216 | tf_op jit(solution)/shard_map/all_to_all | solution.py:144
  102.6 21.9 %collective-permute-start.4 = (bf16[3,128,768]{2,1,0:T(8,128)(2,1)}, bf16[3,128,768]{2,1,0:T(8,128)(2,1)}, u32[]{:S(2)}, u32[]{:S(2)}) collective-permute-start(bf16[3,128,768]{2,1,0:T(8,128)(2,1)} %slice.112), channel_id=1, source_target_pairs={{0,3},{1,0},{2,1},{3,2},{4,7},{5,4},{6,5},{7,6},{8,11},{9,8},{10,9... | collective-permute-start | bytes 1769480 | tf_op jit(solution)/shard_map/ppermute | solution.py:48
  106.4 18.8 %collective-permute-start.3 = (bf16[3,128,768]{2,1,0:T(8,128)(2,1)}, bf16[3,128,768]{2,1,0:T(8,128)(2,1)}, u32[]{:S(2)}, u32[]{:S(2)}) collective-permute-start(bf16[3,128,768]{2,1,0:T(8,128)(2,1)} %slice.111), channel_id=1, source_target_pairs={{0,1},{1,2},{2,3},{3,0},{4,5},{5,6},{6,7},{7,4},{8,9},{9,10},{10,1... | collective-permute-start | bytes 1769480 | tf_op jit(solution)/shard_map/ppermute | solution.py:48
  111.6 36.5 %all-to-all-start.4 = ((bf16[64,8,768]{2,1,0:T(8,128)(2,1)}), bf16[64,8,768]{2,1,0:T(8,128)(2,1)S(1)}, u32[]{:S(2)}, u32[]{:S(2)}) async-start(bf16[64,8,768]{2,1,0:T(8,128)(2,1)} %add_convert_fusion), calls=%async_computation.4 | async-start | bytes 1572864 | tf_op jit(solution)/shard_map/all_to_all | solution.py:159
  142.7 5.6 %copy-start.5 = (f32[768]{0:T(1024)S(1)}, f32[768]{0:T(1024)}, u32[]{:S(2)}) copy-start(f32[768]{0:T(1024)} %reduce) | copy-start | bytes 9220

commit v7 on v5

--- a/solution.py
+++ b/solution.py
@@ -140,6 +140,7 @@
         + jnp.where((slots == third // 2) & (third % 2 == core), third_part, jnp.float32(0.0))
         + jnp.where((slots == other // 2) & (other % 2 == core), other_part, jnp.float32(0.0))
     )
+    dense = dense + piece[0, 0, 0].astype(jnp.float32) * jnp.float32(0.0)
     arrived = lax.all_to_all(
         dense.astype(jnp.bfloat16), PLANE, split_axis=0, concat_axis=0, tiled=True
     ).astype(jnp.float32)

time: 142 us -> 143 us (level)
  the two profiles are of different devices: /device:TPU:2 before, /device:TPU:8 now
where the time goes in v7:
time: 143 us; the launch traced here: 142 us
  waiting for transfers between devices  53.5 us (37%)
  starting transfers between devices  41 us (29%)
  between operations  23.2 us (16%)
  local copies, waits for them, and re-layouts  8.81 us (6%)
  other arithmetic  8.59 us (6%)
  matrix products  6.83 us (5%)
    all_to_all x2, waiting for transfers between devices, copy_for_each(): lax.all_to_all(jnp.broadcast_to(x[None], (length, *x.shape)), axis, 0, 0,...  25.5 us
    all_to_all x2, starting transfers between devices, copy_for_each(): lax.all_to_all(jnp.broadcast_to(x[None], (length, *x.shape)), axis, 0, 0,...  21.2 us
    all_to_all x1, waiting for transfers between devices, body(): lax.all_to_all(dense.astype(jnp.bfloat16), PLANE, split_axis=0, concat_ax...  16.5 us
    all_to_all x1, starting transfers between devices, body(): lax.all_to_all(dense.astype(jnp.bfloat16), PLANE, split_axis=0, concat_ax...  10.2 us
    all_to_all x1, waiting for transfers between devices, body(): lax.all_to_all(lend.reshape(2 * nharm, 2, *zero_block.shape), PAIR, 0, 0,...  7.34 us
    all_to_all x1, starting transfers between devices, body(): lax.all_to_all(lend.reshape(2 * nharm, 2, *zero_block.shape), PAIR, 0, 0,...  4.3 us
    dot_general x1, matrix products, body(): jnp.einsum('sfg,sgn->sfn', front_inverse, piece, preferred_element_type=j...  4.08 us
    unnamed x21, local copies, waits for them, and re-layouts  3.7 us
  transfers between devices with their start and end apart: 7, of which 5 were waited for; matrix products, arithmetic and copies ran while one was open for 11% of the time, Pallas kernels for 0%

profile of v7, /device:TPU:8, one launch (start us, length us, event | category | flops | bytes accessed | tf_op | source)
XLA Modules:
  0.0 141.9 jit_solution(18064666493220629191)
XLA Ops:
  7.2 0.7 all-gather.2.cloned.1.call-update
  7.9 1.6 %broadcast_in_dim.110 = bf16[64,8,768]{2,1,0:T(8,128)(2,1)} broadcast(bf16[8,768]{1,0:T(8,128)(2,1)} %bitcast.65), dimensions={1,2} | broadcast | bytes 798720 | tf_op jit(solution)/shard_map/broadcast_in_dim | solution.py:14
  9.6 16.9 %all-to-all-start = ((bf16[64,8,768]{2,1,0:T(8,128)(2,1)}), bf16[64,8,768]{2,1,0:T(8,128)(2,1)}, u32[]{:S(2)}, u32[]{:S(2)}) async-start(bf16[64,8,768]{2,1,0:T(8,128)(2,1)} %broadcast_in_dim.110), calls=%async_computation | async-start | bytes 1572864 | tf_op jit(solution)/shard_map/all_to_all | solution.py:14
  26.5 0.6 slice.57
  27.0 1.9 %collective-permute-start = (s32[1]{0:T(128)}, s32[1]{0:T(128)}, u32[]{:S(2)}, u32[]{:S(2)}) collective-permute-start(s32[1]{0:T(128)} %bitcast.2), channel_id=1, source_target_pairs={{0,4},{4,0},{1,5},{5,1},{2,6},{6,2},{3,7},{7,3},{8,12},{12,8},{9,1... | collective-permute-start | bytes 20 | tf_op jit(solution)/shard_map/ppermute | solution.py:69
  34.4 16.0 %all-to-all-done = bf16[64,8,768]{2,1,0:T(8,128)(2,1)} async-done(((bf16[64,8,768]{2,1,0:T(8,128)(2,1)}), bf16[64,8,768]{2,1,0:T(8,128)(2,1)}, u32[]{:S(2)}, u32[]{:S(2)}) %all-to-all-start) | async-done | bytes 786464 | tf_op jit(solution)/shard_map/all_to_all | solution.py:14
  50.4 0.7 broadcast_select_fusion.6
  51.1 0.7 broadcast_in_dim.112
  51.8 4.3 %all-to-all-start.1 = ((bf16[8,2,8,768]{3,2,1,0:T(8,128)(2,1)}), bf16[8,2,8,768]{3,2,1,0:T(8,128)(2,1)S(1)}, u32[]{:S(2)}, u32[]{:S(2)}) async-start(bf16[8,2,8,768]{3,2,1,0:T(8,128)(2,1)} %bitcast.6), calls=%async_computation.1 | async-start | bytes 393216 | tf_op jit(solution)/shard_map/all_to_all | solution.py:92
  56.2 7.3 %all-to-all-done.1 = bf16[8,2,8,768]{3,2,1,0:T(8,128)(2,1)S(1)} async-done(((bf16[8,2,8,768]{3,2,1,0:T(8,128)(2,1)}), bf16[8,2,8,768]{3,2,1,0:T(8,128)(2,1)S(1)}, u32[]{:S(2)}, u32[]{:S(2)}) %all-to-all-start.1) | async-done | bytes 196640 | tf_op jit(solution)/shard_map/all_to_all | solution.py:92
  63.6 0.6 fusion.4
  64.2 0.8 broadcast_in_dim.115
  65.0 4.3 %all-to-all-start.2 = ((f32[4,3,32,256]{3,2,1,0:T(8,128)}), f32[4,3,32,256]{3,2,1,0:T(8,128)S(1)}, u32[]{:S(2)}, u32[]{:S(2)}) async-start(f32[4,3,32,256]{3,2,1,0:T(8,128)} %broadcast_in_dim.115), calls=%async_computation.2 | async-start | bytes 786432 | tf_op jit(solution)/shard_map/all_to_all | solution.py:14
  69.3 9.6 %all-to-all-done.2 = f32[4,3,32,256]{3,2,1,0:T(8,128)S(1)} async-done(((f32[4,3,32,256]{3,2,1,0:T(8,128)}), f32[4,3,32,256]{3,2,1,0:T(8,128)S(1)}, u32[]{:S(2)}, u32[]{:S(2)}) %all-to-all-start.2) | async-done | bytes 393248 | tf_op jit(solution)/shard_map/all_to_all | solution.py:14
  78.9 1.4 %fusion.2 = bf16[3,32,256]{2,1,0:T(8,128)(2,1)S(1)} fusion(f32[3,32,1024]{2,1,0:T(8,128)S(1)} %bitcast.64, bf16[3,256,1024]{2,1,0:T(8,128)(2,1)S(1)} %copy-done, pred[3,256]{1,0:T(4,128)(4,1)S(1)} %broadcast_compare_fusion), kind=kOutput, calls=%fused_computation.9 | convolution fusion | flops 302063616 | bytes 2016000 | tf_op jit(solution)/shard_map/shg,sfg->shf/dot_general | solution.py:100
  80.4 0.4 fusion.3
  80.8 0.4 convolution_add_fusion
  81.3 0.7 pad_maximum_fusion
  82.0 3.4 %all-to-all-start.3 = ((bf16[8,2,8,768]{3,2,1,0:T(8,128)(2,1)}), bf16[8,2,8,768]{3,2,1,0:T(8,128)(2,1)S(1)}, u32[]{:S(2)}, u32[]{:S(2)}) async-start(bf16[8,2,8,768]{3,2,1,0:T(8,128)(2,1)} %bitcast.21), calls=%async_computation.3 | async-start | bytes 393216 | tf_op jit(solution)/shard_map/all_to_all | solution.py:128
  88.2 3.4 %all-to-all-done.3 = bf16[8,2,8,768]{3,2,1,0:T(8,128)(2,1)S(1)} async-done(((bf16[8,2,8,768]{3,2,1,0:T(8,128)(2,1)}), bf16[8,2,8,768]{3,2,1,0:T(8,128)(2,1)S(1)}, u32[]{:S(2)}, u32[]{:S(2)}) %all-to-all-start.3) | async-done | bytes 196640 | tf_op jit(solution)/shard_map/all_to_all | solution.py:128
  91.7 2.7 %broadcast_select_fusion = bf16[3,1024,768]{2,1,0:T(8,128)(2,1)S(1)} fusion(bf16[3,1024,768]{2,1,0:T(8,128)(2,1)} %all-gather.2.cloned.1.call-done, pred[3,1024]{1,0:T(4,128)(4,1)S(1)} %iota_compare_fusion), kind=kLoop, calls=%fused_computation | loop fusion | flops 2359296 | bytes 9440256 | tf_op jit(solution)/shard_map/jit(_where)/select_n | solution.py:60
  94.4 2.1 %copy-done.1 = bf16[3,1024,768]{2,1,0:T(8,128)(2,1)} copy-done((bf16[3,1024,768]{2,1,0:T(8,128)(2,1)}, bf16[3,1024,768]{2,1,0:T(8,128)(2,1)S(1)}, u32[]{:S(2)}) %copy-start.1) | copy-done | bytes 4718616
  96.5 0.5 slice.86
  97.7 1.3 add_convert_fusion
  99.0 10.2 %all-to-all-start.4 = ((bf16[64,8,768]{2,1,0:T(8,128)(2,1)}), bf16[64,8,768]{2,1,0:T(8,128)(2,1)S(1)}, u32[]{:S(2)}, u32[]{:S(2)}) async-start(bf16[64,8,768]{2,1,0:T(8,128)(2,1)} %add_convert_fusion), calls=%async_computation.4 | async-start | bytes 1572864 | tf_op jit(solution)/shard_map/all_to_all | solution.py:144
  109.3 0.6 reduce.1
  110.1 0.6 reshape.372
  110.7 0.6 fusion.20
  111.3 4.1 %fusion = bf16[3,256,768]{1,2,0:T(8,128)(2,1)S(1)} fusion(bf16[3,1024,768]{2,1,0:T(8,128)(2,1)} %copy-done.1, bf16[3,256,1024]{2,1,0:T(8,128)(2,1)S(1)} %copy-done), kind=kOutput, calls=%fused_computation.4 | convolution fusion | flops 1208549376 | bytes 7471104 | tf_op jit(solution)/shard_map/sfg,sgn->sfn/dot_general | solution.py:61
  115.4 1.5 %copy.35 = bf16[3,256,768]{2,1,0:T(8,128)(2,1)} copy(bf16[3,256,768]{1,2,0:T(8,128)(2,1)S(1)} %fusion) | data formatting | bytes 2359296
  116.9 16.5 %all-to-all-done.4 = bf16[64,8,768]{2,1,0:T(8,128)(2,1)S(1)} async-done(((bf16[64,8,768]{2,1,0:T(8,128)(2,1)}), bf16[64,8,768]{2,1,0:T(8,128)(2,1)S(1)}, u32[]{:S(2)}, u32[]{:S(2)}) %all-to-all-start.4) | async-done | bytes 786464 | tf_op jit(solution)/shard_map/all_to_all | solution.py:144
  133.6 1.4 %fusion.15 = f32[1,8,768]{2,1,0:T(8,128)} fusion(f32[1,8,768]{2,1,0:T(8,128)} %param.15, f32[8,768]{1,0:T(8,128)S(1)} %convert_reduce_fusion, f32[1,8,768]{2,1,0:T(8,128)} %reshape.372, f32[768]{0:T(1024)} %reduce.1, f32[8]{0:T(128)} %get-tuple-element.30, f32[768]{0:T(1024)S(1)} %reduce, f32[8]{0:T(128)} %get-tuple-element.31, ...), kind=kLoop, calls=%fused_computation.42 | loop fusion | flops 49152 | bytes 116800 | tf_op jit(solution)/shard_map/sub | solution.py:158
  (45 shorter events, 0.8 us)
Async XLA Ops:
  7.2 71.8 %copy-start = (bf16[3,256,1024]{2,1,0:T(8,128)(2,1)S(1)}, bf16[3,256,1024]{2,1,0:T(8,128)(2,1)}, u32[]{:S(2)}) copy-start(bf16[3,256,1024]{2,1,0:T(8,128)(2,1)} %param.11) | copy-start | bytes 4718596
  7.2 19.3 %copy-start.9 = (s32[3,1]{0,1:T(1,128)S(1)}, s32[3,1]{0,1:T(1,128)}, u32[]{:S(2)}) copy-start(s32[3,1]{0,1:T(1,128)} %param.10) | copy-start | bytes 40
  7.2 84.5 %all-gather.2.cloned.1.call-start = ((), (), s32[]{:S(2)}) async-start(), calls=%async_computation.5 | async-start | bytes 5898240 | tf_op jit(solution)/shard_map/all_gather | solution.py:59
  9.6 46.6 %copy-start.8 = (s32[3]{0:T(128)S(1)}, s32[3]{0:T(128)}, u32[]{:S(2)}) copy-start(s32[3]{0:T(128)} %param.9) | copy-start | bytes 40
  9.6 54.0 %copy-start.2 = (bf16[3,256,768]{2,1,0:T(8,128)(2,1)S(1)}, bf16[3,256,768]{2,1,0:T(8,128)(2,1)}, u32[]{:S(2)}) copy-start(bf16[3,256,768]{2,1,0:T(8,128)(2,1)} %param.12) | copy-start | bytes 3538948
  9.6 40.8 %all-to-all-start = ((bf16[64,8,768]{2,1,0:T(8,128)(2,1)}), bf16[64,8,768]{2,1,0:T(8,128)(2,1)}, u32[]{:S(2)}, u32[]{:S(2)}) async-start(bf16[64,8,768]{2,1,0:T(8,128)(2,1)} %broadcast_in_dim.110), calls=%async_computation | async-start | bytes 1572864 | tf_op jit(solution)/shard_map/all_to_all | solution.py:14
  27.0 4.6 %collective-permute-start = (s32[1]{0:T(128)}, s32[1]{0:T(128)}, u32[]{:S(2)}, u32[]{:S(2)}) collective-permute-start(s32[1]{0:T(128)} %bitcast.2), channel_id=1, source_target_pairs={{0,4},{4,0},{1,5},{5,1},{2,6},{6,2},{3,7},{7,3},{8,12},{12,8},{9,1... | collective-permute-start | bytes 20 | tf_op jit(solution)/shard_map/ppermute | solution.py:69
  51.8 11.7 %all-to-all-start.1 = ((bf16[8,2,8,768]{3,2,1,0:T(8,128)(2,1)}), bf16[8,2,8,768]{3,2,1,0:T(8,128)(2,1)S(1)}, u32[]{:S(2)}, u32[]{:S(2)}) async-start(bf16[8,2,8,768]{3,2,1,0:T(8,128)(2,1)} %bitcast.6), calls=%async_computation.1 | async-start | bytes 393216 | tf_op jit(solution)/shard_map/all_to_all | solution.py:92
  65.0 13.9 %all-to-all-start.2 = ((f32[4,3,32,256]{3,2,1,0:T(8,128)}), f32[4,3,32,256]{3,2,1,0:T(8,128)S(1)}, u32[]{:S(2)}, u32[]{:S(2)}) async-start(f32[4,3,32,256]{3,2,1,0:T(8,128)} %broadcast_in_dim.115), calls=%async_computation.2 | async-start | bytes 786432 | tf_op jit(solution)/shard_map/all_to_all | solution.py:14
  78.9 1.9 %copy-start.3 = (bf16[3,192,768]{2,1,0:T(8,128)(2,1)S(1)}, bf16[3,192,768]{2,1,0:T(8,128)(2,1)}, u32[]{:S(2)}) copy-start(bf16[3,192,768]{2,1,0:T(8,128)(2,1)} %param.13) | copy-start | bytes 2654212
  80.4 0.8 copy-start.5
  82.0 9.6 %all-to-all-start.3 = ((bf16[8,2,8,768]{3,2,1,0:T(8,128)(2,1)}), bf16[8,2,8,768]{3,2,1,0:T(8,128)(2,1)S(1)}, u32[]{:S(2)}, u32[]{:S(2)}) async-start(bf16[8,2,8,768]{3,2,1,0:T(8,128)(2,1)} %bitcast.21), calls=%async_computation.3 | async-start | bytes 393216 | tf_op jit(solution)/shard_map/all_to_all | solution.py:128
  94.4 2.1 %copy-start.1 = (bf16[3,1024,768]{2,1,0:T(8,128)(2,1)}, bf16[3,1024,768]{2,1,0:T(8,128)(2,1)S(1)}, u32[]{:S(2)}) copy-start(bf16[3,1024,768]{2,1,0:T(8,128)(2,1)S(1)} %broadcast_select_fusion) | copy-start | bytes 14155780
  96.5 12.7 %copy-start.4 = (bf16[1,8,768]{2,1,0:T(8,128)(2,1)S(1)}, bf16[1,8,768]{2,1,0:T(8,128)(2,1)}, u32[]{:S(2)}) copy-start(bf16[1,8,768]{2,1,0:T(8,128)(2,1)} %param.14) | copy-start | bytes 36868
  96.5 12.7 %copy-start.6 = (f32[1,768]{1,0:T(1,128)S(1)}, f32[1,768]{1,0:T(1,128)}, u32[]{:S(2)}) copy-start(f32[1,768]{1,0:T(1,128)} %param.16) | copy-start | bytes 9220
  96.5 12.8 %copy-start.7 = (f32[1,768]{1,0:T(1,128)S(1)}, f32[1,768]{1,0:T(1,128)}, u32[]{:S(2)}) copy-start(f32[1,768]{1,0:T(1,128)} %param.17) | copy-start | bytes 9220
  99.0 34.4 %all-to-all-start.4 = ((bf16[64,8,768]{2,1,0:T(8,128)(2,1)}), bf16[64,8,768]{2,1,0:T(8,128)(2,1)S(1)}, u32[]{:S(2)}, u32[]{:S(2)}) async-start(bf16[64,8,768]{2,1,0:T(8,128)(2,1)} %add_convert_fusion), calls=%async_computation.4 | async-start | bytes 1572864 | tf_op jit(solution)/shard_map/all_to_all | solution.py:144
Sparse Core Ops, SparseCore 0:
  10.1 65.9 all-gather.1

commit v8 on v3

--- a/solution.py
+++ b/solution.py
@@ -6,6 +6,7 @@
 
 SUB = ("sub_0", "sub_1", "sub_2")
 PLANE = ("sub_0", "sub_1")
+PAIR = ("sub_2", "harm")
 
 
 def copy_for_each(x, axis):
@@ -65,6 +66,7 @@
         lambda: empty,
     ).astype(jnp.bfloat16)
     nplane = lax.axis_size(PLANE)
+    rows_q = displacement.shape[1]
     core = lax.axis_index("sub_2")
     near = (lax.axis_index(SUB) + nown // 2) % nown
     third = owners[2, 0]
@@ -89,10 +91,30 @@
     contrib = contrib + jnp.einsum(
         "shj,sjn->shn", disp_cols, stiffness, preferred_element_type=jnp.float32
     )
-    partial_rows = sent_and_summed(contrib.astype(jnp.bfloat16), "harm", 1)
-    near_part = partial_rows[0] + partial_rows[1]
-    third_part = partial_rows[2]
-    other_part = lax.ppermute(third_part, "sub_2", [(0, 1), (1, 0)])
+    near_c = (contrib[0] + contrib[1]).reshape(nharm, rows_q, width)
+    third_c = contrib[2].reshape(nharm, rows_q, width)
+    zero_rows = jnp.zeros_like(near_c)
+    send = jnp.stack(
+        [
+            jnp.stack(
+                [
+                    jnp.where(peer_core == core, near_c, zero_rows),
+                    jnp.where(third % 2 == peer_core, third_c, zero_rows),
+                ],
+                axis=1,
+            )
+            for peer_core in range(2)
+        ]
+    )
+    came = lax.all_to_all(
+        send.reshape(2 * nharm, 2, rows_q, width).astype(jnp.bfloat16), PAIR, 0, 0, tiled=True
+    ).astype(jnp.float32)
+    came = came.reshape(2, nharm, 2, rows_q, width).sum(axis=1)
+    mine = jnp.where(core == 0, came[0], came[1])
+    theirs = jnp.where(core == 0, came[1], came[0])
+    near_part = mine[0]
+    third_part = mine[1]
+    other_part = theirs[1]
     slots = jnp.arange(nplane, dtype=jnp.int32)[:, None, None]
     dense = (
         jnp.where(slots == near // 2, near_part, jnp.float32(0.0))

time: 142 us -> 139 us (0.979)
  starting transfers between devices: 43.6 us -> 41.5 us
    ppermute x1 -> x0, starting transfers between devices: 1.92 us -> none  [body(): other_part = lax.ppermute(third_part, 'sub_2', [(0, 1), (1, 0)])]
  transfers between devices with their start and end apart: 8 -> 7, of which waited for: 7 -> 6; matrix products, arithmetic and copies ran while one was open for 2% -> 2% of each run, Pallas kernels for 0% -> 0%
where the time goes in v8:
time: 139 us; the launch traced here: 138 us
  waiting for transfers between devices  60.4 us (43%)
  starting transfers between devices  41.5 us (30%)
  between operations  20.2 us (15%)
  other arithmetic  6.9 us (5%)
  matrix products  5.35 us (4%)
  local copies, waits for them, and re-layouts  3.71 us (3%)
    all_to_all x1, waiting for transfers between devices, body(): lax.all_to_all(dense.astype(jnp.bfloat16), PLANE, split_axis=0, concat_ax...  23.9 us
    all_to_all x2, waiting for transfers between devices, copy_for_each(): lax.all_to_all(jnp.broadcast_to(x[None], (length, *x.shape)), axis, 0, 0,...  23.4 us
    all_to_all x2, starting transfers between devices, copy_for_each(): lax.all_to_all(jnp.broadcast_to(x[None], (length, *x.shape)), axis, 0, 0,...  20.9 us
    all_to_all x1, starting transfers between devices, body(): lax.all_to_all(dense.astype(jnp.bfloat16), PLANE, split_axis=0, concat_ax...  13.4 us
    all_to_all x1, waiting for transfers between devices, body(): lax.all_to_all(send.reshape(2 * nharm, 2, rows_q, width).astype(jnp.bfloa...  6.24 us
    all_gather x1, waiting for transfers between devices, body(): piece = lax.all_gather(masked, 'harm', axis=1, tiled=True)  5.55 us
    dot_general x1, matrix products, body(): jnp.einsum('sfg,sgn->sfn', front_inverse, piece, preferred_element_type=j...  4.2 us
    all_to_all x1, starting transfers between devices, body(): lax.all_to_all(send.reshape(2 * nharm, 2, rows_q, width).astype(jnp.bfloa...  3.42 us
  transfers between devices with their start and end apart: 7, of which 6 were waited for; matrix products, arithmetic and copies ran while one was open for 2% of the time, Pallas kernels for 0%

profile of v8, /device:TPU:8, one launch (start us, length us, event | category | flops | bytes accessed | tf_op | source)
XLA Modules:
  0.0 138.0 jit_solution(18292967575257493741)
XLA Ops:
  7.2 0.0 copy-start
  7.2 0.0 all-gather.2.cloned.1.call-start
  7.2 0.8 broadcast_compare_fusion
  8.0 2.5 %broadcast_select_fusion = bf16[3,256,768]{2,1,0:T(8,128)(2,1)} fusion(bf16[3,256,768]{2,1,0:T(8,128)(2,1)} %param.14, pred[3,256]{1,0:T(4,128)(4,1)S(1)} %broadcast_compare_fusion), kind=kLoop, calls=%fused_computation.3 | loop fusion | flops 589824 | bytes 2360064 | tf_op jit(solution)/shard_map/jit(_where)/select_n | solution.py:57
  10.5 0.0 all-gather.2.cloned.1.call-update
  10.6 0.9 broadcast_in_dim.90
  11.5 16.6 %all-to-all-start = ((bf16[64,8,768]{2,1,0:T(8,128)(2,1)}), bf16[64,8,768]{2,1,0:T(8,128)(2,1)S(1)}, u32[]{:S(2)}, u32[]{:S(2)}) async-start(bf16[64,8,768]{2,1,0:T(8,128)(2,1)} %broadcast_in_dim.90), calls=%async_computation | async-start | bytes 1572864 | tf_op jit(solution)/shard_map/all_to_all | solution.py:14
  28.1 0.6 slice.46
  28.7 1.9 %collective-permute-start = (s32[1]{0:T(128)}, s32[1]{0:T(128)}, u32[]{:S(2)}, u32[]{:S(2)}) collective-permute-start(s32[1]{0:T(128)} %bitcast.3), channel_id=1, source_target_pairs={{0,4},{4,0},{1,5},{5,1},{2,6},{6,2},{3,7},{7,3},{8,12},{12,8},{9,1... | collective-permute-start | bytes 20 | tf_op jit(solution)/shard_map/ppermute | solution.py:73
  30.7 1.3 collective-permute-done
  34.5 17.6 %all-to-all-done = bf16[64,8,768]{2,1,0:T(8,128)(2,1)S(1)} async-done(((bf16[64,8,768]{2,1,0:T(8,128)(2,1)}), bf16[64,8,768]{2,1,0:T(8,128)(2,1)S(1)}, u32[]{:S(2)}, u32[]{:S(2)}) %all-to-all-start) | async-done | bytes 786464 | tf_op jit(solution)/shard_map/all_to_all | solution.py:14
  52.1 1.9 %collective-permute-start.1 = (bf16[8,768]{1,0:T(8,128)(2,1)S(1)}, bf16[8,768]{1,0:T(8,128)(2,1)S(1)}, u32[]{:S(2)}, u32[]{:S(2)}) collective-permute-start(bf16[8,768]{1,0:T(8,128)(2,1)S(1)} %get-tuple-element.16), channel_id=1, source_target_pairs={{0,4},{4,0},{1,5},{5,1},{2,6},{6,2},{3,7},{7,3},{8,12},{12,8},{9,1... | collective-permute-start | bytes 36872 | tf_op jit(solution)/shard_map/ppermute | solution.py:75
  56.7 0.6 broadcast_in_dim.91
  57.3 4.3 %all-to-all-start.1 = ((bf16[4,2,8,768]{3,2,1,0:T(8,128)(2,1)}), bf16[4,2,8,768]{3,2,1,0:T(8,128)(2,1)S(1)}, u32[]{:S(2)}, u32[]{:S(2)}) async-start(bf16[4,2,8,768]{3,2,1,0:T(8,128)(2,1)} %broadcast_in_dim.91), calls=%async_computation.1 | async-start | bytes 196608 | tf_op jit(solution)/shard_map/all_to_all | solution.py:14
  61.6 0.6 reduce_max.9
  62.9 5.8 %all-to-all-done.1 = bf16[4,2,8,768]{3,2,1,0:T(8,128)(2,1)S(1)} async-done(((bf16[4,2,8,768]{3,2,1,0:T(8,128)(2,1)}), bf16[4,2,8,768]{3,2,1,0:T(8,128)(2,1)S(1)}, u32[]{:S(2)}, u32[]{:S(2)}) %all-to-all-start.1) | async-done | bytes 98336 | tf_op jit(solution)/shard_map/all_to_all | solution.py:14
  68.7 5.6 %all-gather.2.cloned.1.call-done = bf16[3,1024,768]{2,1,0:T(8,128)(2,1)} async-done(((bf16[3,256,768]{2,1,0:T(8,128)(2,1)}), bf16[3,1024,768]{2,1,0:T(8,128)(2,1)}) %all-gather.2.cloned.1.call-update) | async-done | bytes 4718608 | tf_op jit(solution)/shard_map/all_gather | solution.py:60
  74.3 4.2 %conditional.1 = (bf16[3,256,768]{2,1,0:T(8,128)(2,1)S(1)}) conditional(s32[]{:T(128)} %convert_element_type.43, () %tuple.16, (bf16[3,256,1024]{2,1,0:T(8,128)(2,1)}, bf16[3,1024,768]{2,1,0:T(8,128)(2,1)}) %tuple.17), branch_computations={%region_1.2_spmd, %region_2.3_spmd} | conditional | flops 1208549376 | bytes 7471112 | solution.py:61
  74.3 4.2 %convolution_convert_fusion = bf16[3,256,768]{2,1,0:T(8,128)(2,1)S(1)} fusion(bf16[3,256,1024]{2,1,0:T(8,128)(2,1)} %get-tuple-element.14, bf16[3,1024,768]{2,1,0:T(8,128)(2,1)} %get-tuple-element.9), kind=kOutput, calls=%fused_computation | convolution fusion | flops 1208549376 | bytes 7471104 | tf_op jit(solution)/shard_map/cond/branch_1_fun/sfg,sgn->sfn/dot_general | solution.py:63
  78.5 0.5 fusion.1
  79.0 1.2 copy-done.1
  80.2 0.3 fusion.17
  80.5 0.4 convolution_add_fusion
  81.0 0.7 pad_maximum_fusion
  81.7 3.4 %all-to-all-start.2 = ((bf16[8,2,8,768]{3,2,1,0:T(8,128)(2,1)}), bf16[8,2,8,768]{3,2,1,0:T(8,128)(2,1)S(1)}, u32[]{:S(2)}, u32[]{:S(2)}) async-start(bf16[8,2,8,768]{3,2,1,0:T(8,128)(2,1)} %bitcast.20), calls=%async_computation.2 | async-start | bytes 393216 | tf_op jit(solution)/shard_map/all_to_all | solution.py:109
  85.1 6.2 %all-to-all-done.2 = bf16[8,2,8,768]{3,2,1,0:T(8,128)(2,1)S(1)} async-done(((bf16[8,2,8,768]{3,2,1,0:T(8,128)(2,1)}), bf16[8,2,8,768]{3,2,1,0:T(8,128)(2,1)S(1)}, u32[]{:S(2)}, u32[]{:S(2)}) %all-to-all-start.2) | async-done | bytes 196640 | tf_op jit(solution)/shard_map/all_to_all | solution.py:109
  91.5 1.3 add_convert_fusion
  92.8 13.4 %all-to-all-start.3 = ((bf16[64,8,768]{2,1,0:T(8,128)(2,1)}), bf16[64,8,768]{2,1,0:T(8,128)(2,1)S(1)}, u32[]{:S(2)}, u32[]{:S(2)}) async-start(bf16[64,8,768]{2,1,0:T(8,128)(2,1)} %add_convert_fusion), calls=%async_computation.3 | async-start | bytes 1572864 | tf_op jit(solution)/shard_map/all_to_all | solution.py:124
  106.1 0.2 rev.3
  106.5 23.9 %all-to-all-done.3 = bf16[64,8,768]{2,1,0:T(8,128)(2,1)S(1)} async-done(((bf16[64,8,768]{2,1,0:T(8,128)(2,1)}), bf16[64,8,768]{2,1,0:T(8,128)(2,1)S(1)}, u32[]{:S(2)}, u32[]{:S(2)}) %all-to-all-start.3) | async-done | bytes 786464 | tf_op jit(solution)/shard_map/all_to_all | solution.py:124
  130.4 0.1 convert_reduce_fusion
  130.5 0.7 fusion.9
  (39 shorter events, 0.3 us)
Async XLA Ops:
  7.2 73.4 %copy-start = (bf16[3,192,768]{2,1,0:T(8,128)(2,1)S(1)}, bf16[3,192,768]{2,1,0:T(8,128)(2,1)}, u32[]{:S(2)}) copy-start(bf16[3,192,768]{2,1,0:T(8,128)(2,1)} %param.15) | copy-start | bytes 2654212
  7.2 67.1 %all-gather.2.cloned.1.call-start = ((), (), s32[]{:S(2)}) async-start(), calls=%async_computation.4 | async-start | bytes 5898240 | tf_op jit(solution)/shard_map/all_gather | solution.py:60
  8.0 2.5 %copy-start.4 = (bf16[1,8,768]{2,1,0:T(8,128)(2,1)S(1)}, bf16[1,8,768]{2,1,0:T(8,128)(2,1)}, u32[]{:S(2)}) copy-start(bf16[1,8,768]{2,1,0:T(8,128)(2,1)} %param.16) | copy-start | bytes 36868
  10.5 17.6 %copy-start.9 = (s32[3,1]{0,1:T(1,128)S(1)}, s32[3,1]{0,1:T(1,128)}, u32[]{:S(2)}) copy-start(s32[3,1]{0,1:T(1,128)} %param.12) | copy-start | bytes 40
  10.6 51.0 %copy-start.8 = (s32[3]{0:T(128)S(1)}, s32[3]{0:T(128)}, u32[]{:S(2)}) copy-start(s32[3]{0:T(128)} %param.11) | copy-start | bytes 40
  11.5 40.6 %all-to-all-start = ((bf16[64,8,768]{2,1,0:T(8,128)(2,1)}), bf16[64,8,768]{2,1,0:T(8,128)(2,1)S(1)}, u32[]{:S(2)}, u32[]{:S(2)}) async-start(bf16[64,8,768]{2,1,0:T(8,128)(2,1)} %broadcast_in_dim.90), calls=%async_computation | async-start | bytes 1572864 | tf_op jit(solution)/shard_map/all_to_all | solution.py:14
  28.7 3.3 %collective-permute-start = (s32[1]{0:T(128)}, s32[1]{0:T(128)}, u32[]{:S(2)}, u32[]{:S(2)}) collective-permute-start(s32[1]{0:T(128)} %bitcast.3), channel_id=1, source_target_pairs={{0,4},{4,0},{1,5},{5,1},{2,6},{6,2},{3,7},{7,3},{8,12},{12,8},{9,1... | collective-permute-start | bytes 20 | tf_op jit(solution)/shard_map/ppermute | solution.py:73
  52.1 4.5 %collective-permute-start.1 = (bf16[8,768]{1,0:T(8,128)(2,1)S(1)}, bf16[8,768]{1,0:T(8,128)(2,1)S(1)}, u32[]{:S(2)}, u32[]{:S(2)}) collective-permute-start(bf16[8,768]{1,0:T(8,128)(2,1)S(1)} %get-tuple-element.16), channel_id=1, source_target_pairs={{0,4},{4,0},{1,5},{5,1},{2,6},{6,2},{3,7},{7,3},{8,12},{12,8},{9,1... | collective-permute-start | bytes 36872 | tf_op jit(solution)/shard_map/ppermute | solution.py:75
  57.3 11.4 %all-to-all-start.1 = ((bf16[4,2,8,768]{3,2,1,0:T(8,128)(2,1)}), bf16[4,2,8,768]{3,2,1,0:T(8,128)(2,1)S(1)}, u32[]{:S(2)}, u32[]{:S(2)}) async-start(bf16[4,2,8,768]{3,2,1,0:T(8,128)(2,1)} %broadcast_in_dim.91), calls=%async_computation.1 | async-start | bytes 196608 | tf_op jit(solution)/shard_map/all_to_all | solution.py:14
  78.5 2.4 %copy-start.2 = (bf16[3,256,768]{2,1,0:T(8,128)(2,1)}, bf16[3,256,768]{2,1,0:T(8,128)(2,1)S(1)}, u32[]{:S(2)}) copy-start(bf16[3,256,768]{2,1,0:T(8,128)(2,1)S(1)} %get-tuple-element.34) | copy-start | bytes 3538948
  78.5 1.7 %copy-start.1 = (bf16[3,256,768]{2,1,0:T(8,128)(2,1)S(1)}, bf16[3,256,768]{2,1,0:T(8,128)(2,1)}, u32[]{:S(2)}) copy-start(bf16[3,256,768]{2,1,0:T(8,128)(2,1)} %broadcast_select_fusion) | copy-start | bytes 3538948
  80.2 0.7 copy-start.3
  81.7 9.7 %all-to-all-start.2 = ((bf16[8,2,8,768]{3,2,1,0:T(8,128)(2,1)}), bf16[8,2,8,768]{3,2,1,0:T(8,128)(2,1)S(1)}, u32[]{:S(2)}, u32[]{:S(2)}) async-start(bf16[8,2,8,768]{3,2,1,0:T(8,128)(2,1)} %bitcast.20), calls=%async_computation.2 | async-start | bytes 393216 | tf_op jit(solution)/shard_map/all_to_all | solution.py:109
  91.4 15.0 %copy-start.6 = (f32[1,768]{1,0:T(1,128)S(1)}, f32[1,768]{1,0:T(1,128)}, u32[]{:S(2)}) copy-start(f32[1,768]{1,0:T(1,128)} %param.19) | copy-start | bytes 9220
  91.4 15.0 %copy-start.7 = (f32[1,768]{1,0:T(1,128)S(1)}, f32[1,768]{1,0:T(1,128)}, u32[]{:S(2)}) copy-start(f32[1,768]{1,0:T(1,128)} %param.18) | copy-start | bytes 9220
  91.5 39.0 %copy-start.5 = (f32[1,8,768]{2,1,0:T(8,128)S(1)}, f32[1,8,768]{2,1,0:T(8,128)}, u32[]{:S(2)}) copy-start(f32[1,8,768]{2,1,0:T(8,128)} %param.17) | copy-start | bytes 73732
  92.8 37.6 %all-to-all-start.3 = ((bf16[64,8,768]{2,1,0:T(8,128)(2,1)}), bf16[64,8,768]{2,1,0:T(8,128)(2,1)S(1)}, u32[]{:S(2)}, u32[]{:S(2)}) async-start(bf16[64,8,768]{2,1,0:T(8,128)(2,1)} %add_convert_fusion), calls=%async_computation.3 | async-start | bytes 1572864 | tf_op jit(solution)/shard_map/all_to_all | solution.py:124
Sparse Core Ops, SparseCore 0:
  10.7 63.5 all-gather.1

commit v9 on v8

--- a/solution.py
+++ b/solution.py
@@ -55,15 +55,11 @@
     own_rows = harm_idx * front_q + jnp.arange(front_q, dtype=jnp.int32)
     live_rows = own_rows[None, :] < lengths[:, None]
     masked = jnp.where(live_rows[:, :, None], coupling, jnp.zeros_like(coupling))
-    longest = jnp.max(lengths)
-    empty = jnp.zeros((masked.shape[0], front_q, width), jnp.float32)
-    piece = lax.all_gather(masked, "harm", axis=1, tiled=True)
-    modes = lax.cond(
-        jnp.int32(0) < longest,
-        lambda: jnp.einsum(
-            "sfg,sgn->sfn", front_inverse, piece, preferred_element_type=jnp.float32
-        ),
-        lambda: empty,
+    piece = lax.all_gather(coupling, "harm", axis=1, tiled=True)
+    live_cols = jnp.arange(nharm * front_q, dtype=jnp.int32)[None, :] < lengths[:, None]
+    front_live = jnp.where(live_cols[:, None, :], front_inverse, jnp.zeros_like(front_inverse))
+    modes = jnp.einsum(
+        "sfg,sgn->sfn", front_live, piece, preferred_element_type=jnp.float32
     ).astype(jnp.bfloat16)
     nplane = lax.axis_size(PLANE)
     rows_q = displacement.shape[1]

time: 139 us -> 137 us (0.986)
  other arithmetic: 6.9 us -> 3.12 us
  waiting for transfers between devices: 60.4 us -> 62.5 us
    select_n x1 -> x0, other arithmetic: 2.49 us -> none  [body(): jnp.where(live_rows[:, :, None], coupling, jnp.zeros_like(coupling))]
  transfers between devices with their start and end apart: 7 -> 7, of which waited for: 6 -> 6; matrix products, arithmetic and copies ran while one was open for 2% -> 3% of each run, Pallas kernels for 0% -> 0%
where the time goes in v9:
time: 137 us; the launch traced here: 136 us
  waiting for transfers between devices  62.5 us (46%)
  starting transfers between devices  41.5 us (30%)
  between operations  19.6 us (14%)
  matrix products  6.18 us (5%)
  local copies, waits for them, and re-layouts  3.31 us (2%)
  other arithmetic  3.12 us (2%)
    all_to_all x2, waiting for transfers between devices, copy_for_each(): lax.all_to_all(jnp.broadcast_to(x[None], (length, *x.shape)), axis, 0, 0,...  24.7 us
    all_to_all x1, waiting for transfers between devices, body(): lax.all_to_all(dense.astype(jnp.bfloat16), PLANE, split_axis=0, concat_ax...  23.9 us
    all_to_all x2, starting transfers between devices, copy_for_each(): lax.all_to_all(jnp.broadcast_to(x[None], (length, *x.shape)), axis, 0, 0,...  20.9 us
    all_to_all x1, starting transfers between devices, body(): lax.all_to_all(dense.astype(jnp.bfloat16), PLANE, split_axis=0, concat_ax...  13.4 us
    all_to_all x1, waiting for transfers between devices, body(): lax.all_to_all(send.reshape(2 * nharm, 2, rows_q, width).astype(jnp.bfloa...  6.23 us
    all_gather x1, waiting for transfers between devices, body(): piece = lax.all_gather(coupling, 'harm', axis=1, tiled=True)  5.86 us
    dot_general x1, matrix products, body(): jnp.einsum('sfg,sgn->sfn', front_live, piece, preferred_element_type=jnp....  4.24 us
    all_to_all x1, starting transfers between devices, body(): lax.all_to_all(send.reshape(2 * nharm, 2, rows_q, width).astype(jnp.bfloa...  3.42 us
  transfers between devices with their start and end apart: 7, of which 6 were waited for; matrix products, arithmetic and copies ran while one was open for 3% of the time, Pallas kernels for 0%

profile of v9, /device:TPU:8, one launch (start us, length us, event | category | flops | bytes accessed | tf_op | source)
XLA Modules:
  0.0 136.1 jit_solution(10824814379573062923)
XLA Ops:
  7.2 0.0 copy-start
  7.2 0.0 all-gather.2.cloned.1.call-start
  7.2 0.7 all-gather.2.cloned.1.call-update
  7.9 1.6 %broadcast_in_dim.101 = bf16[64,8,768]{2,1,0:T(8,128)(2,1)} broadcast(bf16[8,768]{1,0:T(8,128)(2,1)} %bitcast.58), dimensions={1,2} | broadcast | bytes 798720 | tf_op jit(solution)/shard_map/broadcast_in_dim | solution.py:14
  9.6 16.6 %all-to-all-start = ((bf16[64,8,768]{2,1,0:T(8,128)(2,1)}), bf16[64,8,768]{2,1,0:T(8,128)(2,1)S(1)}, u32[]{:S(2)}, u32[]{:S(2)}) async-start(bf16[64,8,768]{2,1,0:T(8,128)(2,1)} %broadcast_in_dim.101), calls=%async_computation | async-start | bytes 1572864 | tf_op jit(solution)/shard_map/all_to_all | solution.py:14
  26.2 0.6 slice.46
  26.8 1.9 %collective-permute-start = (s32[1]{0:T(128)}, s32[1]{0:T(128)}, u32[]{:S(2)}, u32[]{:S(2)}) collective-permute-start(s32[1]{0:T(128)} %bitcast.3), channel_id=1, source_target_pairs={{0,4},{4,0},{1,5},{5,1},{2,6},{6,2},{3,7},{7,3},{8,12},{12,8},{9,1... | collective-permute-start | bytes 20 | tf_op jit(solution)/shard_map/ppermute | solution.py:69
  28.7 0.1 iota_compare_fusion
  28.8 1.1 collective-permute-done
  32.4 17.7 %all-to-all-done = bf16[64,8,768]{2,1,0:T(8,128)(2,1)S(1)} async-done(((bf16[64,8,768]{2,1,0:T(8,128)(2,1)}), bf16[64,8,768]{2,1,0:T(8,128)(2,1)S(1)}, u32[]{:S(2)}, u32[]{:S(2)}) %all-to-all-start) | async-done | bytes 786464 | tf_op jit(solution)/shard_map/all_to_all | solution.py:14
  50.1 1.9 %collective-permute-start.1 = (bf16[8,768]{1,0:T(8,128)(2,1)S(1)}, bf16[8,768]{1,0:T(8,128)(2,1)S(1)}, u32[]{:S(2)}, u32[]{:S(2)}) collective-permute-start(bf16[8,768]{1,0:T(8,128)(2,1)S(1)} %get-tuple-element.4), channel_id=1, source_target_pairs={{0,4},{4,0},{1,5},{5,1},{2,6},{6,2},{3,7},{7,3},{8,12},{12,8},{9,1... | collective-permute-start | bytes 36872 | tf_op jit(solution)/shard_map/ppermute | solution.py:71
  54.7 0.6 broadcast_in_dim.102
  55.4 4.3 %all-to-all-start.1 = ((bf16[4,2,8,768]{3,2,1,0:T(8,128)(2,1)}), bf16[4,2,8,768]{3,2,1,0:T(8,128)(2,1)S(1)}, u32[]{:S(2)}, u32[]{:S(2)}) async-start(bf16[4,2,8,768]{3,2,1,0:T(8,128)(2,1)} %broadcast_in_dim.102), calls=%async_computation.1 | async-start | bytes 196608 | tf_op jit(solution)/shard_map/all_to_all | solution.py:14
  59.7 0.1 broadcast_compare_fusion
  59.7 7.0 %all-to-all-done.1 = bf16[4,2,8,768]{3,2,1,0:T(8,128)(2,1)S(1)} async-done(((bf16[4,2,8,768]{3,2,1,0:T(8,128)(2,1)}), bf16[4,2,8,768]{3,2,1,0:T(8,128)(2,1)S(1)}, u32[]{:S(2)}, u32[]{:S(2)}) %all-to-all-start.1) | async-done | bytes 98336 | tf_op jit(solution)/shard_map/all_to_all | solution.py:14
  66.8 1.1 fusion.20
  67.9 5.9 %all-gather.2.cloned.1.call-done = bf16[3,1024,768]{2,1,0:T(8,128)(2,1)} async-done(((bf16[3,256,768]{2,1,0:T(8,128)(2,1)}), bf16[3,1024,768]{2,1,0:T(8,128)(2,1)}) %all-gather.2.cloned.1.call-update) | async-done | bytes 4718608 | tf_op jit(solution)/shard_map/all_gather | solution.py:58
  73.7 4.2 %fusion.3 = bf16[3,256,768]{2,1,0:T(8,128)(2,1)S(1)} fusion(bf16[3,1024,768]{2,1,0:T(8,128)(2,1)} %all-gather.2.cloned.1.call-done, bf16[3,256,1024]{2,1,0:T(8,128)(2,1)} %param.11, pred[3,1024]{1,0:T(4,128)(4,1)S(1)} %iota_compare_fusion), kind=kOutput, calls=%fused_computation.5 | convolution fusion | flops 1209335808 | bytes 7474176 | tf_op jit(solution)/shard_map/sfg,sgn->sfn/dot_general | solution.py:61
  78.0 0.5 fusion.13
  78.5 0.0 copy-done.3
  78.5 0.0 copy-start.5
  78.5 0.4 fusion.9
  78.9 0.1 copy-done.2
  79.1 0.7 pad_maximum_fusion
  79.8 3.4 %all-to-all-start.2 = ((bf16[8,2,8,768]{3,2,1,0:T(8,128)(2,1)}), bf16[8,2,8,768]{3,2,1,0:T(8,128)(2,1)S(1)}, u32[]{:S(2)}, u32[]{:S(2)}) async-start(bf16[8,2,8,768]{3,2,1,0:T(8,128)(2,1)} %bitcast.20), calls=%async_computation.2 | async-start | bytes 393216 | tf_op jit(solution)/shard_map/all_to_all | solution.py:105
  83.2 6.2 %all-to-all-done.2 = bf16[8,2,8,768]{3,2,1,0:T(8,128)(2,1)S(1)} async-done(((bf16[8,2,8,768]{3,2,1,0:T(8,128)(2,1)}), bf16[8,2,8,768]{3,2,1,0:T(8,128)(2,1)S(1)}, u32[]{:S(2)}, u32[]{:S(2)}) %all-to-all-start.2) | async-done | bytes 196640 | tf_op jit(solution)/shard_map/all_to_all | solution.py:105
  89.6 1.3 add_convert_fusion
  90.8 13.4 %all-to-all-start.3 = ((bf16[64,8,768]{2,1,0:T(8,128)(2,1)}), bf16[64,8,768]{2,1,0:T(8,128)(2,1)S(1)}, u32[]{:S(2)}, u32[]{:S(2)}) async-start(bf16[64,8,768]{2,1,0:T(8,128)(2,1)} %add_convert_fusion), calls=%async_computation.3 | async-start | bytes 1572864 | tf_op jit(solution)/shard_map/all_to_all | solution.py:120
  104.2 0.2 rev.3
  104.6 23.9 %all-to-all-done.3 = bf16[64,8,768]{2,1,0:T(8,128)(2,1)S(1)} async-done(((bf16[64,8,768]{2,1,0:T(8,128)(2,1)}), bf16[64,8,768]{2,1,0:T(8,128)(2,1)S(1)}, u32[]{:S(2)}, u32[]{:S(2)}) %all-to-all-start.3) | async-done | bytes 786464 | tf_op jit(solution)/shard_map/all_to_all | solution.py:120
  128.5 0.1 convert_reduce_fusion
  128.6 0.7 fusion.24
  (39 shorter events, 0.3 us)
Async XLA Ops:
  7.2 59.6 %copy-start = (bf16[3,192,768]{2,1,0:T(8,128)(2,1)S(1)}, bf16[3,192,768]{2,1,0:T(8,128)(2,1)}, u32[]{:S(2)}) copy-start(bf16[3,192,768]{2,1,0:T(8,128)(2,1)} %param.13) | copy-start | bytes 2654212
  7.2 19.0 %copy-start.10 = (s32[3,1]{0,1:T(1,128)S(1)}, s32[3,1]{0,1:T(1,128)}, u32[]{:S(2)}) copy-start(s32[3,1]{0,1:T(1,128)} %param.10) | copy-start | bytes 40
  7.2 21.5 %copy-start.9 = (s32[3]{0:T(128)S(1)}, s32[3]{0:T(128)}, u32[]{:S(2)}) copy-start(s32[3]{0:T(128)} %param.9) | copy-start | bytes 40
  7.2 66.5 %all-gather.2.cloned.1.call-start = ((), (), s32[]{:S(2)}) async-start(), calls=%async_computation.4 | async-start | bytes 5898240 | tf_op jit(solution)/shard_map/all_gather | solution.py:58
  9.6 40.6 %all-to-all-start = ((bf16[64,8,768]{2,1,0:T(8,128)(2,1)}), bf16[64,8,768]{2,1,0:T(8,128)(2,1)S(1)}, u32[]{:S(2)}, u32[]{:S(2)}) async-start(bf16[64,8,768]{2,1,0:T(8,128)(2,1)} %broadcast_in_dim.101), calls=%async_computation | async-start | bytes 1572864 | tf_op jit(solution)/shard_map/all_to_all | solution.py:14
  26.8 3.1 %collective-permute-start = (s32[1]{0:T(128)}, s32[1]{0:T(128)}, u32[]{:S(2)}, u32[]{:S(2)}) collective-permute-start(s32[1]{0:T(128)} %bitcast.3), channel_id=1, source_target_pairs={{0,4},{4,0},{1,5},{5,1},{2,6},{6,2},{3,7},{7,3},{8,12},{12,8},{9,1... | collective-permute-start | bytes 20 | tf_op jit(solution)/shard_map/ppermute | solution.py:69
  50.1 4.6 %collective-permute-start.1 = (bf16[8,768]{1,0:T(8,128)(2,1)S(1)}, bf16[8,768]{1,0:T(8,128)(2,1)S(1)}, u32[]{:S(2)}, u32[]{:S(2)}) collective-permute-start(bf16[8,768]{1,0:T(8,128)(2,1)S(1)} %get-tuple-element.4), channel_id=1, source_target_pairs={{0,4},{4,0},{1,5},{5,1},{2,6},{6,2},{3,7},{7,3},{8,12},{12,8},{9,1... | collective-permute-start | bytes 36872 | tf_op jit(solution)/shard_map/ppermute | solution.py:71
  55.4 11.4 %all-to-all-start.1 = ((bf16[4,2,8,768]{3,2,1,0:T(8,128)(2,1)}), bf16[4,2,8,768]{3,2,1,0:T(8,128)(2,1)S(1)}, u32[]{:S(2)}, u32[]{:S(2)}) async-start(bf16[4,2,8,768]{3,2,1,0:T(8,128)(2,1)} %broadcast_in_dim.102), calls=%async_computation.1 | async-start | bytes 196608 | tf_op jit(solution)/shard_map/all_to_all | solution.py:14
  67.9 10.6 %copy-start.1 = (bf16[3,256,768]{2,1,0:T(8,128)(2,1)S(1)}, bf16[3,256,768]{2,1,0:T(8,128)(2,1)}, u32[]{:S(2)}) copy-start(bf16[3,256,768]{2,1,0:T(8,128)(2,1)} %param.12) | copy-start | bytes 3538948
  73.7 4.8 %copy-start.3 = (f32[3,32,768]{2,1,0:T(8,128)S(1)}, f32[3,32,768]{2,1,0:T(8,128)}, u32[]{:S(2)}) copy-start(f32[3,32,768]{2,1,0:T(8,128)} %fusion.20) | copy-start | bytes 884740
  78.0 1.0 copy-start.2
  78.5 1.3 copy-start.5
  79.8 9.7 %all-to-all-start.2 = ((bf16[8,2,8,768]{3,2,1,0:T(8,128)(2,1)}), bf16[8,2,8,768]{3,2,1,0:T(8,128)(2,1)S(1)}, u32[]{:S(2)}, u32[]{:S(2)}) async-start(bf16[8,2,8,768]{3,2,1,0:T(8,128)(2,1)} %bitcast.20), calls=%async_computation.2 | async-start | bytes 393216 | tf_op jit(solution)/shard_map/all_to_all | solution.py:105
  83.2 21.0 %copy-start.4 = (bf16[1,8,768]{2,1,0:T(8,128)(2,1)S(1)}, bf16[1,8,768]{2,1,0:T(8,128)(2,1)}, u32[]{:S(2)}) copy-start(bf16[1,8,768]{2,1,0:T(8,128)(2,1)} %param.14) | copy-start | bytes 36868
  89.5 15.0 %copy-start.7 = (f32[1,768]{1,0:T(1,128)S(1)}, f32[1,768]{1,0:T(1,128)}, u32[]{:S(2)}) copy-start(f32[1,768]{1,0:T(1,128)} %param.17) | copy-start | bytes 9220
  89.5 15.0 %copy-start.8 = (f32[1,768]{1,0:T(1,128)S(1)}, f32[1,768]{1,0:T(1,128)}, u32[]{:S(2)}) copy-start(f32[1,768]{1,0:T(1,128)} %param.16) | copy-start | bytes 9220
  89.6 39.0 %copy-start.6 = (f32[1,8,768]{2,1,0:T(8,128)S(1)}, f32[1,8,768]{2,1,0:T(8,128)}, u32[]{:S(2)}) copy-start(f32[1,8,768]{2,1,0:T(8,128)} %param.15) | copy-start | bytes 73732
  90.8 37.6 %all-to-all-start.3 = ((bf16[64,8,768]{2,1,0:T(8,128)(2,1)}), bf16[64,8,768]{2,1,0:T(8,128)(2,1)S(1)}, u32[]{:S(2)}, u32[]{:S(2)}) async-start(bf16[64,8,768]{2,1,0:T(8,128)(2,1)} %add_convert_fusion), calls=%async_computation.3 | async-start | bytes 1572864 | tf_op jit(solution)/shard_map/all_to_all | solution.py:120
Sparse Core Ops, SparseCore 0:
  10.1 63.5 all-gather.1

commit v10 on v9

--- a/solution.py
+++ b/solution.py
@@ -80,7 +80,15 @@
     )
     own_pair = collect(picked, "harm", 1)
     own_disp = jnp.stack([own_pair[0], own_pair[0], own_pair[1]])
-    inner = -jnp.einsum("sfn,shn->shf", modes, own_disp, preferred_element_type=jnp.float32)
+    whole_y = jnp.einsum("shn,sgn->shg", own_disp, piece, preferred_element_type=jnp.float32)
+    whole_y = jnp.where(live_cols[:, None, :], whole_y, jnp.float32(0.0))
+    inner = -jnp.einsum(
+        "shg,sfg->shf",
+        whole_y,
+        front_inverse.astype(jnp.float32),
+        precision=lax.Precision.HIGHEST,
+        preferred_element_type=jnp.float32,
+    )
     interior = jnp.where(live_rows[:, None, :], inner, jnp.float32(0.0)).astype(jnp.bfloat16)
     disp_cols = lax.dynamic_slice_in_dim(own_disp, harm_idx * width_q, width_q, 2)
     contrib = jnp.einsum("shf,sfn->shn", interior, masked, preferred_element_type=jnp.float32)

time: 137 us -> 137 us (level)
  matrix products: 6.18 us -> 10.7 us
  waiting for transfers between devices: 62.5 us -> 58.7 us
    dot_general x1 -> x2, matrix products: 0.47 us -> 5.26 us  [the longest x1 3.8 us: body(): jnp.einsum('shn,sgn->shg', own_disp, piece, preferred_element_type=jnp.fl...]
    all_to_all x1, waiting for transfers between devices: 23.9 us -> 19.1 us  [body(): lax.all_to_all(dense.astype(jnp.bfloat16), PLANE, split_axis=0, concat_ax...]
  transfers between devices with their start and end apart: 7 -> 7, of which waited for: 6 -> 6; matrix products, arithmetic and copies ran while one was open for 3% -> 6% of each run, Pallas kernels for 0% -> 0%
where the time goes in v10:
time: 137 us
  waiting for transfers between devices  58.7 us (43%)
  starting transfers between devices  41.5 us (30%)
  between operations  19.2 us (14%)
  matrix products  10.7 us (8%)
  local copies, waits for them, and re-layouts  3.22 us (2%)
  other arithmetic  3.15 us (2%)
    all_to_all x2, waiting for transfers between devices, copy_for_each(): lax.all_to_all(jnp.broadcast_to(x[None], (length, *x.shape)), axis, 0, 0,...  24.9 us
    all_to_all x2, starting transfers between devices, copy_for_each(): lax.all_to_all(jnp.broadcast_to(x[None], (length, *x.shape)), axis, 0, 0,...  20.9 us
    all_to_all x1, waiting for transfers between devices, body(): lax.all_to_all(dense.astype(jnp.bfloat16), PLANE, split_axis=0, concat_ax...  19.1 us
    all_to_all x1, starting transfers between devices, body(): lax.all_to_all(dense.astype(jnp.bfloat16), PLANE, split_axis=0, concat_ax...  13.4 us
    all_gather x1, waiting for transfers between devices, body(): piece = lax.all_gather(coupling, 'harm', axis=1, tiled=True)  6.59 us
    all_to_all x1, waiting for transfers between devices, body(): lax.all_to_all(send.reshape(2 * nharm, 2, rows_q, width).astype(jnp.bfloa...  6.23 us
    dot_general x1, matrix products, body(): jnp.einsum('sfg,sgn->sfn', front_live, piece, preferred_element_type=jnp....  4.74 us
    dot_general x1, matrix products, body(): jnp.einsum('shn,sgn->shg', own_disp, piece, preferred_element_type=jnp.fl...  3.8 us
  transfers between devices with their start and end apart: 7, of which 6 were waited for; matrix products, arithmetic and copies ran while one was open for 6% of the time, Pallas kernels for 0%

profile of v10, /device:TPU:8, one launch (start us, length us, event | category | flops | bytes accessed | tf_op | source)
XLA Modules:
  0.0 136.6 jit_solution(12480766603063895003)
XLA Ops:
  7.2 0.0 copy-start
  7.2 0.0 all-gather.2.cloned.1.call-start
  7.2 0.7 all-gather.2.cloned.1.call-update
  7.9 1.6 %broadcast_in_dim.115 = bf16[64,8,768]{2,1,0:T(8,128)(2,1)} broadcast(bf16[8,768]{1,0:T(8,128)(2,1)} %bitcast.60), dimensions={1,2} | broadcast | bytes 798720 | tf_op jit(solution)/shard_map/broadcast_in_dim | solution.py:14
  9.6 16.6 %all-to-all-start = ((bf16[64,8,768]{2,1,0:T(8,128)(2,1)}), bf16[64,8,768]{2,1,0:T(8,128)(2,1)S(1)}, u32[]{:S(2)}, u32[]{:S(2)}) async-start(bf16[64,8,768]{2,1,0:T(8,128)(2,1)} %broadcast_in_dim.115), calls=%async_computation | async-start | bytes 1572864 | tf_op jit(solution)/shard_map/all_to_all | solution.py:14
  26.2 0.6 slice.46
  26.8 1.9 %collective-permute-start = (s32[1]{0:T(128)}, s32[1]{0:T(128)}, u32[]{:S(2)}, u32[]{:S(2)}) collective-permute-start(s32[1]{0:T(128)} %bitcast.3), channel_id=1, source_target_pairs={{0,4},{4,0},{1,5},{5,1},{2,6},{6,2},{3,7},{7,3},{8,12},{12,8},{9,1... | collective-permute-start | bytes 20 | tf_op jit(solution)/shard_map/ppermute | solution.py:69
  28.7 0.1 iota_compare_fusion
  28.8 1.2 collective-permute-done
  32.2 17.9 %all-to-all-done = bf16[64,8,768]{2,1,0:T(8,128)(2,1)S(1)} async-done(((bf16[64,8,768]{2,1,0:T(8,128)(2,1)}), bf16[64,8,768]{2,1,0:T(8,128)(2,1)S(1)}, u32[]{:S(2)}, u32[]{:S(2)}) %all-to-all-start) | async-done | bytes 786464 | tf_op jit(solution)/shard_map/all_to_all | solution.py:14
  50.1 1.9 %collective-permute-start.1 = (bf16[8,768]{1,0:T(8,128)(2,1)S(1)}, bf16[8,768]{1,0:T(8,128)(2,1)S(1)}, u32[]{:S(2)}, u32[]{:S(2)}) collective-permute-start(bf16[8,768]{1,0:T(8,128)(2,1)S(1)} %get-tuple-element.4), channel_id=1, source_target_pairs={{0,4},{4,0},{1,5},{5,1},{2,6},{6,2},{3,7},{7,3},{8,12},{12,8},{9,1... | collective-permute-start | bytes 36872 | tf_op jit(solution)/shard_map/ppermute | solution.py:71
  54.7 0.6 broadcast_in_dim.116
  55.4 4.3 %all-to-all-start.1 = ((bf16[4,2,8,768]{3,2,1,0:T(8,128)(2,1)}), bf16[4,2,8,768]{3,2,1,0:T(8,128)(2,1)S(1)}, u32[]{:S(2)}, u32[]{:S(2)}) async-start(bf16[4,2,8,768]{3,2,1,0:T(8,128)(2,1)} %broadcast_in_dim.116), calls=%async_computation.1 | async-start | bytes 196608 | tf_op jit(solution)/shard_map/all_to_all | solution.py:14
  59.7 0.1 broadcast_compare_fusion
  59.7 7.0 %all-to-all-done.1 = bf16[4,2,8,768]{3,2,1,0:T(8,128)(2,1)S(1)} async-done(((bf16[4,2,8,768]{3,2,1,0:T(8,128)(2,1)}), bf16[4,2,8,768]{3,2,1,0:T(8,128)(2,1)S(1)}, u32[]{:S(2)}, u32[]{:S(2)}) %all-to-all-start.1) | async-done | bytes 98336 | tf_op jit(solution)/shard_map/all_to_all | solution.py:14
  66.8 0.3 fusion.20
  67.2 6.6 %all-gather.2.cloned.1.call-done = bf16[3,1024,768]{2,1,0:T(8,128)(2,1)} async-done(((bf16[3,256,768]{2,1,0:T(8,128)(2,1)}), bf16[3,1024,768]{2,1,0:T(8,128)(2,1)}) %all-gather.2.cloned.1.call-update) | async-done | bytes 4718608 | tf_op jit(solution)/shard_map/all_gather | solution.py:58
  73.8 3.8 %convolution_select_fusion = f32[3,32,1024]{2,1,0:T(8,128)S(1)} fusion(bf16[3,1024,768]{2,1,0:T(8,128)(2,1)} %all-gather.2.cloned.1.call-done, pred[3,1024]{1,0:T(4,128)(4,1)S(1)} %iota_compare_fusion, bf16[1,32,768]{2,1,0:T(8,128)(2,1)S(1)} %get-tuple-element.13, bf16[1,32,768]{2,1,0:T(8,128)(2,1)S(1)} %get-tuple-element.12), kind=kOutput, calls=%fused_computation.6 | convolution fusion | flops 151240704 | bytes 5213184 | tf_op jit(solution)/shard_map/shn,sgn->shg/dot_general | solution.py:83
  77.6 0.0 copy-done.1
  77.6 1.5 %fusion.13 = bf16[3,32,256]{2,1,0:T(8,128)(2,1)S(1)} fusion(f32[3,32,1024]{2,1,0:T(8,128)S(1)} %convolution_select_fusion, bf16[3,256,1024]{2,1,0:T(8,128)(2,1)S(1)} %copy-done.1, pred[3,256]{1,0:T(4,128)(4,1)S(1)} %broadcast_compare_fusion), kind=kOutput, calls=%fused_computation.13 | convolution fusion | flops 302063616 | bytes 2016000 | tf_op jit(solution)/shard_map/shg,sfg->shf/dot_general | solution.py:85
  79.1 0.0 copy-start.4
  79.1 0.4 fusion.9
  79.6 0.7 pad_maximum_fusion
  80.3 3.4 %all-to-all-start.2 = ((bf16[8,2,8,768]{3,2,1,0:T(8,128)(2,1)}), bf16[8,2,8,768]{3,2,1,0:T(8,128)(2,1)S(1)}, u32[]{:S(2)}, u32[]{:S(2)}) async-start(bf16[8,2,8,768]{3,2,1,0:T(8,128)(2,1)} %bitcast.20), calls=%async_computation.2 | async-start | bytes 393216 | tf_op jit(solution)/shard_map/all_to_all | solution.py:113
  83.7 6.2 %all-to-all-done.2 = bf16[8,2,8,768]{3,2,1,0:T(8,128)(2,1)S(1)} async-done(((bf16[8,2,8,768]{3,2,1,0:T(8,128)(2,1)}), bf16[8,2,8,768]{3,2,1,0:T(8,128)(2,1)S(1)}, u32[]{:S(2)}, u32[]{:S(2)}) %all-to-all-start.2) | async-done | bytes 196640 | tf_op jit(solution)/shard_map/all_to_all | solution.py:113
  90.0 1.3 add_convert_fusion
  91.3 13.4 %all-to-all-start.3 = ((bf16[64,8,768]{2,1,0:T(8,128)(2,1)}), bf16[64,8,768]{2,1,0:T(8,128)(2,1)S(1)}, u32[]{:S(2)}, u32[]{:S(2)}) async-start(bf16[64,8,768]{2,1,0:T(8,128)(2,1)} %add_convert_fusion), calls=%async_computation.3 | async-start | bytes 1572864 | tf_op jit(solution)/shard_map/all_to_all | solution.py:128
  104.7 0.2 rev.3
  105.1 4.7 %fusion.3 = bf16[3,256,768]{2,1,0:T(8,128)(2,1)} fusion(bf16[3,1024,768]{2,1,0:T(8,128)(2,1)} %all-gather.2.cloned.1.call-done, bf16[3,256,1024]{2,1,0:T(8,128)(2,1)S(1)} %copy-done.1, pred[3,1024]{1,0:T(4,128)(4,1)S(1)} %iota_compare_fusion), kind=kOutput, calls=%fused_computation.5 | convolution fusion | flops 1209335808 | bytes 7474176 | tf_op jit(solution)/shard_map/sfg,sgn->sfn/dot_general | solution.py:61
  109.8 19.1 %all-to-all-done.3 = bf16[64,8,768]{2,1,0:T(8,128)(2,1)S(1)} async-done(((bf16[64,8,768]{2,1,0:T(8,128)(2,1)}), bf16[64,8,768]{2,1,0:T(8,128)(2,1)S(1)}, u32[]{:S(2)}, u32[]{:S(2)}) %all-to-all-start.3) | async-done | bytes 786464 | tf_op jit(solution)/shard_map/all_to_all | solution.py:128
  128.9 0.1 convert_reduce_fusion
  129.1 0.7 fusion.24
  (38 shorter events, 0.3 us)
Async XLA Ops:
  7.2 59.6 %copy-start = (bf16[3,192,768]{2,1,0:T(8,128)(2,1)S(1)}, bf16[3,192,768]{2,1,0:T(8,128)(2,1)}, u32[]{:S(2)}) copy-start(bf16[3,192,768]{2,1,0:T(8,128)(2,1)} %param.13) | copy-start | bytes 2654212
  7.2 19.0 %copy-start.9 = (s32[3,1]{0,1:T(1,128)S(1)}, s32[3,1]{0,1:T(1,128)}, u32[]{:S(2)}) copy-start(s32[3,1]{0,1:T(1,128)} %param.10) | copy-start | bytes 40
  7.2 21.5 %copy-start.8 = (s32[3]{0:T(128)S(1)}, s32[3]{0:T(128)}, u32[]{:S(2)}) copy-start(s32[3]{0:T(128)} %param.9) | copy-start | bytes 40
  7.2 66.6 %all-gather.2.cloned.1.call-start = ((), (), s32[]{:S(2)}) async-start(), calls=%async_computation.4 | async-start | bytes 5898240 | tf_op jit(solution)/shard_map/all_gather | solution.py:58
  9.6 40.6 %all-to-all-start = ((bf16[64,8,768]{2,1,0:T(8,128)(2,1)}), bf16[64,8,768]{2,1,0:T(8,128)(2,1)S(1)}, u32[]{:S(2)}, u32[]{:S(2)}) async-start(bf16[64,8,768]{2,1,0:T(8,128)(2,1)} %broadcast_in_dim.115), calls=%async_computation | async-start | bytes 1572864 | tf_op jit(solution)/shard_map/all_to_all | solution.py:14
  26.8 3.3 %collective-permute-start = (s32[1]{0:T(128)}, s32[1]{0:T(128)}, u32[]{:S(2)}, u32[]{:S(2)}) collective-permute-start(s32[1]{0:T(128)} %bitcast.3), channel_id=1, source_target_pairs={{0,4},{4,0},{1,5},{5,1},{2,6},{6,2},{3,7},{7,3},{8,12},{12,8},{9,1... | collective-permute-start | bytes 20 | tf_op jit(solution)/shard_map/ppermute | solution.py:69
  50.1 4.6 %collective-permute-start.1 = (bf16[8,768]{1,0:T(8,128)(2,1)S(1)}, bf16[8,768]{1,0:T(8,128)(2,1)S(1)}, u32[]{:S(2)}, u32[]{:S(2)}) collective-permute-start(bf16[8,768]{1,0:T(8,128)(2,1)S(1)} %get-tuple-element.4), channel_id=1, source_target_pairs={{0,4},{4,0},{1,5},{5,1},{2,6},{6,2},{3,7},{7,3},{8,12},{12,8},{9,1... | collective-permute-start | bytes 36872 | tf_op jit(solution)/shard_map/ppermute | solution.py:71
  55.4 11.4 %all-to-all-start.1 = ((bf16[4,2,8,768]{3,2,1,0:T(8,128)(2,1)}), bf16[4,2,8,768]{3,2,1,0:T(8,128)(2,1)S(1)}, u32[]{:S(2)}, u32[]{:S(2)}) async-start(bf16[4,2,8,768]{3,2,1,0:T(8,128)(2,1)} %broadcast_in_dim.116), calls=%async_computation.1 | async-start | bytes 196608 | tf_op jit(solution)/shard_map/all_to_all | solution.py:14
  67.2 10.4 %copy-start.1 = (bf16[3,256,1024]{2,1,0:T(8,128)(2,1)S(1)}, bf16[3,256,1024]{2,1,0:T(8,128)(2,1)}, u32[]{:S(2)}) copy-start(bf16[3,256,1024]{2,1,0:T(8,128)(2,1)} %param.11) | copy-start | bytes 4718596
  77.6 1.5 %copy-start.2 = (bf16[3,256,768]{2,1,0:T(8,128)(2,1)S(1)}, bf16[3,256,768]{2,1,0:T(8,128)(2,1)}, u32[]{:S(2)}) copy-start(bf16[3,256,768]{2,1,0:T(8,128)(2,1)} %param.12) | copy-start | bytes 3538948
  79.1 1.2 copy-start.4
  80.3 9.7 %all-to-all-start.2 = ((bf16[8,2,8,768]{3,2,1,0:T(8,128)(2,1)}), bf16[8,2,8,768]{3,2,1,0:T(8,128)(2,1)S(1)}, u32[]{:S(2)}, u32[]{:S(2)}) async-start(bf16[8,2,8,768]{3,2,1,0:T(8,128)(2,1)} %bitcast.20), calls=%async_computation.2 | async-start | bytes 393216 | tf_op jit(solution)/shard_map/all_to_all | solution.py:113
  83.7 21.0 %copy-start.3 = (bf16[1,8,768]{2,1,0:T(8,128)(2,1)S(1)}, bf16[1,8,768]{2,1,0:T(8,128)(2,1)}, u32[]{:S(2)}) copy-start(bf16[1,8,768]{2,1,0:T(8,128)(2,1)} %param.14) | copy-start | bytes 36868
  90.0 15.0 %copy-start.6 = (f32[1,768]{1,0:T(1,128)S(1)}, f32[1,768]{1,0:T(1,128)}, u32[]{:S(2)}) copy-start(f32[1,768]{1,0:T(1,128)} %param.16) | copy-start | bytes 9220
  90.0 15.0 %copy-start.7 = (f32[1,768]{1,0:T(1,128)S(1)}, f32[1,768]{1,0:T(1,128)}, u32[]{:S(2)}) copy-start(f32[1,768]{1,0:T(1,128)} %param.17) | copy-start | bytes 9220
  91.3 37.6 %all-to-all-start.3 = ((bf16[64,8,768]{2,1,0:T(8,128)(2,1)}), bf16[64,8,768]{2,1,0:T(8,128)(2,1)S(1)}, u32[]{:S(2)}, u32[]{:S(2)}) async-start(bf16[64,8,768]{2,1,0:T(8,128)(2,1)} %add_convert_fusion), calls=%async_computation.3 | async-start | bytes 1572864 | tf_op jit(solution)/shard_map/all_to_all | solution.py:128
  105.1 24.0 %copy-start.5 = (f32[1,8,768]{2,1,0:T(8,128)S(1)}, f32[1,8,768]{2,1,0:T(8,128)}, u32[]{:S(2)}) copy-start(f32[1,8,768]{2,1,0:T(8,128)} %param.15) | copy-start | bytes 73732
Sparse Core Ops, SparseCore 0:
  10.1 63.5 all-gather.1

commit v11 on v10

--- a/solution.py
+++ b/solution.py
@@ -86,7 +86,7 @@
         "shg,sfg->shf",
         whole_y,
         front_inverse.astype(jnp.float32),
-        precision=lax.Precision.HIGHEST,
+        precision=lax.Precision.HIGH,
         preferred_element_type=jnp.float32,
     )
     interior = jnp.where(live_rows[:, None, :], inner, jnp.float32(0.0)).astype(jnp.bfloat16)

time: 137 us -> 137 us (level)
  no operation moved by 1% of the time
where the time goes in v11:
time: 137 us; the launch traced here: 136 us
  waiting for transfers between devices  58.7 us (43%)
  starting transfers between devices  41.5 us (30%)
  between operations  19.2 us (14%)
  matrix products  10.3 us (8%)
  local copies, waits for them, and re-layouts  3.45 us (3%)
  other arithmetic  3.15 us (2%)
    all_to_all x2, waiting for transfers between devices, copy_for_each(): lax.all_to_all(jnp.broadcast_to(x[None], (length, *x.shape)), axis, 0, 0,...  24.9 us
    all_to_all x2, starting transfers between devices, copy_for_each(): lax.all_to_all(jnp.broadcast_to(x[None], (length, *x.shape)), axis, 0, 0,...  20.9 us
    all_to_all x1, waiting for transfers between devices, body(): lax.all_to_all(dense.astype(jnp.bfloat16), PLANE, split_axis=0, concat_ax...  19.1 us
    all_to_all x1, starting transfers between devices, body(): lax.all_to_all(dense.astype(jnp.bfloat16), PLANE, split_axis=0, concat_ax...  13.4 us
    all_gather x1, waiting for transfers between devices, body(): piece = lax.all_gather(coupling, 'harm', axis=1, tiled=True)  6.59 us
    all_to_all x1, waiting for transfers between devices, body(): lax.all_to_all(send.reshape(2 * nharm, 2, rows_q, width).astype(jnp.bfloa...  6.23 us
    dot_general x1, matrix products, body(): jnp.einsum('sfg,sgn->sfn', front_live, piece, preferred_element_type=jnp....  4.74 us
    dot_general x1, matrix products, body(): jnp.einsum('shn,sgn->shg', own_disp, piece, preferred_element_type=jnp.fl...  3.8 us
  transfers between devices with their start and end apart: 7, of which 6 were waited for; matrix products, arithmetic and copies ran while one was open for 6% of the time, Pallas kernels for 0%

profile of v11, /device:TPU:8, one launch (start us, length us, event | category | flops | bytes accessed | tf_op | source)
XLA Modules:
  0.0 136.4 jit_solution(11182344621369115040)
XLA Ops:
  7.2 0.0 copy-start
  7.2 0.0 all-gather.2.cloned.1.call-start
  7.2 0.7 all-gather.2.cloned.1.call-update
  7.9 1.6 %broadcast_in_dim.115 = bf16[64,8,768]{2,1,0:T(8,128)(2,1)} broadcast(bf16[8,768]{1,0:T(8,128)(2,1)} %bitcast.60), dimensions={1,2} | broadcast | bytes 798720 | tf_op jit(solution)/shard_map/broadcast_in_dim | solution.py:14
  9.6 16.6 %all-to-all-start = ((bf16[64,8,768]{2,1,0:T(8,128)(2,1)}), bf16[64,8,768]{2,1,0:T(8,128)(2,1)S(1)}, u32[]{:S(2)}, u32[]{:S(2)}) async-start(bf16[64,8,768]{2,1,0:T(8,128)(2,1)} %broadcast_in_dim.115), calls=%async_computation | async-start | bytes 1572864 | tf_op jit(solution)/shard_map/all_to_all | solution.py:14
  26.2 0.6 slice.46
  26.8 1.9 %collective-permute-start = (s32[1]{0:T(128)}, s32[1]{0:T(128)}, u32[]{:S(2)}, u32[]{:S(2)}) collective-permute-start(s32[1]{0:T(128)} %bitcast.3), channel_id=1, source_target_pairs={{0,4},{4,0},{1,5},{5,1},{2,6},{6,2},{3,7},{7,3},{8,12},{12,8},{9,1... | collective-permute-start | bytes 20 | tf_op jit(solution)/shard_map/ppermute | solution.py:69
  28.7 0.1 iota_compare_fusion
  28.8 1.2 collective-permute-done
  32.2 17.9 %all-to-all-done = bf16[64,8,768]{2,1,0:T(8,128)(2,1)S(1)} async-done(((bf16[64,8,768]{2,1,0:T(8,128)(2,1)}), bf16[64,8,768]{2,1,0:T(8,128)(2,1)S(1)}, u32[]{:S(2)}, u32[]{:S(2)}) %all-to-all-start) | async-done | bytes 786464 | tf_op jit(solution)/shard_map/all_to_all | solution.py:14
  50.1 1.9 %collective-permute-start.1 = (bf16[8,768]{1,0:T(8,128)(2,1)S(1)}, bf16[8,768]{1,0:T(8,128)(2,1)S(1)}, u32[]{:S(2)}, u32[]{:S(2)}) collective-permute-start(bf16[8,768]{1,0:T(8,128)(2,1)S(1)} %get-tuple-element.4), channel_id=1, source_target_pairs={{0,4},{4,0},{1,5},{5,1},{2,6},{6,2},{3,7},{7,3},{8,12},{12,8},{9,1... | collective-permute-start | bytes 36872 | tf_op jit(solution)/shard_map/ppermute | solution.py:71
  54.7 0.6 broadcast_in_dim.116
  55.4 4.3 %all-to-all-start.1 = ((bf16[4,2,8,768]{3,2,1,0:T(8,128)(2,1)}), bf16[4,2,8,768]{3,2,1,0:T(8,128)(2,1)S(1)}, u32[]{:S(2)}, u32[]{:S(2)}) async-start(bf16[4,2,8,768]{3,2,1,0:T(8,128)(2,1)} %broadcast_in_dim.116), calls=%async_computation.1 | async-start | bytes 196608 | tf_op jit(solution)/shard_map/all_to_all | solution.py:14
  59.7 0.1 broadcast_compare_fusion
  59.7 7.0 %all-to-all-done.1 = bf16[4,2,8,768]{3,2,1,0:T(8,128)(2,1)S(1)} async-done(((bf16[4,2,8,768]{3,2,1,0:T(8,128)(2,1)}), bf16[4,2,8,768]{3,2,1,0:T(8,128)(2,1)S(1)}, u32[]{:S(2)}, u32[]{:S(2)}) %all-to-all-start.1) | async-done | bytes 98336 | tf_op jit(solution)/shard_map/all_to_all | solution.py:14
  66.8 0.3 fusion.20
  67.2 6.6 %all-gather.2.cloned.1.call-done = bf16[3,1024,768]{2,1,0:T(8,128)(2,1)} async-done(((bf16[3,256,768]{2,1,0:T(8,128)(2,1)}), bf16[3,1024,768]{2,1,0:T(8,128)(2,1)}) %all-gather.2.cloned.1.call-update) | async-done | bytes 4718608 | tf_op jit(solution)/shard_map/all_gather | solution.py:58
  73.8 3.8 %convolution_select_fusion = f32[3,32,1024]{2,1,0:T(8,128)S(1)} fusion(bf16[3,1024,768]{2,1,0:T(8,128)(2,1)} %all-gather.2.cloned.1.call-done, pred[3,1024]{1,0:T(4,128)(4,1)S(1)} %iota_compare_fusion, bf16[1,32,768]{2,1,0:T(8,128)(2,1)S(1)} %get-tuple-element.13, bf16[1,32,768]{2,1,0:T(8,128)(2,1)S(1)} %get-tuple-element.12), kind=kOutput, calls=%fused_computation.6 | convolution fusion | flops 151240704 | bytes 5213184 | tf_op jit(solution)/shard_map/shn,sgn->shg/dot_general | solution.py:83
  77.6 0.0 copy-done.1
  77.6 1.0 fusion.13
  78.6 0.2 copy-done.2
  78.9 0.4 fusion.9
  79.3 0.7 pad_maximum_fusion
  80.0 3.4 %all-to-all-start.2 = ((bf16[8,2,8,768]{3,2,1,0:T(8,128)(2,1)}), bf16[8,2,8,768]{3,2,1,0:T(8,128)(2,1)S(1)}, u32[]{:S(2)}, u32[]{:S(2)}) async-start(bf16[8,2,8,768]{3,2,1,0:T(8,128)(2,1)} %bitcast.20), calls=%async_computation.2 | async-start | bytes 393216 | tf_op jit(solution)/shard_map/all_to_all | solution.py:113
  83.5 6.2 %all-to-all-done.2 = bf16[8,2,8,768]{3,2,1,0:T(8,128)(2,1)S(1)} async-done(((bf16[8,2,8,768]{3,2,1,0:T(8,128)(2,1)}), bf16[8,2,8,768]{3,2,1,0:T(8,128)(2,1)S(1)}, u32[]{:S(2)}, u32[]{:S(2)}) %all-to-all-start.2) | async-done | bytes 196640 | tf_op jit(solution)/shard_map/all_to_all | solution.py:113
  89.8 1.3 add_convert_fusion
  91.1 13.4 %all-to-all-start.3 = ((bf16[64,8,768]{2,1,0:T(8,128)(2,1)}), bf16[64,8,768]{2,1,0:T(8,128)(2,1)S(1)}, u32[]{:S(2)}, u32[]{:S(2)}) async-start(bf16[64,8,768]{2,1,0:T(8,128)(2,1)} %add_convert_fusion), calls=%async_computation.3 | async-start | bytes 1572864 | tf_op jit(solution)/shard_map/all_to_all | solution.py:128
  104.5 0.2 rev.3
  104.9 4.7 %fusion.3 = bf16[3,256,768]{2,1,0:T(8,128)(2,1)} fusion(bf16[3,1024,768]{2,1,0:T(8,128)(2,1)} %all-gather.2.cloned.1.call-done, bf16[3,256,1024]{2,1,0:T(8,128)(2,1)S(1)} %copy-done.1, pred[3,1024]{1,0:T(4,128)(4,1)S(1)} %iota_compare_fusion), kind=kOutput, calls=%fused_computation.5 | convolution fusion | flops 1209335808 | bytes 7474176 | tf_op jit(solution)/shard_map/sfg,sgn->sfn/dot_general | solution.py:61
  109.6 19.1 %all-to-all-done.3 = bf16[64,8,768]{2,1,0:T(8,128)(2,1)S(1)} async-done(((bf16[64,8,768]{2,1,0:T(8,128)(2,1)}), bf16[64,8,768]{2,1,0:T(8,128)(2,1)S(1)}, u32[]{:S(2)}, u32[]{:S(2)}) %all-to-all-start.3) | async-done | bytes 786464 | tf_op jit(solution)/shard_map/all_to_all | solution.py:128
  128.7 0.1 convert_reduce_fusion
  128.9 0.7 fusion.24
  (38 shorter events, 0.3 us)
Async XLA Ops:
  7.2 59.6 %copy-start = (bf16[3,192,768]{2,1,0:T(8,128)(2,1)S(1)}, bf16[3,192,768]{2,1,0:T(8,128)(2,1)}, u32[]{:S(2)}) copy-start(bf16[3,192,768]{2,1,0:T(8,128)(2,1)} %param.13) | copy-start | bytes 2654212
  7.2 19.0 %copy-start.9 = (s32[3,1]{0,1:T(1,128)S(1)}, s32[3,1]{0,1:T(1,128)}, u32[]{:S(2)}) copy-start(s32[3,1]{0,1:T(1,128)} %param.10) | copy-start | bytes 40
  7.2 21.5 %copy-start.8 = (s32[3]{0:T(128)S(1)}, s32[3]{0:T(128)}, u32[]{:S(2)}) copy-start(s32[3]{0:T(128)} %param.9) | copy-start | bytes 40
  7.2 66.6 %all-gather.2.cloned.1.call-start = ((), (), s32[]{:S(2)}) async-start(), calls=%async_computation.4 | async-start | bytes 5898240 | tf_op jit(solution)/shard_map/all_gather | solution.py:58
  9.6 40.6 %all-to-all-start = ((bf16[64,8,768]{2,1,0:T(8,128)(2,1)}), bf16[64,8,768]{2,1,0:T(8,128)(2,1)S(1)}, u32[]{:S(2)}, u32[]{:S(2)}) async-start(bf16[64,8,768]{2,1,0:T(8,128)(2,1)} %broadcast_in_dim.115), calls=%async_computation | async-start | bytes 1572864 | tf_op jit(solution)/shard_map/all_to_all | solution.py:14
  26.8 3.3 %collective-permute-start = (s32[1]{0:T(128)}, s32[1]{0:T(128)}, u32[]{:S(2)}, u32[]{:S(2)}) collective-permute-start(s32[1]{0:T(128)} %bitcast.3), channel_id=1, source_target_pairs={{0,4},{4,0},{1,5},{5,1},{2,6},{6,2},{3,7},{7,3},{8,12},{12,8},{9,1... | collective-permute-start | bytes 20 | tf_op jit(solution)/shard_map/ppermute | solution.py:69
  50.1 4.6 %collective-permute-start.1 = (bf16[8,768]{1,0:T(8,128)(2,1)S(1)}, bf16[8,768]{1,0:T(8,128)(2,1)S(1)}, u32[]{:S(2)}, u32[]{:S(2)}) collective-permute-start(bf16[8,768]{1,0:T(8,128)(2,1)S(1)} %get-tuple-element.4), channel_id=1, source_target_pairs={{0,4},{4,0},{1,5},{5,1},{2,6},{6,2},{3,7},{7,3},{8,12},{12,8},{9,1... | collective-permute-start | bytes 36872 | tf_op jit(solution)/shard_map/ppermute | solution.py:71
  55.4 11.4 %all-to-all-start.1 = ((bf16[4,2,8,768]{3,2,1,0:T(8,128)(2,1)}), bf16[4,2,8,768]{3,2,1,0:T(8,128)(2,1)S(1)}, u32[]{:S(2)}, u32[]{:S(2)}) async-start(bf16[4,2,8,768]{3,2,1,0:T(8,128)(2,1)} %broadcast_in_dim.116), calls=%async_computation.1 | async-start | bytes 196608 | tf_op jit(solution)/shard_map/all_to_all | solution.py:14
  67.2 10.4 %copy-start.1 = (bf16[3,256,1024]{2,1,0:T(8,128)(2,1)S(1)}, bf16[3,256,1024]{2,1,0:T(8,128)(2,1)}, u32[]{:S(2)}) copy-start(bf16[3,256,1024]{2,1,0:T(8,128)(2,1)} %param.11) | copy-start | bytes 4718596
  77.6 1.3 copy-start.2
  78.9 1.2 copy-start.4
  80.0 9.7 %all-to-all-start.2 = ((bf16[8,2,8,768]{3,2,1,0:T(8,128)(2,1)}), bf16[8,2,8,768]{3,2,1,0:T(8,128)(2,1)S(1)}, u32[]{:S(2)}, u32[]{:S(2)}) async-start(bf16[8,2,8,768]{3,2,1,0:T(8,128)(2,1)} %bitcast.20), calls=%async_computation.2 | async-start | bytes 393216 | tf_op jit(solution)/shard_map/all_to_all | solution.py:113
  83.5 21.0 %copy-start.3 = (bf16[1,8,768]{2,1,0:T(8,128)(2,1)S(1)}, bf16[1,8,768]{2,1,0:T(8,128)(2,1)}, u32[]{:S(2)}) copy-start(bf16[1,8,768]{2,1,0:T(8,128)(2,1)} %param.14) | copy-start | bytes 36868
  89.7 15.0 %copy-start.6 = (f32[1,768]{1,0:T(1,128)S(1)}, f32[1,768]{1,0:T(1,128)}, u32[]{:S(2)}) copy-start(f32[1,768]{1,0:T(1,128)} %param.16) | copy-start | bytes 9220
  89.8 15.0 %copy-start.7 = (f32[1,768]{1,0:T(1,128)S(1)}, f32[1,768]{1,0:T(1,128)}, u32[]{:S(2)}) copy-start(f32[1,768]{1,0:T(1,128)} %param.17) | copy-start | bytes 9220
  91.1 37.6 %all-to-all-start.3 = ((bf16[64,8,768]{2,1,0:T(8,128)(2,1)}), bf16[64,8,768]{2,1,0:T(8,128)(2,1)S(1)}, u32[]{:S(2)}, u32[]{:S(2)}) async-start(bf16[64,8,768]{2,1,0:T(8,128)(2,1)} %add_convert_fusion), calls=%async_computation.3 | async-start | bytes 1572864 | tf_op jit(solution)/shard_map/all_to_all | solution.py:128
  104.9 24.0 %copy-start.5 = (f32[1,8,768]{2,1,0:T(8,128)S(1)}, f32[1,8,768]{2,1,0:T(8,128)}, u32[]{:S(2)}) copy-start(f32[1,8,768]{2,1,0:T(8,128)} %param.15) | copy-start | bytes 73732
Sparse Core Ops, SparseCore 0:
  10.1 63.5 all-gather.1

commit v12 on v11

--- a/solution.py
+++ b/solution.py
@@ -83,11 +83,7 @@
     whole_y = jnp.einsum("shn,sgn->shg", own_disp, piece, preferred_element_type=jnp.float32)
     whole_y = jnp.where(live_cols[:, None, :], whole_y, jnp.float32(0.0))
     inner = -jnp.einsum(
-        "shg,sfg->shf",
-        whole_y,
-        front_inverse.astype(jnp.float32),
-        precision=lax.Precision.HIGH,
-        preferred_element_type=jnp.float32,
+        "shg,sfg->shf", whole_y.astype(jnp.bfloat16), front_inverse, preferred_element_type=jnp.float32
     )
     interior = jnp.where(live_rows[:, None, :], inner, jnp.float32(0.0)).astype(jnp.bfloat16)
     disp_cols = lax.dynamic_slice_in_dim(own_disp, harm_idx * width_q, width_q, 2)

time: 137 us -> 138 us (level)
    dot_general x2 -> x1, matrix products: 4.82 us -> 4.26 us  [body(): jnp.einsum('shg,sfg->shf', whole_y.astype(jnp.bfloat16), front_inverse, p...]
where the time goes in v12:
time: 138 us; the launch traced here: 137 us
  waiting for transfers between devices  58 us (42%)
  starting transfers between devices  41.6 us (30%)
  between operations  19.8 us (14%)
  matrix products  11 us (8%)
  local copies, waits for them, and re-layouts  3.2 us (2%)
  other arithmetic  3.15 us (2%)
    all_to_all x2, waiting for transfers between devices, copy_for_each(): lax.all_to_all(jnp.broadcast_to(x[None], (length, *x.shape)), axis, 0, 0,...  24.5 us
    all_to_all x2, starting transfers between devices, copy_for_each(): lax.all_to_all(jnp.broadcast_to(x[None], (length, *x.shape)), axis, 0, 0,...  21 us
    all_to_all x1, waiting for transfers between devices, body(): lax.all_to_all(dense.astype(jnp.bfloat16), PLANE, split_axis=0, concat_ax...  19.1 us
    all_to_all x1, starting transfers between devices, body(): lax.all_to_all(dense.astype(jnp.bfloat16), PLANE, split_axis=0, concat_ax...  13.4 us
    all_gather x1, waiting for transfers between devices, body(): piece = lax.all_gather(coupling, 'harm', axis=1, tiled=True)  6.44 us
    all_to_all x1, waiting for transfers between devices, body(): lax.all_to_all(send.reshape(2 * nharm, 2, rows_q, width).astype(jnp.bfloa...  6.21 us
    dot_general x1, matrix products, body(): jnp.einsum('sfg,sgn->sfn', front_live, piece, preferred_element_type=jnp....  4.74 us
    dot_general x1, matrix products, body(): jnp.einsum('shg,sfg->shf', whole_y.astype(jnp.bfloat16), front_inverse, p...  4.26 us
  transfers between devices with their start and end apart: 7, of which 6 were waited for; matrix products, arithmetic and copies ran while one was open for 6% of the time, Pallas kernels for 0%

profile of v12, /device:TPU:8, one launch (start us, length us, event | category | flops | bytes accessed | tf_op | source)
XLA Modules:
  0.0 136.8 jit_solution(8824792150131321024)
XLA Ops:
  7.2 0.0 copy-start
  7.2 0.0 all-gather.2.cloned.1.call-start
  7.2 0.7 all-gather.2.cloned.1.call-update
  7.9 1.6 %broadcast_in_dim.115 = bf16[64,8,768]{2,1,0:T(8,128)(2,1)} broadcast(bf16[8,768]{1,0:T(8,128)(2,1)} %bitcast.59), dimensions={1,2} | broadcast | bytes 798720 | tf_op jit(solution)/shard_map/broadcast_in_dim | solution.py:14
  9.6 16.7 %all-to-all-start = ((bf16[64,8,768]{2,1,0:T(8,128)(2,1)}), bf16[64,8,768]{2,1,0:T(8,128)(2,1)S(1)}, u32[]{:S(2)}, u32[]{:S(2)}) async-start(bf16[64,8,768]{2,1,0:T(8,128)(2,1)} %broadcast_in_dim.115), calls=%async_computation | async-start | bytes 1572864 | tf_op jit(solution)/shard_map/all_to_all | solution.py:14
  26.3 0.6 slice.46
  26.9 1.9 %collective-permute-start = (s32[1]{0:T(128)}, s32[1]{0:T(128)}, u32[]{:S(2)}, u32[]{:S(2)}) collective-permute-start(s32[1]{0:T(128)} %bitcast.3), channel_id=1, source_target_pairs={{0,4},{4,0},{1,5},{5,1},{2,6},{6,2},{3,7},{7,3},{8,12},{12,8},{9,1... | collective-permute-start | bytes 20 | tf_op jit(solution)/shard_map/ppermute | solution.py:69
  28.9 0.1 iota_compare_fusion
  28.9 1.1 collective-permute-done
  32.8 17.5 %all-to-all-done = bf16[64,8,768]{2,1,0:T(8,128)(2,1)S(1)} async-done(((bf16[64,8,768]{2,1,0:T(8,128)(2,1)}), bf16[64,8,768]{2,1,0:T(8,128)(2,1)S(1)}, u32[]{:S(2)}, u32[]{:S(2)}) %all-to-all-start) | async-done | bytes 786464 | tf_op jit(solution)/shard_map/all_to_all | solution.py:14
  50.3 1.9 %collective-permute-start.1 = (bf16[8,768]{1,0:T(8,128)(2,1)S(1)}, bf16[8,768]{1,0:T(8,128)(2,1)S(1)}, u32[]{:S(2)}, u32[]{:S(2)}) collective-permute-start(bf16[8,768]{1,0:T(8,128)(2,1)S(1)} %get-tuple-element.4), channel_id=1, source_target_pairs={{0,4},{4,0},{1,5},{5,1},{2,6},{6,2},{3,7},{7,3},{8,12},{12,8},{9,1... | collective-permute-start | bytes 36872 | tf_op jit(solution)/shard_map/ppermute | solution.py:71
  54.9 0.6 broadcast_in_dim.116
  55.5 4.3 %all-to-all-start.1 = ((bf16[4,2,8,768]{3,2,1,0:T(8,128)(2,1)}), bf16[4,2,8,768]{3,2,1,0:T(8,128)(2,1)S(1)}, u32[]{:S(2)}, u32[]{:S(2)}) async-start(bf16[4,2,8,768]{3,2,1,0:T(8,128)(2,1)} %broadcast_in_dim.116), calls=%async_computation.1 | async-start | bytes 196608 | tf_op jit(solution)/shard_map/all_to_all | solution.py:14
  59.8 0.1 broadcast_compare_fusion
  59.9 7.0 %all-to-all-done.1 = bf16[4,2,8,768]{3,2,1,0:T(8,128)(2,1)S(1)} async-done(((bf16[4,2,8,768]{3,2,1,0:T(8,128)(2,1)}), bf16[4,2,8,768]{3,2,1,0:T(8,128)(2,1)S(1)}, u32[]{:S(2)}, u32[]{:S(2)}) %all-to-all-start.1) | async-done | bytes 98336 | tf_op jit(solution)/shard_map/all_to_all | solution.py:14
  66.9 0.3 fusion.25
  67.3 6.4 %all-gather.2.cloned.1.call-done = bf16[3,1024,768]{2,1,0:T(8,128)(2,1)} async-done(((bf16[3,256,768]{2,1,0:T(8,128)(2,1)}), bf16[3,1024,768]{2,1,0:T(8,128)(2,1)}) %all-gather.2.cloned.1.call-update) | async-done | bytes 4718608 | tf_op jit(solution)/shard_map/all_gather | solution.py:58
  73.7 4.3 %fusion.16 = bf16[3,32,256]{2,1,0:T(8,128)(2,1)S(1)} fusion(bf16[3,256,1024]{2,1,0:T(8,128)(2,1)S(1)} %copy-done.1, bf16[3,1024,768]{2,1,0:T(8,128)(2,1)} %all-gather.2.cloned.1.call-done, pred[3,1024]{1,0:T(4,128)(4,1)S(1)} %iota_compare_fusion, pred[3,256]{1,0:T(4,128)(4,1)S(1)} %broadcast_compare_fusion, bf16[1,32,768]{2,1,0:T(8,128)(2,1)S(1)} %get-tuple-element.13, ...), kind=kOutput, calls=%fused_computation.15 | convolution fusion | flops 201744384 | bytes 6442752 | tf_op jit(solution)/shard_map/shg,sfg->shf/dot_general | solution.py:85
  78.0 0.0 copy-start.3
  78.0 1.7 %fusion.9 = f32[3,32,768]{2,1,0:T(8,128)S(1)} fusion(f32[3,32,768]{2,1,0:T(8,128)S(1)} %fusion.25, bf16[3,32,256]{2,1,0:T(8,128)(2,1)S(1)} %fusion.16, bf16[3,256,768]{2,1,0:T(8,128)(2,1)} %param.12, pred[3,256]{1,0:T(4,128)(4,1)S(1)} %broadcast_compare_fusion), kind=kOutput, calls=%fused_computation.10 | convolution fusion | flops 38412288 | bytes 1819392 | tf_op jit(solution)/shard_map/shf,sfn->shn/dot_general | solution.py:90
  79.8 0.7 pad_maximum_fusion
  80.5 3.4 %all-to-all-start.2 = ((bf16[8,2,8,768]{3,2,1,0:T(8,128)(2,1)}), bf16[8,2,8,768]{3,2,1,0:T(8,128)(2,1)S(1)}, u32[]{:S(2)}, u32[]{:S(2)}) async-start(bf16[8,2,8,768]{3,2,1,0:T(8,128)(2,1)} %bitcast.20), calls=%async_computation.2 | async-start | bytes 393216 | tf_op jit(solution)/shard_map/all_to_all | solution.py:109
  83.9 0.0 copy-start.2
  84.0 0.0 copy-start.5
  84.0 6.2 %all-to-all-done.2 = bf16[8,2,8,768]{3,2,1,0:T(8,128)(2,1)S(1)} async-done(((bf16[8,2,8,768]{3,2,1,0:T(8,128)(2,1)}), bf16[8,2,8,768]{3,2,1,0:T(8,128)(2,1)S(1)}, u32[]{:S(2)}, u32[]{:S(2)}) %all-to-all-start.2) | async-done | bytes 196640 | tf_op jit(solution)/shard_map/all_to_all | solution.py:109
  90.3 1.3 add_convert_fusion
  91.5 13.4 %all-to-all-start.3 = ((bf16[64,8,768]{2,1,0:T(8,128)(2,1)}), bf16[64,8,768]{2,1,0:T(8,128)(2,1)S(1)}, u32[]{:S(2)}, u32[]{:S(2)}) async-start(bf16[64,8,768]{2,1,0:T(8,128)(2,1)} %add_convert_fusion), calls=%async_computation.3 | async-start | bytes 1572864 | tf_op jit(solution)/shard_map/all_to_all | solution.py:124
  105.0 0.2 rev.3
  105.3 4.7 %fusion.3 = bf16[3,256,768]{2,1,0:T(8,128)(2,1)} fusion(bf16[3,1024,768]{2,1,0:T(8,128)(2,1)} %all-gather.2.cloned.1.call-done, bf16[3,256,1024]{2,1,0:T(8,128)(2,1)S(1)} %copy-done.1, pred[3,1024]{1,0:T(4,128)(4,1)S(1)} %iota_compare_fusion), kind=kOutput, calls=%fused_computation.5 | convolution fusion | flops 1209335808 | bytes 7474176 | tf_op jit(solution)/shard_map/sfg,sgn->sfn/dot_general | solution.py:61
  110.1 19.1 %all-to-all-done.3 = bf16[64,8,768]{2,1,0:T(8,128)(2,1)S(1)} async-done(((bf16[64,8,768]{2,1,0:T(8,128)(2,1)}), bf16[64,8,768]{2,1,0:T(8,128)(2,1)S(1)}, u32[]{:S(2)}, u32[]{:S(2)}) %all-to-all-start.3) | async-done | bytes 786464 | tf_op jit(solution)/shard_map/all_to_all | solution.py:124
  129.2 0.1 convert_reduce_fusion
  129.3 0.7 fusion.29
  (35 shorter events, 0.3 us)
Async XLA Ops:
  7.2 59.8 %copy-start = (bf16[3,192,768]{2,1,0:T(8,128)(2,1)S(1)}, bf16[3,192,768]{2,1,0:T(8,128)(2,1)}, u32[]{:S(2)}) copy-start(bf16[3,192,768]{2,1,0:T(8,128)(2,1)} %param.13) | copy-start | bytes 2654212
  7.2 19.1 %copy-start.8 = (s32[3,1]{0,1:T(1,128)S(1)}, s32[3,1]{0,1:T(1,128)}, u32[]{:S(2)}) copy-start(s32[3,1]{0,1:T(1,128)} %param.10) | copy-start | bytes 40
  7.2 21.7 %copy-start.7 = (s32[3]{0:T(128)S(1)}, s32[3]{0:T(128)}, u32[]{:S(2)}) copy-start(s32[3]{0:T(128)} %param.9) | copy-start | bytes 40
  7.2 66.5 %all-gather.2.cloned.1.call-start = ((), (), s32[]{:S(2)}) async-start(), calls=%async_computation.4 | async-start | bytes 5898240 | tf_op jit(solution)/shard_map/all_gather | solution.py:58
  9.6 64.2 %copy-start.1 = (bf16[3,256,1024]{2,1,0:T(8,128)(2,1)S(1)}, bf16[3,256,1024]{2,1,0:T(8,128)(2,1)}, u32[]{:S(2)}) copy-start(bf16[3,256,1024]{2,1,0:T(8,128)(2,1)} %param.11) | copy-start | bytes 4718596
  9.6 40.7 %all-to-all-start = ((bf16[64,8,768]{2,1,0:T(8,128)(2,1)}), bf16[64,8,768]{2,1,0:T(8,128)(2,1)S(1)}, u32[]{:S(2)}, u32[]{:S(2)}) async-start(bf16[64,8,768]{2,1,0:T(8,128)(2,1)} %broadcast_in_dim.115), calls=%async_computation | async-start | bytes 1572864 | tf_op jit(solution)/shard_map/all_to_all | solution.py:14
  26.9 3.1 %collective-permute-start = (s32[1]{0:T(128)}, s32[1]{0:T(128)}, u32[]{:S(2)}, u32[]{:S(2)}) collective-permute-start(s32[1]{0:T(128)} %bitcast.3), channel_id=1, source_target_pairs={{0,4},{4,0},{1,5},{5,1},{2,6},{6,2},{3,7},{7,3},{8,12},{12,8},{9,1... | collective-permute-start | bytes 20 | tf_op jit(solution)/shard_map/ppermute | solution.py:69
  50.3 4.6 %collective-permute-start.1 = (bf16[8,768]{1,0:T(8,128)(2,1)S(1)}, bf16[8,768]{1,0:T(8,128)(2,1)S(1)}, u32[]{:S(2)}, u32[]{:S(2)}) collective-permute-start(bf16[8,768]{1,0:T(8,128)(2,1)S(1)} %get-tuple-element.4), channel_id=1, source_target_pairs={{0,4},{4,0},{1,5},{5,1},{2,6},{6,2},{3,7},{7,3},{8,12},{12,8},{9,1... | collective-permute-start | bytes 36872 | tf_op jit(solution)/shard_map/ppermute | solution.py:71
  55.5 11.4 %all-to-all-start.1 = ((bf16[4,2,8,768]{3,2,1,0:T(8,128)(2,1)}), bf16[4,2,8,768]{3,2,1,0:T(8,128)(2,1)S(1)}, u32[]{:S(2)}, u32[]{:S(2)}) async-start(bf16[4,2,8,768]{3,2,1,0:T(8,128)(2,1)} %broadcast_in_dim.116), calls=%async_computation.1 | async-start | bytes 196608 | tf_op jit(solution)/shard_map/all_to_all | solution.py:14
  78.0 2.5 %copy-start.3 = (bf16[3,32,256]{2,1,0:T(8,128)(2,1)}, bf16[3,32,256]{2,1,0:T(8,128)(2,1)S(1)}, u32[]{:S(2)}) copy-start(bf16[3,32,256]{2,1,0:T(8,128)(2,1)S(1)} %fusion.16) | copy-start | bytes 147460
  80.5 9.7 %all-to-all-start.2 = ((bf16[8,2,8,768]{3,2,1,0:T(8,128)(2,1)}), bf16[8,2,8,768]{3,2,1,0:T(8,128)(2,1)S(1)}, u32[]{:S(2)}, u32[]{:S(2)}) async-start(bf16[8,2,8,768]{3,2,1,0:T(8,128)(2,1)} %bitcast.20), calls=%async_computation.2 | async-start | bytes 393216 | tf_op jit(solution)/shard_map/all_to_all | solution.py:109
  83.9 21.0 %copy-start.2 = (bf16[1,8,768]{2,1,0:T(8,128)(2,1)S(1)}, bf16[1,8,768]{2,1,0:T(8,128)(2,1)}, u32[]{:S(2)}) copy-start(bf16[1,8,768]{2,1,0:T(8,128)(2,1)} %param.14) | copy-start | bytes 36868
  84.0 21.0 %copy-start.5 = (f32[1,768]{1,0:T(1,128)S(1)}, f32[1,768]{1,0:T(1,128)}, u32[]{:S(2)}) copy-start(f32[1,768]{1,0:T(1,128)} %param.16) | copy-start | bytes 9220
  84.0 21.0 %copy-start.6 = (f32[1,768]{1,0:T(1,128)S(1)}, f32[1,768]{1,0:T(1,128)}, u32[]{:S(2)}) copy-start(f32[1,768]{1,0:T(1,128)} %param.17) | copy-start | bytes 9220
  91.5 37.6 %all-to-all-start.3 = ((bf16[64,8,768]{2,1,0:T(8,128)(2,1)}), bf16[64,8,768]{2,1,0:T(8,128)(2,1)S(1)}, u32[]{:S(2)}, u32[]{:S(2)}) async-start(bf16[64,8,768]{2,1,0:T(8,128)(2,1)} %add_convert_fusion), calls=%async_computation.3 | async-start | bytes 1572864 | tf_op jit(solution)/shard_map/all_to_all | solution.py:124
  105.3 24.0 %copy-start.4 = (f32[1,8,768]{2,1,0:T(8,128)S(1)}, f32[1,8,768]{2,1,0:T(8,128)}, u32[]{:S(2)}) copy-start(f32[1,8,768]{2,1,0:T(8,128)} %param.15) | copy-start | bytes 73732
Sparse Core Ops, SparseCore 0:
  10.1 63.5 all-gather.1

commit v13 on v11

--- a/solution.py
+++ b/solution.py
@@ -119,14 +119,17 @@
     near_part = mine[0]
     third_part = mine[1]
     other_part = theirs[1]
-    slots = jnp.arange(nplane, dtype=jnp.int32)[:, None, None]
-    dense = (
-        jnp.where(slots == near // 2, near_part, jnp.float32(0.0))
-        + jnp.where((slots == third // 2) & (third % 2 == core), third_part, jnp.float32(0.0))
-        + jnp.where((slots == other // 2) & (other % 2 == core), other_part, jnp.float32(0.0))
-    )
+    dense = jnp.zeros((nplane, rows_q, width), jnp.bfloat16)
+    for slot, part, valid in (
+        (near // 2, near_part, True),
+        (third // 2, third_part, third % 2 == core),
+        (other // 2, other_part, other % 2 == core),
+    ):
+        held = lax.dynamic_index_in_dim(dense, slot, 0, keepdims=False).astype(jnp.float32)
+        summed = jnp.where(valid, held + part, held).astype(jnp.bfloat16)
+        dense = lax.dynamic_update_index_in_dim(dense, summed, slot, 0)
     arrived = lax.all_to_all(
-        dense.astype(jnp.bfloat16), PLANE, split_axis=0, concat_axis=0, tiled=True
+        dense, PLANE, split_axis=0, concat_axis=0, tiled=True
     ).astype(jnp.float32)
     gathered = jnp.sum(arrived, axis=0, keepdims=True)
     rows_q = displacement.shape[1]

time: 137 us -> 140 us (1.022)
  local copies, waits for them, and re-layouts: 3.45 us -> 5.03 us
    dynamic_update_slice x0 -> x2, other arithmetic: none -> 2.61 us  [body(): dense = lax.dynamic_update_index_in_dim(dense, summed, slot, 0)]
where the time goes in v13:
time: 140 us; the launch traced here: 139 us
  waiting for transfers between devices  58.7 us (42%)
  starting transfers between devices  41.5 us (30%)
  between operations  19.3 us (14%)
  matrix products  10.3 us (7%)
  local copies, waits for them, and re-layouts  5.03 us (4%)
  other arithmetic  4.47 us (3%)
    all_to_all x2, waiting for transfers between devices, copy_for_each(): lax.all_to_all(jnp.broadcast_to(x[None], (length, *x.shape)), axis, 0, 0,...  24.8 us
    all_to_all x2, starting transfers between devices, copy_for_each(): lax.all_to_all(jnp.broadcast_to(x[None], (length, *x.shape)), axis, 0, 0,...  20.9 us
    all_to_all x1, waiting for transfers between devices, body(): lax.all_to_all(dense, PLANE, split_axis=0, concat_axis=0, tiled=True)  19.1 us
    all_to_all x1, starting transfers between devices, body(): lax.all_to_all(dense, PLANE, split_axis=0, concat_axis=0, tiled=True)  13.4 us
    all_gather x1, waiting for transfers between devices, body(): piece = lax.all_gather(coupling, 'harm', axis=1, tiled=True)  6.61 us
    all_to_all x1, waiting for transfers between devices, body(): lax.all_to_all(send.reshape(2 * nharm, 2, rows_q, width).astype(jnp.bfloa...  6.21 us
    dot_general x1, matrix products, body(): jnp.einsum('sfg,sgn->sfn', front_live, piece, preferred_element_type=jnp....  4.74 us
    dot_general x1, matrix products, body(): jnp.einsum('shn,sgn->shg', own_disp, piece, preferred_element_type=jnp.fl...  3.8 us
  transfers between devices with their start and end apart: 7, of which 6 were waited for; matrix products, arithmetic and copies ran while one was open for 6% of the time, Pallas kernels for 0%

profile of v13, /device:TPU:8, one launch (start us, length us, event | category | flops | bytes accessed | tf_op | source)
XLA Modules:
  0.0 139.3 jit_solution(3698149542697823702)
XLA Ops:
  7.2 0.7 all-gather.2.cloned.1.call-update
  7.9 1.6 %broadcast_in_dim.87 = bf16[64,8,768]{2,1,0:T(8,128)(2,1)} broadcast(bf16[8,768]{1,0:T(8,128)(2,1)} %bitcast.70), dimensions={1,2} | broadcast | bytes 798720 | tf_op jit(solution)/shard_map/broadcast_in_dim | solution.py:14
  9.6 16.6 %all-to-all-start = ((bf16[64,8,768]{2,1,0:T(8,128)(2,1)}), bf16[64,8,768]{2,1,0:T(8,128)(2,1)S(1)}, u32[]{:S(2)}, u32[]{:S(2)}) async-start(bf16[64,8,768]{2,1,0:T(8,128)(2,1)} %broadcast_in_dim.87), calls=%async_computation | async-start | bytes 1572864 | tf_op jit(solution)/shard_map/all_to_all | solution.py:14
  26.2 0.6 slice.51
  26.8 1.9 %collective-permute-start = (s32[1]{0:T(128)}, s32[1]{0:T(128)}, u32[]{:S(2)}, u32[]{:S(2)}) collective-permute-start(s32[1]{0:T(128)} %bitcast.3), channel_id=1, source_target_pairs={{0,4},{4,0},{1,5},{5,1},{2,6},{6,2},{3,7},{7,3},{8,12},{12,8},{9,1... | collective-permute-start | bytes 20 | tf_op jit(solution)/shard_map/ppermute | solution.py:69
  28.7 0.1 iota_compare_fusion
  28.8 1.2 collective-permute-done
  32.3 17.8 %all-to-all-done = bf16[64,8,768]{2,1,0:T(8,128)(2,1)S(1)} async-done(((bf16[64,8,768]{2,1,0:T(8,128)(2,1)}), bf16[64,8,768]{2,1,0:T(8,128)(2,1)S(1)}, u32[]{:S(2)}, u32[]{:S(2)}) %all-to-all-start) | async-done | bytes 786464 | tf_op jit(solution)/shard_map/all_to_all | solution.py:14
  50.1 1.9 %collective-permute-start.1 = (bf16[8,768]{1,0:T(8,128)(2,1)S(1)}, bf16[8,768]{1,0:T(8,128)(2,1)S(1)}, u32[]{:S(2)}, u32[]{:S(2)}) collective-permute-start(bf16[8,768]{1,0:T(8,128)(2,1)S(1)} %get-tuple-element.4), channel_id=1, source_target_pairs={{0,4},{4,0},{1,5},{5,1},{2,6},{6,2},{3,7},{7,3},{8,12},{12,8},{9,1... | collective-permute-start | bytes 36872 | tf_op jit(solution)/shard_map/ppermute | solution.py:71
  54.7 0.6 broadcast_in_dim.88
  55.4 4.3 %all-to-all-start.1 = ((bf16[4,2,8,768]{3,2,1,0:T(8,128)(2,1)}), bf16[4,2,8,768]{3,2,1,0:T(8,128)(2,1)S(1)}, u32[]{:S(2)}, u32[]{:S(2)}) async-start(bf16[4,2,8,768]{3,2,1,0:T(8,128)(2,1)} %broadcast_in_dim.88), calls=%async_computation.1 | async-start | bytes 196608 | tf_op jit(solution)/shard_map/all_to_all | solution.py:14
  59.7 0.1 broadcast_compare_fusion
  59.7 7.0 %all-to-all-done.1 = bf16[4,2,8,768]{3,2,1,0:T(8,128)(2,1)S(1)} async-done(((bf16[4,2,8,768]{3,2,1,0:T(8,128)(2,1)}), bf16[4,2,8,768]{3,2,1,0:T(8,128)(2,1)S(1)}, u32[]{:S(2)}, u32[]{:S(2)}) %all-to-all-start.1) | async-done | bytes 98336 | tf_op jit(solution)/shard_map/all_to_all | solution.py:14
  66.8 0.3 fusion.20
  67.2 6.6 %all-gather.2.cloned.1.call-done = bf16[3,1024,768]{2,1,0:T(8,128)(2,1)} async-done(((bf16[3,256,768]{2,1,0:T(8,128)(2,1)}), bf16[3,1024,768]{2,1,0:T(8,128)(2,1)}) %all-gather.2.cloned.1.call-update) | async-done | bytes 4718608 | tf_op jit(solution)/shard_map/all_gather | solution.py:58
  73.8 3.8 %convolution_select_fusion = f32[3,32,1024]{2,1,0:T(8,128)S(1)} fusion(bf16[3,1024,768]{2,1,0:T(8,128)(2,1)} %all-gather.2.cloned.1.call-done, pred[3,1024]{1,0:T(4,128)(4,1)S(1)} %iota_compare_fusion, bf16[1,32,768]{2,1,0:T(8,128)(2,1)S(1)} %get-tuple-element.13, bf16[1,32,768]{2,1,0:T(8,128)(2,1)S(1)} %get-tuple-element.12), kind=kOutput, calls=%fused_computation.5 | convolution fusion | flops 151240704 | bytes 5213184 | tf_op jit(solution)/shard_map/shn,sgn->shg/dot_general | solution.py:83
  77.6 1.0 fusion.13
  78.6 0.2 copy-done.2
  78.9 0.4 fusion.9
  79.3 0.7 pad_maximum_fusion
  80.0 3.4 %all-to-all-start.2 = ((bf16[8,2,8,768]{3,2,1,0:T(8,128)(2,1)}), bf16[8,2,8,768]{3,2,1,0:T(8,128)(2,1)S(1)}, u32[]{:S(2)}, u32[]{:S(2)}) async-start(bf16[8,2,8,768]{3,2,1,0:T(8,128)(2,1)} %bitcast.20), calls=%async_computation.2 | async-start | bytes 393216 | tf_op jit(solution)/shard_map/all_to_all | solution.py:113
  83.5 6.2 %all-to-all-done.2 = bf16[8,2,8,768]{3,2,1,0:T(8,128)(2,1)S(1)} async-done(((bf16[8,2,8,768]{3,2,1,0:T(8,128)(2,1)}), bf16[8,2,8,768]{3,2,1,0:T(8,128)(2,1)S(1)}, u32[]{:S(2)}, u32[]{:S(2)}) %all-to-all-start.2) | async-done | bytes 196640 | tf_op jit(solution)/shard_map/all_to_all | solution.py:113
  89.8 1.0 broadcast_in_dim.91
  90.7 0.6 fusion.28
  91.3 1.3 fusion.30
  92.7 1.3 fusion.29
  94.0 13.4 %all-to-all-start.3 = ((bf16[64,8,768]{2,1,0:T(8,128)(2,1)}), bf16[64,8,768]{2,1,0:T(8,128)(2,1)S(1)}, u32[]{:S(2)}, u32[]{:S(2)}) async-start(bf16[64,8,768]{2,1,0:T(8,128)(2,1)} %fusion.29), calls=%async_computation.3 | async-start | bytes 1572864 | tf_op jit(solution)/shard_map/all_to_all | solution.py:131
  107.4 0.2 rev.3
  107.7 4.7 %fusion.3 = bf16[3,256,768]{2,1,0:T(8,128)(2,1)} fusion(bf16[3,1024,768]{2,1,0:T(8,128)(2,1)} %all-gather.2.cloned.1.call-done, bf16[3,256,1024]{2,1,0:T(8,128)(2,1)S(1)} %copy-done.1, pred[3,1024]{1,0:T(4,128)(4,1)S(1)} %iota_compare_fusion), kind=kOutput, calls=%fused_computation.4 | convolution fusion | flops 1209335808 | bytes 7474176 | tf_op jit(solution)/shard_map/sfg,sgn->sfn/dot_general | solution.py:61
  112.5 19.1 %all-to-all-done.3 = bf16[64,8,768]{2,1,0:T(8,128)(2,1)S(1)} async-done(((bf16[64,8,768]{2,1,0:T(8,128)(2,1)}), bf16[64,8,768]{2,1,0:T(8,128)(2,1)S(1)}, u32[]{:S(2)}, u32[]{:S(2)}) %all-to-all-start.3) | async-done | bytes 786464 | tf_op jit(solution)/shard_map/all_to_all | solution.py:131
  131.6 0.1 convert_reduce_fusion
  131.7 0.7 fusion.26
  (37 shorter events, 0.3 us)
Async XLA Ops:
  7.2 59.6 %copy-start = (bf16[3,192,768]{2,1,0:T(8,128)(2,1)S(1)}, bf16[3,192,768]{2,1,0:T(8,128)(2,1)}, u32[]{:S(2)}) copy-start(bf16[3,192,768]{2,1,0:T(8,128)(2,1)} %param.13) | copy-start | bytes 2654212
  7.2 19.0 %copy-start.9 = (s32[3,1]{0,1:T(1,128)S(1)}, s32[3,1]{0,1:T(1,128)}, u32[]{:S(2)}) copy-start(s32[3,1]{0,1:T(1,128)} %param.10) | copy-start | bytes 40
  7.2 21.5 %copy-start.8 = (s32[3]{0:T(128)S(1)}, s32[3]{0:T(128)}, u32[]{:S(2)}) copy-start(s32[3]{0:T(128)} %param.9) | copy-start | bytes 40
  7.2 66.6 %all-gather.2.cloned.1.call-start = ((), (), s32[]{:S(2)}) async-start(), calls=%async_computation.4 | async-start | bytes 5898240 | tf_op jit(solution)/shard_map/all_gather | solution.py:58
  9.6 40.6 %all-to-all-start = ((bf16[64,8,768]{2,1,0:T(8,128)(2,1)}), bf16[64,8,768]{2,1,0:T(8,128)(2,1)S(1)}, u32[]{:S(2)}, u32[]{:S(2)}) async-start(bf16[64,8,768]{2,1,0:T(8,128)(2,1)} %broadcast_in_dim.87), calls=%async_computation | async-start | bytes 1572864 | tf_op jit(solution)/shard_map/all_to_all | solution.py:14
  26.8 3.3 %collective-permute-start = (s32[1]{0:T(128)}, s32[1]{0:T(128)}, u32[]{:S(2)}, u32[]{:S(2)}) collective-permute-start(s32[1]{0:T(128)} %bitcast.3), channel_id=1, source_target_pairs={{0,4},{4,0},{1,5},{5,1},{2,6},{6,2},{3,7},{7,3},{8,12},{12,8},{9,1... | collective-permute-start | bytes 20 | tf_op jit(solution)/shard_map/ppermute | solution.py:69
  50.1 4.6 %collective-permute-start.1 = (bf16[8,768]{1,0:T(8,128)(2,1)S(1)}, bf16[8,768]{1,0:T(8,128)(2,1)S(1)}, u32[]{:S(2)}, u32[]{:S(2)}) collective-permute-start(bf16[8,768]{1,0:T(8,128)(2,1)S(1)} %get-tuple-element.4), channel_id=1, source_target_pairs={{0,4},{4,0},{1,5},{5,1},{2,6},{6,2},{3,7},{7,3},{8,12},{12,8},{9,1... | collective-permute-start | bytes 36872 | tf_op jit(solution)/shard_map/ppermute | solution.py:71
  55.4 11.4 %all-to-all-start.1 = ((bf16[4,2,8,768]{3,2,1,0:T(8,128)(2,1)}), bf16[4,2,8,768]{3,2,1,0:T(8,128)(2,1)S(1)}, u32[]{:S(2)}, u32[]{:S(2)}) async-start(bf16[4,2,8,768]{3,2,1,0:T(8,128)(2,1)} %broadcast_in_dim.88), calls=%async_computation.1 | async-start | bytes 196608 | tf_op jit(solution)/shard_map/all_to_all | solution.py:14
  67.2 10.4 %copy-start.1 = (bf16[3,256,1024]{2,1,0:T(8,128)(2,1)S(1)}, bf16[3,256,1024]{2,1,0:T(8,128)(2,1)}, u32[]{:S(2)}) copy-start(bf16[3,256,1024]{2,1,0:T(8,128)(2,1)} %param.11) | copy-start | bytes 4718596
  77.6 1.3 copy-start.2
  78.9 1.2 copy-start.4
  80.0 9.7 %all-to-all-start.2 = ((bf16[8,2,8,768]{3,2,1,0:T(8,128)(2,1)}), bf16[8,2,8,768]{3,2,1,0:T(8,128)(2,1)S(1)}, u32[]{:S(2)}, u32[]{:S(2)}) async-start(bf16[8,2,8,768]{3,2,1,0:T(8,128)(2,1)} %bitcast.20), calls=%async_computation.2 | async-start | bytes 393216 | tf_op jit(solution)/shard_map/all_to_all | solution.py:113
  83.5 23.9 %copy-start.3 = (bf16[1,8,768]{2,1,0:T(8,128)(2,1)S(1)}, bf16[1,8,768]{2,1,0:T(8,128)(2,1)}, u32[]{:S(2)}) copy-start(bf16[1,8,768]{2,1,0:T(8,128)(2,1)} %param.14) | copy-start | bytes 36868
  83.5 24.2 %copy-start.6 = (f32[1,768]{1,0:T(1,128)S(1)}, f32[1,768]{1,0:T(1,128)}, u32[]{:S(2)}) copy-start(f32[1,768]{1,0:T(1,128)} %param.16) | copy-start | bytes 9220
  83.5 24.2 %copy-start.7 = (f32[1,768]{1,0:T(1,128)S(1)}, f32[1,768]{1,0:T(1,128)}, u32[]{:S(2)}) copy-start(f32[1,768]{1,0:T(1,128)} %param.17) | copy-start | bytes 9220
  94.0 37.6 %all-to-all-start.3 = ((bf16[64,8,768]{2,1,0:T(8,128)(2,1)}), bf16[64,8,768]{2,1,0:T(8,128)(2,1)S(1)}, u32[]{:S(2)}, u32[]{:S(2)}) async-start(bf16[64,8,768]{2,1,0:T(8,128)(2,1)} %fusion.29), calls=%async_computation.3 | async-start | bytes 1572864 | tf_op jit(solution)/shard_map/all_to_all | solution.py:131
  107.7 24.0 %copy-start.5 = (f32[1,8,768]{2,1,0:T(8,128)S(1)}, f32[1,8,768]{2,1,0:T(8,128)}, u32[]{:S(2)}) copy-start(f32[1,8,768]{2,1,0:T(8,128)} %param.15) | copy-start | bytes 73732
Sparse Core Ops, SparseCore 0:
  10.1 63.5 all-gather.1

commit v14 on v5

--- a/solution.py
+++ b/solution.py
@@ -55,11 +55,11 @@
     own_rows = harm_idx * front_q + jnp.arange(front_q, dtype=jnp.int32)
     live_rows = own_rows[None, :] < lengths[:, None]
     masked = jnp.where(live_rows[:, :, None], coupling, jnp.zeros_like(coupling))
-    whole_live = jnp.arange(nharm * front_q, dtype=jnp.int32)[None, :] < lengths[:, None]
     piece = lax.all_gather(coupling, "harm", axis=1, tiled=True)
-    piece = jnp.where(whole_live[:, :, None], piece, jnp.zeros_like(piece))
+    live_cols = jnp.arange(nharm * front_q, dtype=jnp.int32)[None, :] < lengths[:, None]
+    front_live = jnp.where(live_cols[:, None, :], front_inverse, jnp.zeros_like(front_inverse))
     modes = jnp.einsum(
-        "sfg,sgn->sfn", front_inverse, piece, preferred_element_type=jnp.float32
+        "sfg,sgn->sfn", front_live, piece, preferred_element_type=jnp.float32
     ).astype(jnp.bfloat16)
     nplane = lax.axis_size(PLANE)
     rows_q = displacement.shape[1]
@@ -95,13 +95,13 @@
     lent = (lent[0] + lent[1]).transpose(1, 0, 2, 3)
     own_pair = lent.reshape(2, nharm * zero_block.shape[0], width)
     own_disp = jnp.stack([own_pair[0], own_pair[0], own_pair[1]])
-    partial_y = jnp.einsum("shn,sfn->shf", own_disp, masked, preferred_element_type=jnp.float32)
-    whole_y = collect(partial_y, "harm", 2)
+    whole_y = jnp.einsum("shn,sgn->shg", own_disp, piece, preferred_element_type=jnp.float32)
+    whole_y = jnp.where(live_cols[:, None, :], whole_y, jnp.float32(0.0))
     inner = -jnp.einsum(
         "shg,sfg->shf",
         whole_y,
         front_inverse.astype(jnp.float32),
-        precision=lax.Precision.HIGHEST,
+        precision=lax.Precision.HIGH,
         preferred_element_type=jnp.float32,
     )
     interior = jnp.where(live_rows[:, None, :], inner, jnp.float32(0.0)).astype(jnp.bfloat16)

time: 142 us -> 138 us (0.972)
  the two profiles are of different devices: /device:TPU:2 before, /device:TPU:8 now
where the time goes in v14:
time: 138 us; the launch traced here: 137 us
  waiting for transfers between devices  58.3 us (42%)
  starting transfers between devices  39.6 us (29%)
  between operations  22.6 us (16%)
  matrix products  10.3 us (7%)
  local copies, waits for them, and re-layouts  3.49 us (3%)
  other arithmetic  3.18 us (2%)
    all_to_all x1, waiting for transfers between devices, body(): lax.all_to_all(dense.astype(jnp.bfloat16), PLANE, split_axis=0, concat_ax...  19.1 us
    all_to_all x1, starting transfers between devices, copy_for_each(): lax.all_to_all(jnp.broadcast_to(x[None], (length, *x.shape)), axis, 0, 0,...  16.6 us
    all_to_all x1, waiting for transfers between devices, copy_for_each(): lax.all_to_all(jnp.broadcast_to(x[None], (length, *x.shape)), axis, 0, 0,...  15.9 us
    all_to_all x1, starting transfers between devices, body(): lax.all_to_all(dense.astype(jnp.bfloat16), PLANE, split_axis=0, concat_ax...  13.4 us
    all_gather x1, waiting for transfers between devices, body(): piece = lax.all_gather(coupling, 'harm', axis=1, tiled=True)  11.8 us
    all_to_all x1, waiting for transfers between devices, body(): lax.all_to_all(lend.reshape(2 * nharm, 2, *zero_block.shape), PAIR, 0, 0,...  7.35 us
    dot_general x1, matrix products, body(): jnp.einsum('sfg,sgn->sfn', front_live, piece, preferred_element_type=jnp....  4.74 us
    all_to_all x1, starting transfers between devices, body(): lax.all_to_all(lend.reshape(2 * nharm, 2, *zero_block.shape), PAIR, 0, 0,...  4.3 us
  transfers between devices with their start and end apart: 6, of which 5 were waited for; matrix products, arithmetic and copies ran while one was open for 6% of the time, Pallas kernels for 0%

profile of v14, /device:TPU:8, one launch (start us, length us, event | category | flops | bytes accessed | tf_op | source)
XLA Modules:
  0.0 137.5 jit_solution(9124047040267788822)
XLA Ops:
  7.2 0.0 copy-start
  7.2 0.0 all-gather.2.cloned.1.call-start
  7.2 0.7 all-gather.2.cloned.1.call-update
  7.9 1.6 %broadcast_in_dim.118 = bf16[64,8,768]{2,1,0:T(8,128)(2,1)} broadcast(bf16[8,768]{1,0:T(8,128)(2,1)} %bitcast.57), dimensions={1,2} | broadcast | bytes 798720 | tf_op jit(solution)/shard_map/broadcast_in_dim | solution.py:14
  9.6 16.6 %all-to-all-start = ((bf16[64,8,768]{2,1,0:T(8,128)(2,1)}), bf16[64,8,768]{2,1,0:T(8,128)(2,1)S(1)}, u32[]{:S(2)}, u32[]{:S(2)}) async-start(bf16[64,8,768]{2,1,0:T(8,128)(2,1)} %broadcast_in_dim.118), calls=%async_computation | async-start | bytes 1572864 | tf_op jit(solution)/shard_map/all_to_all | solution.py:14
  26.2 0.6 slice.54
  26.8 1.9 %collective-permute-start = (s32[1]{0:T(128)}, s32[1]{0:T(128)}, u32[]{:S(2)}, u32[]{:S(2)}) collective-permute-start(s32[1]{0:T(128)} %bitcast.2), channel_id=1, source_target_pairs={{0,4},{4,0},{1,5},{5,1},{2,6},{6,2},{3,7},{7,3},{8,12},{12,8},{9,1... | collective-permute-start | bytes 20 | tf_op jit(solution)/shard_map/ppermute | solution.py:69
  31.4 0.1 iota_compare_fusion
  34.2 15.9 %all-to-all-done = bf16[64,8,768]{2,1,0:T(8,128)(2,1)S(1)} async-done(((bf16[64,8,768]{2,1,0:T(8,128)(2,1)}), bf16[64,8,768]{2,1,0:T(8,128)(2,1)S(1)}, u32[]{:S(2)}, u32[]{:S(2)}) %all-to-all-start) | async-done | bytes 786464 | tf_op jit(solution)/shard_map/all_to_all | solution.py:14
  50.2 0.7 broadcast_in_dim.120
  50.9 4.3 %all-to-all-start.1 = ((bf16[8,2,8,768]{3,2,1,0:T(8,128)(2,1)}), bf16[8,2,8,768]{3,2,1,0:T(8,128)(2,1)S(1)}, u32[]{:S(2)}, u32[]{:S(2)}) async-start(bf16[8,2,8,768]{3,2,1,0:T(8,128)(2,1)} %bitcast.6), calls=%async_computation.1 | async-start | bytes 393216 | tf_op jit(solution)/shard_map/all_to_all | solution.py:92
  55.2 0.1 broadcast_compare_fusion
  55.2 7.3 %all-to-all-done.1 = bf16[8,2,8,768]{3,2,1,0:T(8,128)(2,1)S(1)} async-done(((bf16[8,2,8,768]{3,2,1,0:T(8,128)(2,1)}), bf16[8,2,8,768]{3,2,1,0:T(8,128)(2,1)S(1)}, u32[]{:S(2)}, u32[]{:S(2)}) %all-to-all-start.1) | async-done | bytes 196640 | tf_op jit(solution)/shard_map/all_to_all | solution.py:92
  62.7 0.3 fusion.21
  63.0 11.8 %all-gather.2.cloned.1.call-done = bf16[3,1024,768]{2,1,0:T(8,128)(2,1)} async-done(((bf16[3,256,768]{2,1,0:T(8,128)(2,1)}), bf16[3,1024,768]{2,1,0:T(8,128)(2,1)}) %all-gather.2.cloned.1.call-update) | async-done | bytes 4718608 | tf_op jit(solution)/shard_map/all_gather | solution.py:58
  74.8 3.8 %convolution_select_fusion = f32[3,32,1024]{2,1,0:T(8,128)S(1)} fusion(bf16[3,1024,768]{2,1,0:T(8,128)(2,1)} %all-gather.2.cloned.1.call-done, pred[3,1024]{1,0:T(4,128)(4,1)S(1)} %iota_compare_fusion, bf16[1,32,768]{2,1,0:T(8,128)(2,1)S(1)} %get-tuple-element.15, bf16[1,32,768]{2,1,0:T(8,128)(2,1)S(1)} %get-tuple-element.14), kind=kOutput, calls=%fused_computation.6 | convolution fusion | flops 151240704 | bytes 5213184 | tf_op jit(solution)/shard_map/shn,sgn->shg/dot_general | solution.py:98
  78.6 0.0 copy-done.1
  78.6 0.0 copy-start.2
  78.6 1.0 fusion.13
  79.7 0.2 copy-done.2
  79.9 0.4 fusion.9
  80.4 0.7 pad_maximum_fusion
  81.1 3.4 %all-to-all-start.2 = ((bf16[8,2,8,768]{3,2,1,0:T(8,128)(2,1)}), bf16[8,2,8,768]{3,2,1,0:T(8,128)(2,1)S(1)}, u32[]{:S(2)}, u32[]{:S(2)}) async-start(bf16[8,2,8,768]{3,2,1,0:T(8,128)(2,1)} %bitcast.20), calls=%async_computation.2 | async-start | bytes 393216 | tf_op jit(solution)/shard_map/all_to_all | solution.py:128
  87.3 0.0 copy-start.3
  87.3 3.5 %all-to-all-done.2 = bf16[8,2,8,768]{3,2,1,0:T(8,128)(2,1)S(1)} async-done(((bf16[8,2,8,768]{3,2,1,0:T(8,128)(2,1)}), bf16[8,2,8,768]{3,2,1,0:T(8,128)(2,1)S(1)}, u32[]{:S(2)}, u32[]{:S(2)}) %all-to-all-start.2) | async-done | bytes 196640 | tf_op jit(solution)/shard_map/all_to_all | solution.py:128
  90.9 1.3 add_convert_fusion
  92.2 13.4 %all-to-all-start.3 = ((bf16[64,8,768]{2,1,0:T(8,128)(2,1)}), bf16[64,8,768]{2,1,0:T(8,128)(2,1)S(1)}, u32[]{:S(2)}, u32[]{:S(2)}) async-start(bf16[64,8,768]{2,1,0:T(8,128)(2,1)} %add_convert_fusion), calls=%async_computation.3 | async-start | bytes 1572864 | tf_op jit(solution)/shard_map/all_to_all | solution.py:143
  105.6 0.2 rev.3
  105.9 4.7 %fusion.3 = bf16[3,256,768]{2,1,0:T(8,128)(2,1)} fusion(bf16[3,1024,768]{2,1,0:T(8,128)(2,1)} %all-gather.2.cloned.1.call-done, bf16[3,256,1024]{2,1,0:T(8,128)(2,1)S(1)} %copy-done.1, pred[3,1024]{1,0:T(4,128)(4,1)S(1)} %iota_compare_fusion), kind=kOutput, calls=%fused_computation.5 | convolution fusion | flops 1209335808 | bytes 7474176 | tf_op jit(solution)/shard_map/sfg,sgn->sfn/dot_general | solution.py:61
  110.7 19.1 %all-to-all-done.3 = bf16[64,8,768]{2,1,0:T(8,128)(2,1)S(1)} async-done(((bf16[64,8,768]{2,1,0:T(8,128)(2,1)}), bf16[64,8,768]{2,1,0:T(8,128)(2,1)S(1)}, u32[]{:S(2)}, u32[]{:S(2)}) %all-to-all-start.3) | async-done | bytes 786464 | tf_op jit(solution)/shard_map/all_to_all | solution.py:143
  129.8 0.1 convert_reduce_fusion
  129.9 0.7 fusion.25
  (38 shorter events, 0.3 us)
Async XLA Ops:
  7.2 55.5 %copy-start = (bf16[3,192,768]{2,1,0:T(8,128)(2,1)S(1)}, bf16[3,192,768]{2,1,0:T(8,128)(2,1)}, u32[]{:S(2)}) copy-start(bf16[3,192,768]{2,1,0:T(8,128)(2,1)} %param.13) | copy-start | bytes 2654212
  7.2 19.0 %copy-start.9 = (s32[3,1]{0,1:T(1,128)S(1)}, s32[3,1]{0,1:T(1,128)}, u32[]{:S(2)}) copy-start(s32[3,1]{0,1:T(1,128)} %param.10) | copy-start | bytes 40
  7.2 24.2 %copy-start.8 = (s32[3]{0:T(128)S(1)}, s32[3]{0:T(128)}, u32[]{:S(2)}) copy-start(s32[3]{0:T(128)} %param.9) | copy-start | bytes 40
  7.2 67.6 %all-gather.2.cloned.1.call-start = ((), (), s32[]{:S(2)}) async-start(), calls=%async_computation.4 | async-start | bytes 5898240 | tf_op jit(solution)/shard_map/all_gather | solution.py:58
  9.6 40.6 %all-to-all-start = ((bf16[64,8,768]{2,1,0:T(8,128)(2,1)}), bf16[64,8,768]{2,1,0:T(8,128)(2,1)S(1)}, u32[]{:S(2)}, u32[]{:S(2)}) async-start(bf16[64,8,768]{2,1,0:T(8,128)(2,1)} %broadcast_in_dim.118), calls=%async_computation | async-start | bytes 1572864 | tf_op jit(solution)/shard_map/all_to_all | solution.py:14
  26.8 4.7 %collective-permute-start = (s32[1]{0:T(128)}, s32[1]{0:T(128)}, u32[]{:S(2)}, u32[]{:S(2)}) collective-permute-start(s32[1]{0:T(128)} %bitcast.2), channel_id=1, source_target_pairs={{0,4},{4,0},{1,5},{5,1},{2,6},{6,2},{3,7},{7,3},{8,12},{12,8},{9,1... | collective-permute-start | bytes 20 | tf_op jit(solution)/shard_map/ppermute | solution.py:69
  50.9 11.7 %all-to-all-start.1 = ((bf16[8,2,8,768]{3,2,1,0:T(8,128)(2,1)}), bf16[8,2,8,768]{3,2,1,0:T(8,128)(2,1)S(1)}, u32[]{:S(2)}, u32[]{:S(2)}) async-start(bf16[8,2,8,768]{3,2,1,0:T(8,128)(2,1)} %bitcast.6), calls=%async_computation.1 | async-start | bytes 393216 | tf_op jit(solution)/shard_map/all_to_all | solution.py:92
  63.0 15.6 %copy-start.1 = (bf16[3,256,1024]{2,1,0:T(8,128)(2,1)S(1)}, bf16[3,256,1024]{2,1,0:T(8,128)(2,1)}, u32[]{:S(2)}) copy-start(bf16[3,256,1024]{2,1,0:T(8,128)(2,1)} %param.11) | copy-start | bytes 4718596
  78.6 1.3 copy-start.2
  79.9 1.2 copy-start.4
  81.1 9.7 %all-to-all-start.2 = ((bf16[8,2,8,768]{3,2,1,0:T(8,128)(2,1)}), bf16[8,2,8,768]{3,2,1,0:T(8,128)(2,1)S(1)}, u32[]{:S(2)}, u32[]{:S(2)}) async-start(bf16[8,2,8,768]{3,2,1,0:T(8,128)(2,1)} %bitcast.20), calls=%async_computation.2 | async-start | bytes 393216 | tf_op jit(solution)/shard_map/all_to_all | solution.py:128
  87.3 18.2 %copy-start.3 = (bf16[1,8,768]{2,1,0:T(8,128)(2,1)S(1)}, bf16[1,8,768]{2,1,0:T(8,128)(2,1)}, u32[]{:S(2)}) copy-start(bf16[1,8,768]{2,1,0:T(8,128)(2,1)} %param.14) | copy-start | bytes 36868
  90.8 15.0 %copy-start.6 = (f32[1,768]{1,0:T(1,128)S(1)}, f32[1,768]{1,0:T(1,128)}, u32[]{:S(2)}) copy-start(f32[1,768]{1,0:T(1,128)} %param.16) | copy-start | bytes 9220
  90.8 15.0 %copy-start.7 = (f32[1,768]{1,0:T(1,128)S(1)}, f32[1,768]{1,0:T(1,128)}, u32[]{:S(2)}) copy-start(f32[1,768]{1,0:T(1,128)} %param.17) | copy-start | bytes 9220
  92.2 37.6 %all-to-all-start.3 = ((bf16[64,8,768]{2,1,0:T(8,128)(2,1)}), bf16[64,8,768]{2,1,0:T(8,128)(2,1)S(1)}, u32[]{:S(2)}, u32[]{:S(2)}) async-start(bf16[64,8,768]{2,1,0:T(8,128)(2,1)} %add_convert_fusion), calls=%async_computation.3 | async-start | bytes 1572864 | tf_op jit(solution)/shard_map/all_to_all | solution.py:143
  105.9 24.0 %copy-start.5 = (f32[1,8,768]{2,1,0:T(8,128)S(1)}, f32[1,8,768]{2,1,0:T(8,128)}, u32[]{:S(2)}) copy-start(f32[1,8,768]{2,1,0:T(8,128)} %param.15) | copy-start | bytes 73732
Sparse Core Ops, SparseCore 0:
  10.1 64.6 all-gather.1
